TPU v7x, 128 devices: a whole 4x4x4 slice. The times are simulated.
128 devices in a mesh: expert: 32 (over x, y, core), hidden: 4 (over z).
Axes of the slice: x: 4, y: 4, z: 4, core: 2. Of those that a mesh axis runs over, the one named last changes fastest.
Arguments:
- tokens: bfloat16 [4096, 4096], P('expert', 'hidden'), may hold values from -6 to 6
- w_gate: bfloat16 [64, 4096, 1536], P('expert', None, 'hidden'), may hold values from -0.09375 to 0.09375
- w_up: bfloat16 [64, 4096, 1536], P('expert', None, 'hidden'), may hold values from -0.09375 to 0.09375
- w_down: bfloat16 [64, 1536, 4096], P('expert', 'hidden'), may hold values from -0.15625 to 0.15625
- routes: int32 [4096, 8], P('expert'), may hold values from 0 to 63, all different within a row; in each aligned block of 128 rows (0 to 127, 128 to 255, ...) at most 24 rows name the same one
- gate_levels: int32 [4096, 8], P('expert'), may hold values from 1 to 16
- ancestors: int32 [4096], P('expert'), may hold values from 0 to 127
Outputs:
- mixed: bfloat16 [4096, 4096], P('expert', 'hidden')
Inputs may be any that keep to these rules, and one draw needn't show every extreme that they name: `routes`: in each aligned block of 128 rows no expert is chosen by more than 24 rows, a bound that some block reaches; a row chooses 8 different experts. `ancestors`: an ancestor lies in the same aligned block of 128 rows.
All inputs are finite; a program needn't handle non-finite values.
Results may differ from a plain program's by a relative error of at most 0.014.
Values may be sent and summed in bfloat16 or wider, within the bound.
No kernel may reach another device: no remote copies, remote signals or barrier semaphores. Data moves between devices by JAX's collectives and lax.ppermute only.
A program may use at most 192 MiB of HBM per device.

v0:
```python
import jax
import jax.numpy as jnp
from jax import lax
from jax.sharding import PartitionSpec as P

def expert_part(arrived, w_gate, w_up, w_down):
    gate_acts = jnp.einsum("scd,df->scf", arrived, w_gate, preferred_element_type=jnp.float32)
    up_acts = jnp.einsum("scd,df->scf", arrived, w_up, preferred_element_type=jnp.float32)
    hidden_acts = (jax.nn.silu(gate_acts) * up_acts).astype(jnp.bfloat16)
    partial_value = jnp.einsum("scf,fd->scd", hidden_acts, w_down, preferred_element_type=jnp.float32)
    return partial_value.astype(jnp.bfloat16)


def body(tokens, w_gate, w_up, w_down, routes, gate_levels, ancestors):
    local_rows = routes.shape[0]
    choose = routes.shape[1]
    groups = lax.axis_size("expert")
    local_experts = w_gate.shape[0]
    experts = local_experts * groups
    capacity = 3 * local_rows * choose // (2 * experts)
    pairs = local_rows * choose
    chosen = routes.reshape(-1)
    one_hot = (chosen[:, None] == jnp.arange(experts, dtype=jnp.int32)[None, :]).astype(jnp.bfloat16)
    lower = jnp.arange(pairs, dtype=jnp.int32)
    tri = (lower[:, None] > lower[None, :]).astype(jnp.bfloat16)
    earlier = jnp.dot(tri, one_hot, preferred_element_type=jnp.float32)
    places = jnp.sum(earlier * one_hot.astype(jnp.float32), 1).astype(jnp.int32)
    target = chosen * capacity + places
    row_ids = jnp.arange(pairs, dtype=jnp.int32) // choose
    slot_rows = jnp.zeros((experts * capacity,), jnp.int32).at[target].set(row_ids)
    slot_rows = slot_rows.reshape(groups, local_experts, capacity)
    per_expert = []
    for c in range(local_experts):
        send = tokens[slot_rows[:, c]]
        arrived = lax.all_to_all(send, "expert", split_axis=0, concat_axis=0, tiled=True)
        full = lax.all_gather(arrived, "hidden", axis=2, tiled=True)
        part = expert_part(full, w_gate[c], w_up[c], w_down[c])
        summed = lax.psum_scatter(part, "hidden", scatter_dimension=2, tiled=True)
        per_expert.append(lax.all_to_all(summed, "expert", split_axis=0, concat_axis=0, tiled=True))
    returned = jnp.stack(per_expert, 1)
    returned = returned.reshape(experts * capacity, returned.shape[3])
    source = target.reshape(local_rows, choose)[ancestors]
    levels = gate_levels.astype(jnp.float32)[ancestors]
    weights = levels / jnp.sum(levels, 1, keepdims=True)
    picked = returned[source].astype(jnp.float32)
    combined = jnp.sum(weights[:, :, None] * picked, 1)
    return combined.astype(jnp.bfloat16)


def solution(mesh):
    placed = (
        P("expert", "hidden"),
        P("expert", None, "hidden"),
        P("expert", None, "hidden"),
        P("expert", "hidden", None),
        P("expert", None),
        P("expert", None),
        P("expert"),
    )
    return jax.shard_map(
        body, mesh=mesh, in_specs=placed, out_specs=P("expert", "hidden"), check_vma=False
    )
```

profile of v0, /device:TPU:1, one launch (start us, length us, event | category | flops | bytes accessed | tf_op | source)
XLA Modules:
  0.0 359.0 jit_solution(3482871126563848769)
XLA Ops:
  6.5 0.0 copy-start
  6.5 0.0 all-gather.3.cloned.1.call-start
  6.5 0.8 copy.12
  7.4 0.1 eq.15
  7.5 0.6 fusion.31
  8.1 0.1 convert_element_type.54
  8.2 0.1 mul.44
  8.3 4.3 %scatter_custom_fusion = s32[1536]{0:T(1024)S(1)} fusion(s32[1024]{0:T(1024)S(1)} %bitcast.70, s32[1024]{0:T(1024)S(1)} %add_select_fusion, s32[]{:T(128)} %constant.12.clone.1), kind=kCustom, calls=%fused_computation.55 | custom fusion | bytes 6148 | tf_op jit(solution)/shard_map/scatter | solution.py:30
  12.6 0.1 reshape.130
  12.8 0.1 reshape.142
  12.9 2.8 gather_fusion.1
  15.7 31.3 %all_to_all.20 = bf16[32,24,1024]{2,1,0:T(8,128)(2,1)} all-to-all(bf16[32,24,1024]{2,1,0:T(8,128)(2,1)S(1)} %bitcast.65), channel_id=1, replica_groups=mesh['expert'=32,'hidden'=4] {'expert'}, dimensions={0} | all-to-all | bytes 3145728 | tf_op jit(solution)/shard_map/all_to_all | solution.py:35
  47.0 0.0 all-gather.3.cloned.1.call-update
  47.1 0.0 all-gather.5.cloned.1.call-start
  47.1 0.1 reshape.150
  47.2 2.8 gather_fusion.2
  50.0 26.4 %all_to_all.21 = bf16[32,24,1024]{2,1,0:T(8,128)(2,1)} all-to-all(bf16[32,24,1024]{2,1,0:T(8,128)(2,1)S(1)} %bitcast.66), channel_id=1, replica_groups=mesh['expert'=32,'hidden'=4] {'expert'}, dimensions={0} | all-to-all | bytes 3145728 | tf_op jit(solution)/shard_map/all_to_all | solution.py:35
  76.4 0.0 all-gather.5.cloned.1.call-update
  76.4 0.0 reduce-scatter.3.cloned.1.call-start
  76.5 34.7 %all-gather.3.cloned.1.call-done = bf16[32,24,4096]{2,1,0:T(8,128)(2,1)} async-done(((bf16[32,24,1024]{2,1,0:T(8,128)(2,1)}), bf16[32,24,4096]{2,1,0:T(8,128)(2,1)}) %all-gather.3.cloned.1.call-update) | async-done | bytes 6291472 | tf_op jit(solution)/shard_map/all_gather | solution.py:36
  111.1 6.5 %fusion.10 = f32[32,24,384]{2,1,0:T(8,128)S(1)} fusion(bf16[32,24,4096]{2,1,0:T(8,128)(2,1)} %all-gather.3.cloned.1.call-done, bf16[2,4096,384]{2,1,0:T(8,128)(2,1)} %param.8), kind=kOutput, calls=%fused_computation.21 | convolution fusion | flops 2415919104 | bytes 10616832 | tf_op jit(solution)/shard_map/scd,df->scf/dot_general | solution.py:7
  117.6 12.4 %convolution_convert_fusion.1 = bf16[32,24,4096]{2,1,0:T(8,128)(2,1)} fusion(bf16[2,384,4096]{2,1,0:T(8,128)(2,1)} %param.10, bf16[32,24,4096]{2,1,0:T(8,128)(2,1)} %all-gather.3.cloned.1.call-done, bf16[2,4096,384]{2,1,0:T(8,128)(2,1)} %param.9, f32[32,24,384]{2,1,0:T(8,128)S(1)} %fusion.10), kind=kOutput, calls=%fused_computation.7 | convolution fusion | flops 4836753408 | bytes 20054016 | tf_op jit(solution)/shard_map/scf,fd->scd/dot_general | solution.py:10
  130.0 0.0 reduce-scatter.3.cloned.1.call-update
  130.0 0.2 reduce-scatter.5.cloned.1.call-start
  130.3 48.9 %all-gather.5.cloned.1.call-done = bf16[32,24,4096]{2,1,0:T(8,128)(2,1)} async-done(((bf16[32,24,1024]{2,1,0:T(8,128)(2,1)}), bf16[32,24,4096]{2,1,0:T(8,128)(2,1)}) %all-gather.5.cloned.1.call-update) | async-done | bytes 6291472 | tf_op jit(solution)/shard_map/all_gather | solution.py:36
  179.2 6.5 %fusion.5 = f32[32,24,384]{2,1,0:T(8,128)S(1)} fusion(bf16[32,24,4096]{2,1,0:T(8,128)(2,1)} %all-gather.5.cloned.1.call-done, bf16[2,4096,384]{2,1,0:T(8,128)(2,1)} %param.8), kind=kOutput, calls=%fused_computation.16 | convolution fusion | flops 2415919104 | bytes 10616832 | tf_op jit(solution)/shard_map/scd,df->scf/dot_general | solution.py:7
  185.6 12.4 %convolution_convert_fusion = bf16[32,24,4096]{2,1,0:T(8,128)(2,1)} fusion(bf16[2,384,4096]{2,1,0:T(8,128)(2,1)} %param.10, bf16[32,24,4096]{2,1,0:T(8,128)(2,1)} %all-gather.5.cloned.1.call-done, bf16[2,4096,384]{2,1,0:T(8,128)(2,1)} %param.9, f32[32,24,384]{2,1,0:T(8,128)S(1)} %fusion.5), kind=kOutput, calls=%fused_computation.6 | convolution fusion | flops 4836753408 | bytes 20054016 | tf_op jit(solution)/shard_map/scf,fd->scd/dot_general | solution.py:10
  198.1 0.0 reduce-scatter.5.cloned.1.call-update
  198.1 0.0 copy-start.3
  198.1 0.0 copy-start.2
  198.1 48.3 %reduce-scatter.3.cloned.1.call-done = bf16[32,24,1024]{2,1,0:T(8,128)(2,1)} async-done(((bf16[32,24,4096]{2,1,0:T(8,128)(2,1)}), bf16[32,24,1024]{2,1,0:T(8,128)(2,1)}) %reduce-scatter.3.cloned.1.call-update) | async-done | bytes 1572880 | tf_op jit(solution)/shard_map/reduce_scatter | solution.py:38
  246.4 7.6 %all-to-all-start.1 = ((bf16[32,24,1024]{2,1,0:T(8,128)(2,1)}), bf16[32,24,1024]{2,1,0:T(8,128)(2,1)S(1)}, u32[]{:S(2)}, u32[]{:S(2)}) async-start(bf16[32,24,1024]{2,1,0:T(8,128)(2,1)} %reduce-scatter.3.cloned.1.call-done), calls=%async_computation.2 | async-start | bytes 3145728 | tf_op jit(solution)/shard_map/all_to_all | solution.py:39
  254.0 58.5 %reduce-scatter.5.cloned.1.call-done = bf16[32,24,1024]{2,1,0:T(8,128)(2,1)} async-done(((bf16[32,24,4096]{2,1,0:T(8,128)(2,1)}), bf16[32,24,1024]{2,1,0:T(8,128)(2,1)}) %reduce-scatter.5.cloned.1.call-update) | async-done | bytes 1572880 | tf_op jit(solution)/shard_map/reduce_scatter | solution.py:38
  312.5 0.0 all-to-all-done.1
  312.5 7.6 %all-to-all-start.3 = ((bf16[32,24,1024]{2,1,0:T(8,128)(2,1)}), bf16[32,24,1024]{2,1,0:T(8,128)(2,1)S(1)}, u32[]{:S(2)}, u32[]{:S(2)}) async-start(bf16[32,24,1024]{2,1,0:T(8,128)(2,1)} %reduce-scatter.5.cloned.1.call-done), calls=%async_computation.5 | async-start | bytes 3145728 | tf_op jit(solution)/shard_map/all_to_all | solution.py:39
  320.1 0.0 copy-done.3
  320.1 0.6 gather_fusion.3
  320.8 0.1 reshape.166
  320.9 0.1 copy.11
  321.0 0.6 gather_fusion
  321.6 0.1 reduce_sum.27
  321.8 0.1 broadcast_divide_fusion
  321.9 20.9 %all-to-all-done.3 = bf16[32,24,1024]{2,1,0:T(8,128)(2,1)S(1)} async-done(((bf16[32,24,1024]{2,1,0:T(8,128)(2,1)}), bf16[32,24,1024]{2,1,0:T(8,128)(2,1)S(1)}, u32[]{:S(2)}, u32[]{:S(2)}) %all-to-all-start.3) | async-done | bytes 1572896 | tf_op jit(solution)/shard_map/all_to_all | solution.py:39
  342.8 0.3 pad_maximum_fusion
  343.0 0.4 copy.15
  343.5 0.0 copy-start.1
  343.5 5.3 %gather_fusion.4 = bf16[1024,1024]{1,0:T(8,128)(2,1)} fusion(bf16[1536,1024]{1,0:T(8,128)(2,1)S(1)} %bitcast.62, s32[1024]{0:T(1024)S(1)} %broadcast_clamp_fusion), kind=kCustom, calls=%fused_computation.4 | custom fusion | bytes 4198400 | tf_op jit(solution)/shard_map/gather | solution.py:45
  348.8 3.7 %fusion = bf16[128,1024]{1,0:T(8,128)(2,1)} fusion(bf16[1024,1024]{1,0:T(8,128)(2,1)} %gather_fusion.4, f32[128,8]{1,0:T(8,128)S(1)} %broadcast_divide_fusion), kind=kLoop, calls=%fused_computation.9 | loop fusion | flops 3014656 | bytes 2363392 | tf_op jit(solution)/shard_map/reduce_sum | solution.py:46
  (17 shorter events, 0.1 us)
Async XLA Ops:
  6.5 6.4 %copy-start = (bf16[128,1024]{1,0:T(8,128)(2,1)S(1)}, bf16[128,1024]{1,0:T(8,128)(2,1)}, u32[]{:S(2)}) copy-start(bf16[128,1024]{1,0:T(8,128)(2,1)} %param.7) | copy-start | bytes 786436
  6.5 104.6 %all-gather.3.cloned.1.call-start = ((), (), s32[]{:S(2)}) async-start(), calls=%async_computation.6 | async-start | bytes 7864320 | tf_op jit(solution)/shard_map/all_gather | solution.py:36
  47.1 132.1 %all-gather.5.cloned.1.call-start = ((), (), s32[]{:S(2)}) async-start(), calls=%async_computation.8 | async-start | bytes 7864320 | tf_op jit(solution)/shard_map/all_gather | solution.py:36
  76.4 170.0 %reduce-scatter.3.cloned.1.call-start = ((), (), s32[]{:S(2)}) async-start(), calls=%async_computation.7 | async-start | bytes 7864320 | tf_op jit(solution)/shard_map/reduce_scatter | solution.py:38
  130.0 182.5 %reduce-scatter.5.cloned.1.call-start = ((), (), s32[]{:S(2)}) async-start(), calls=%async_computation.9 | async-start | bytes 7864320 | tf_op jit(solution)/shard_map/reduce_scatter | solution.py:38
  198.1 122.0 %copy-start.3 = (s32[128]{0:T(128)S(1)}, s32[128]{0:T(128)}, u32[]{:S(2)}) copy-start(s32[128]{0:T(128)} %param.13) | copy-start | bytes 1540
  198.1 122.8 %copy-start.2 = (s32[128,8]{0,1:T(8,128)S(1)}, s32[128,8]{0,1:T(8,128)}, u32[]{:S(2)}) copy-start(s32[128,8]{0,1:T(8,128)} %param.12) | copy-start | bytes 12292
  246.4 66.1 %all-to-all-start.1 = ((bf16[32,24,1024]{2,1,0:T(8,128)(2,1)}), bf16[32,24,1024]{2,1,0:T(8,128)(2,1)S(1)}, u32[]{:S(2)}, u32[]{:S(2)}) async-start(bf16[32,24,1024]{2,1,0:T(8,128)(2,1)} %reduce-scatter.3.cloned.1.call-done), calls=%async_computation.2 | async-start | bytes 3145728 | tf_op jit(solution)/shard_map/all_to_all | solution.py:39
  312.5 30.3 %all-to-all-start.3 = ((bf16[32,24,1024]{2,1,0:T(8,128)(2,1)}), bf16[32,24,1024]{2,1,0:T(8,128)(2,1)S(1)}, u32[]{:S(2)}, u32[]{:S(2)}) async-start(bf16[32,24,1024]{2,1,0:T(8,128)(2,1)} %reduce-scatter.5.cloned.1.call-done), calls=%async_computation.5 | async-start | bytes 3145728 | tf_op jit(solution)/shard_map/all_to_all | solution.py:39
  343.5 9.0 %copy-start.1 = (bf16[128,1024]{1,0:T(8,128)(2,1)S(1)}, bf16[128,1024]{1,0:T(8,128)(2,1)}, u32[]{:S(2)}) copy-start(bf16[128,1024]{1,0:T(8,128)(2,1)} %param.7) | copy-start | bytes 786436
Sparse Core Ops, SparseCore 0:
  47.2 63.9 all-gather.2
  112.8 66.3 all-gather.4
  181.6 64.7 reduce-scatter.2
  248.7 63.7 reduce-scatter.4
where the time goes:
time: 359 us
  waiting for transfers between devices  211 us (59%)
  blocking collectives  57.7 us (16%)
  matrix products  38.3 us (11%)
  local copies, waits for them, and re-layouts  18.6 us (5%)
  starting transfers between devices  15.5 us (4%)
  between operations  13.4 us (4%)
  other arithmetic  4.21 us (1%)
    reduce_scatter x2, waiting for transfers between devices, body(): summed = lax.psum_scatter(part, 'hidden', scatter_dimension=2, tiled=True)  107 us
    all_gather x2, waiting for transfers between devices, body(): full = lax.all_gather(arrived, 'hidden', axis=2, tiled=True)  83.6 us
    all_to_all x2, blocking collectives, body(): lax.all_to_all(send, 'expert', split_axis=0, concat_axis=0, tiled=True)  57.7 us
    dot_general x2, matrix products, expert_part(): jnp.einsum('scf,fd->scd', hidden_acts, w_down, preferred_element_type=jnp...  24.8 us
    all_to_all x2, waiting for transfers between devices, body(): lax.all_to_all(summed, 'expert', split_axis=0, concat_axis=0, tiled=True)  20.9 us
    all_to_all x2, starting transfers between devices, body(): lax.all_to_all(summed, 'expert', split_axis=0, concat_axis=0, tiled=True)  15.2 us
    dot_general x2, matrix products, expert_part(): jnp.einsum('scd,df->scf', arrived, w_gate, preferred_element_type=jnp.flo...  12.9 us
  transfers between devices with their start and end apart: 6, of which 5 were waited for; matrix products, arithmetic and copies ran while one was open for 12% of the time, Pallas kernels for 0%

commit v1 on v0

--- a/solution.py
+++ b/solution.py
@@ -9,6 +9,18 @@
     hidden_acts = (jax.nn.silu(gate_acts) * up_acts).astype(jnp.bfloat16)
     partial_value = jnp.einsum("scf,fd->scd", hidden_acts, w_down, preferred_element_type=jnp.float32)
     return partial_value.astype(jnp.bfloat16)
+
+
+def gather_hidden(piece):
+    size = lax.axis_size("hidden")
+    here = lax.axis_index("hidden")
+    shifted = [piece] + [
+        lax.ppermute(piece, "hidden", [(i, (i + k) % size) for i in range(size)])
+        for k in range(1, size)
+    ]
+    order = (here - jnp.arange(size, dtype=jnp.int32)) % size
+    stacked = jnp.take(jnp.stack(shifted, 0), order, axis=0)
+    return jnp.moveaxis(stacked, 0, -2).reshape(piece.shape[:-1] + (size * piece.shape[-1],))
 
 
 def body(tokens, w_gate, w_up, w_down, routes, gate_levels, ancestors):
@@ -33,7 +45,7 @@
     for c in range(local_experts):
         send = tokens[slot_rows[:, c]]
         arrived = lax.all_to_all(send, "expert", split_axis=0, concat_axis=0, tiled=True)
-        full = lax.all_gather(arrived, "hidden", axis=2, tiled=True)
+        full = gather_hidden(arrived)
         part = expert_part(full, w_gate[c], w_up[c], w_down[c])
         summed = lax.psum_scatter(part, "hidden", scatter_dimension=2, tiled=True)
         per_expert.append(lax.all_to_all(summed, "expert", split_axis=0, concat_axis=0, tiled=True))

time: 359 us -> 422 us (1.18)
  blocking collectives: 57.7 us -> 0 us
  waiting for transfers between devices: 211 us -> 261 us
  local copies, waits for them, and re-layouts: 18.6 us -> 45.3 us
  starting transfers between devices: 15.5 us -> 38.7 us
  other arithmetic: 4.21 us -> 26.5 us
    ppermute x0 -> x6, waiting for transfers between devices: none -> 98.4 us  [gather_hidden(): lax.ppermute(piece, 'hidden', [(i, (i + k) % size) for i in range(size)])]
    all_gather x2 -> x0, waiting for transfers between devices: 83.6 us -> none  [body(): full = lax.all_gather(arrived, 'hidden', axis=2, tiled=True)]
    all_to_all x2 -> x0, blocking collectives: 57.7 us -> none  [body(): lax.all_to_all(send, 'expert', split_axis=0, concat_axis=0, tiled=True)]
    all_to_all x0 -> x2, waiting for transfers between devices: none -> 41.2 us  [body(): lax.all_to_all(send, 'expert', split_axis=0, concat_axis=0, tiled=True)]
    all_to_all x0 -> x2, starting transfers between devices: none -> 13 us  [body(): lax.all_to_all(send, 'expert', split_axis=0, concat_axis=0, tiled=True)]
    gather x0 -> x2, local copies, waits for them, and re-layouts: none -> 12.7 us  [gather_hidden(): stacked = jnp.take(jnp.stack(shifted, 0), order, axis=0)]
    another operation x0 -> x2, other arithmetic: none -> 11.8 us  [gather_hidden(): stacked = jnp.take(jnp.stack(shifted, 0), order, axis=0)]
    unnamed x0 -> x2, other arithmetic: none -> 10.5 us
  transfers between devices with their start and end apart: 6 -> 12, of which waited for: 5 -> 11; matrix products, arithmetic and copies ran while one was open for 12% -> 9% of each run, Pallas kernels for 0% -> 0%
where the time goes in v1:
time: 422 us; the launch traced here: 421 us
  waiting for transfers between devices  261 us (62%)
  local copies, waits for them, and re-layouts  45.3 us (11%)
  starting transfers between devices  38.7 us (9%)
  matrix products  36.1 us (9%)
  other arithmetic  26.5 us (6%)
  between operations  13.7 us (3%)
    reduce_scatter x2, waiting for transfers between devices, body(): summed = lax.psum_scatter(part, 'hidden', scatter_dimension=2, tiled=True)  101 us
    ppermute x6, waiting for transfers between devices, gather_hidden(): lax.ppermute(piece, 'hidden', [(i, (i + k) % size) for i in range(size)])  98.4 us
    all_to_all x2, waiting for transfers between devices, body(): lax.all_to_all(send, 'expert', split_axis=0, concat_axis=0, tiled=True)  41.2 us
    dot_general x2, matrix products, expert_part(): jnp.einsum('scf,fd->scd', hidden_acts, w_down, preferred_element_type=jnp...  25.6 us
    all_to_all x2, waiting for transfers between devices, body(): lax.all_to_all(summed, 'expert', split_axis=0, concat_axis=0, tiled=True)  20.9 us
    all_to_all x2, starting transfers between devices, body(): lax.all_to_all(summed, 'expert', split_axis=0, concat_axis=0, tiled=True)  15.2 us
    all_to_all x2, starting transfers between devices, body(): lax.all_to_all(send, 'expert', split_axis=0, concat_axis=0, tiled=True)  13 us
    gather x2, local copies, waits for them, and re-layouts, gather_hidden(): stacked = jnp.take(jnp.stack(shifted, 0), order, axis=0)  12.7 us
  transfers between devices with their start and end apart: 12, of which 11 were waited for; matrix products, arithmetic and copies ran while one was open for 9% of the time, Pallas kernels for 0%

profile of v1, /device:TPU:1, one launch (start us, length us, event | category | flops | bytes accessed | tf_op | source)
XLA Modules:
  0.0 421.4 jit_solution(6862483787344179958)
XLA Ops:
  6.5 0.8 copy.14
  7.5 0.6 fusion.31
  8.3 4.3 %scatter_custom_fusion = s32[1536]{0:T(1024)S(1)} fusion(s32[1024]{0:T(1024)S(1)} %bitcast.91, s32[1024]{0:T(1024)S(1)} %add_select_fusion, s32[]{:T(128)} %constant.55.clone.1), kind=kCustom, calls=%fused_computation.62 | custom fusion | bytes 6148 | tf_op jit(solution)/shard_map/scatter | solution.py:42
  12.6 0.1 reshape.141
  12.9 3.6 gather_fusion.2
  16.5 8.6 %all-to-all-start.2 = ((bf16[32,24,1024]{2,1,0:T(8,128)(2,1)}), bf16[32,24,1024]{2,1,0:T(8,128)(2,1)S(1)}, u32[]{:S(2)}, u32[]{:S(2)}) async-start(bf16[32,24,1024]{2,1,0:T(8,128)(2,1)} %bitcast.17), calls=%async_computation.3 | async-start | bytes 3145728 | tf_op jit(solution)/shard_map/all_to_all | solution.py:47
  25.2 22.6 %all-to-all-done.2 = bf16[32,24,1024]{2,1,0:T(8,128)(2,1)S(1)} async-done(((bf16[32,24,1024]{2,1,0:T(8,128)(2,1)}), bf16[32,24,1024]{2,1,0:T(8,128)(2,1)S(1)}, u32[]{:S(2)}, u32[]{:S(2)}) %all-to-all-start.2) | async-done | bytes 1572896 | tf_op jit(solution)/shard_map/all_to_all | solution.py:47
  47.7 1.6 collective-permute-start.3
  49.4 3.6 gather_fusion.1
  53.0 4.4 %all-to-all-start = ((bf16[32,24,1024]{2,1,0:T(8,128)(2,1)}), bf16[32,24,1024]{2,1,0:T(8,128)(2,1)S(1)}, u32[]{:S(2)}, u32[]{:S(2)}) async-start(bf16[32,24,1024]{2,1,0:T(8,128)(2,1)} %bitcast.87), calls=%async_computation | async-start | bytes 3145728 | tf_op jit(solution)/shard_map/all_to_all | solution.py:47
  57.5 3.4 collective-permute-start.4
  60.8 0.7 collective-permute-start.5
  61.6 18.6 %all-to-all-done = bf16[32,24,1024]{2,1,0:T(8,128)(2,1)S(1)} async-done(((bf16[32,24,1024]{2,1,0:T(8,128)(2,1)}), bf16[32,24,1024]{2,1,0:T(8,128)(2,1)S(1)}, u32[]{:S(2)}, u32[]{:S(2)}) %all-to-all-start) | async-done | bytes 1572896 | tf_op jit(solution)/shard_map/all_to_all | solution.py:47
  80.2 1.6 collective-permute-start
  81.8 1.7 collective-permute-start.1
  83.5 2.4 collective-permute-done.3
  85.8 1.2 collective-permute-start.2
  87.1 33.4 %collective-permute-done.4 = bf16[32,24,1024]{2,1,0:T(8,128)(2,1)} collective-permute-done((bf16[32,24,1024]{2,1,0:T(8,128)(2,1)S(1)}, bf16[32,24,1024]{2,1,0:T(8,128)(2,1)}, u32[]{:S(2)}, u32[]{:S(2)}) %collective-permute-start.4) | collective-permute-done | bytes 1572896 | tf_op jit(solution)/shard_map/ppermute | solution.py:18
  120.5 7.5 %collective-permute-done.5 = bf16[32,24,1024]{2,1,0:T(8,128)(2,1)} collective-permute-done((bf16[32,24,1024]{2,1,0:T(8,128)(2,1)S(1)}, bf16[32,24,1024]{2,1,0:T(8,128)(2,1)}, u32[]{:S(2)}, u32[]{:S(2)}) %collective-permute-start.5) | collective-permute-done | bytes 1572896 | tf_op jit(solution)/shard_map/ppermute | solution.py:18
  128.0 5.9 %pad_maximum_fusion.1 = bf16[4,32,24,1024]{3,2,1,0:T(8,128)(2,1)} fusion(bf16[1,32,24,1024]{3,2,1,0:T(8,128)(2,1)} %bitcast.21, bf16[1,32,24,1024]{3,2,1,0:T(8,128)(2,1)} %bitcast.20, bf16[1,32,24,1024]{3,2,1,0:T(8,128)(2,1)} %bitcast.19, bf16[1,32,24,1024]{3,2,1,0:T(8,128)(2,1)S(1)} %bitcast.83), kind=kLoop, calls=%fused_computation.11 | loop fusion | flops 9437184 | bytes 12582912 | tf_op jit(solution)/shard_map/stack | solution.py:22
  133.8 6.4 %gather_fusion.6 = bf16[4,32,24,1024]{3,2,1,0:T(8,128)(2,1)} fusion(bf16[4,32,24,1024]{3,2,1,0:T(8,128)(2,1)} %pad_maximum_fusion.1, s32[1024]{0:T(1024)S(1)} %pad_clamp_fusion.1), kind=kCustom, calls=%fused_computation.1.clone | custom fusion | bytes 12582928 | tf_op jit(solution)/shard_map/jit(_take)/gather | solution.py:22
  140.2 13.0 %collective-permute-done = bf16[32,24,1024]{2,1,0:T(8,128)(2,1)} collective-permute-done((bf16[32,24,1024]{2,1,0:T(8,128)(2,1)S(1)}, bf16[32,24,1024]{2,1,0:T(8,128)(2,1)}, u32[]{:S(2)}, u32[]{:S(2)}) %collective-permute-start) | collective-permute-done | bytes 1572896 | tf_op jit(solution)/shard_map/ppermute | solution.py:18
  153.2 34.6 %collective-permute-done.1 = bf16[32,24,1024]{2,1,0:T(8,128)(2,1)} collective-permute-done((bf16[32,24,1024]{2,1,0:T(8,128)(2,1)S(1)}, bf16[32,24,1024]{2,1,0:T(8,128)(2,1)}, u32[]{:S(2)}, u32[]{:S(2)}) %collective-permute-start.1) | collective-permute-done | bytes 1572896 | tf_op jit(solution)/shard_map/ppermute | solution.py:18
  187.9 7.5 %collective-permute-done.2 = bf16[32,24,1024]{2,1,0:T(8,128)(2,1)} collective-permute-done((bf16[32,24,1024]{2,1,0:T(8,128)(2,1)S(1)}, bf16[32,24,1024]{2,1,0:T(8,128)(2,1)}, u32[]{:S(2)}, u32[]{:S(2)}) %collective-permute-start.2) | collective-permute-done | bytes 1572896 | tf_op jit(solution)/shard_map/ppermute | solution.py:18
  195.4 5.9 %pad_maximum_fusion = bf16[4,32,24,1024]{3,2,1,0:T(8,128)(2,1)} fusion(bf16[1,32,24,1024]{3,2,1,0:T(8,128)(2,1)} %bitcast.7, bf16[1,32,24,1024]{3,2,1,0:T(8,128)(2,1)} %bitcast.6, bf16[1,32,24,1024]{3,2,1,0:T(8,128)(2,1)} %bitcast.5, bf16[1,32,24,1024]{3,2,1,0:T(8,128)(2,1)S(1)} %bitcast.84), kind=kLoop, calls=%fused_computation.10 | loop fusion | flops 9437184 | bytes 12582912 | tf_op jit(solution)/shard_map/stack | solution.py:22
  201.3 6.3 %gather_fusion.5 = bf16[4,32,24,1024]{3,2,1,0:T(8,128)(2,1)} fusion(bf16[4,32,24,1024]{3,2,1,0:T(8,128)(2,1)} %pad_maximum_fusion, s32[1024]{0:T(1024)S(1)} %pad_clamp_fusion.1), kind=kCustom, calls=%fused_computation.clone | custom fusion | bytes 12582928 | tf_op jit(solution)/shard_map/jit(_take)/gather | solution.py:22
  207.6 10.5 %select_bitcast_fusion.1 = (bf16[4,32,3,8,1024]{4,3,2,1,0:T(8,128)(2,1)}, bf16[4,32,3,8,1024]{4,3,2,1,0:T(8,128)(2,1)}) fusion(bf16[4,32,24,1024]{3,2,1,0:T(8,128)(2,1)} %gather_fusion.5, pred[4]{0:T(512)(128)(4,1)S(1)} %compare_and_fusion, bf16[4,32,24,1024]{3,2,1,0:T(8,128)(2,1)} %gather_fusion.6), kind=kLoop, calls=%fused_computation.13 | loop fusion | flops 6291456 | bytes 25165828
  218.1 3.5 copy.21
  221.6 2.6 copy-done.2
  224.2 5.3 %fusion.10 = f32[32,24,384]{2,1,0:T(8,128)S(1)} fusion(bf16[32,24,4096]{2,1,0:T(8,128)(2,1)S(1)} %bitcast.79, bf16[2,4096,384]{2,1,0:T(8,128)(2,1)} %param.10), kind=kOutput, calls=%fused_computation.27 | convolution fusion | flops 2415919104 | bytes 10616832 | tf_op jit(solution)/shard_map/scd,df->scf/dot_general | solution.py:7
  229.5 12.4 %convolution_convert_fusion.1 = bf16[32,24,4096]{2,1,0:T(8,128)(2,1)} fusion(bf16[2,384,4096]{2,1,0:T(8,128)(2,1)} %param.12, bf16[32,24,4096]{2,1,0:T(8,128)(2,1)} %bitcast.80, bf16[2,4096,384]{2,1,0:T(8,128)(2,1)} %param.11, f32[32,24,384]{2,1,0:T(8,128)S(1)} %fusion.10), kind=kOutput, calls=%fused_computation.9 | convolution fusion | flops 4836753408 | bytes 20054016 | tf_op jit(solution)/shard_map/scf,fd->scd/dot_general | solution.py:10
  242.0 0.3 reduce-scatter.5.cloned.1.call-start
  242.3 3.7 copy.22
  246.0 2.6 copy-done.3
  248.6 4.5 %fusion.5 = f32[32,24,384]{2,1,0:T(8,128)} fusion(bf16[32,24,4096]{2,1,0:T(8,128)(2,1)S(1)} %bitcast.81, bf16[2,4096,384]{2,1,0:T(8,128)(2,1)S(1)} %bitcast.93), kind=kOutput, calls=%fused_computation.22 | convolution fusion | flops 2415919104 | bytes 10616832 | tf_op jit(solution)/shard_map/scd,df->scf/dot_general | solution.py:7
  253.1 13.2 %convolution_convert_fusion = bf16[32,24,4096]{2,1,0:T(8,128)(2,1)} fusion(bf16[2,384,4096]{2,1,0:T(8,128)(2,1)} %param.12, bf16[32,24,4096]{2,1,0:T(8,128)(2,1)} %bitcast.82, bf16[2,4096,384]{2,1,0:T(8,128)(2,1)} %param.11, f32[32,24,384]{2,1,0:T(8,128)} %fusion.5), kind=kOutput, calls=%fused_computation.8 | convolution fusion | flops 4836753408 | bytes 20054016 | tf_op jit(solution)/shard_map/scf,fd->scd/dot_general | solution.py:10
  266.3 41.9 %reduce-scatter.3.cloned.1.call-done = bf16[32,24,1024]{2,1,0:T(8,128)(2,1)} async-done(((bf16[32,24,4096]{2,1,0:T(8,128)(2,1)}), bf16[32,24,1024]{2,1,0:T(8,128)(2,1)}) %reduce-scatter.3.cloned.1.call-update) | async-done | bytes 1572880 | tf_op jit(solution)/shard_map/reduce_scatter | solution.py:50
  308.3 7.6 %all-to-all-start.1 = ((bf16[32,24,1024]{2,1,0:T(8,128)(2,1)}), bf16[32,24,1024]{2,1,0:T(8,128)(2,1)S(1)}, u32[]{:S(2)}, u32[]{:S(2)}) async-start(bf16[32,24,1024]{2,1,0:T(8,128)(2,1)} %reduce-scatter.3.cloned.1.call-done), calls=%async_computation.2 | async-start | bytes 3145728 | tf_op jit(solution)/shard_map/all_to_all | solution.py:51
  315.9 58.6 %reduce-scatter.5.cloned.1.call-done = bf16[32,24,1024]{2,1,0:T(8,128)(2,1)} async-done(((bf16[32,24,4096]{2,1,0:T(8,128)(2,1)}), bf16[32,24,1024]{2,1,0:T(8,128)(2,1)}) %reduce-scatter.5.cloned.1.call-update) | async-done | bytes 1572880 | tf_op jit(solution)/shard_map/reduce_scatter | solution.py:50
  374.5 7.6 %all-to-all-start.3 = ((bf16[32,24,1024]{2,1,0:T(8,128)(2,1)}), bf16[32,24,1024]{2,1,0:T(8,128)(2,1)S(1)}, u32[]{:S(2)}, u32[]{:S(2)}) async-start(bf16[32,24,1024]{2,1,0:T(8,128)(2,1)} %reduce-scatter.5.cloned.1.call-done), calls=%async_computation.5 | async-start | bytes 3145728 | tf_op jit(solution)/shard_map/all_to_all | solution.py:51
  382.1 0.6 gather_fusion.3
  383.0 0.6 gather_fusion
  383.6 0.1 reduce_sum.27
  383.8 20.9 %all-to-all-done.3 = bf16[32,24,1024]{2,1,0:T(8,128)(2,1)S(1)} async-done(((bf16[32,24,1024]{2,1,0:T(8,128)(2,1)}), bf16[32,24,1024]{2,1,0:T(8,128)(2,1)S(1)}, u32[]{:S(2)}, u32[]{:S(2)}) %all-to-all-start.3) | async-done | bytes 1572896 | tf_op jit(solution)/shard_map/all_to_all | solution.py:51
  404.7 0.3 pad_maximum_fusion.2
  405.0 0.4 copy.19
  405.5 5.4 %gather_fusion.4 = bf16[1024,1024]{1,0:T(8,128)(2,1)} fusion(bf16[1536,1024]{1,0:T(8,128)(2,1)S(1)} %bitcast.78, s32[1024]{0:T(1024)S(1)} %broadcast_clamp_fusion), kind=kCustom, calls=%fused_computation.6 | custom fusion | bytes 4198400 | tf_op jit(solution)/shard_map/gather | solution.py:57
  410.9 3.7 fusion
  (44 shorter events, 1.0 us)
Async XLA Ops:
  6.5 6.4 %copy-start = (bf16[128,1024]{1,0:T(8,128)(2,1)S(1)}, bf16[128,1024]{1,0:T(8,128)(2,1)}, u32[]{:S(2)}) copy-start(bf16[128,1024]{1,0:T(8,128)(2,1)} %param.9) | copy-start | bytes 786436
  16.5 31.2 %all-to-all-start.2 = ((bf16[32,24,1024]{2,1,0:T(8,128)(2,1)}), bf16[32,24,1024]{2,1,0:T(8,128)(2,1)S(1)}, u32[]{:S(2)}, u32[]{:S(2)}) async-start(bf16[32,24,1024]{2,1,0:T(8,128)(2,1)} %bitcast.17), calls=%async_computation.3 | async-start | bytes 3145728 | tf_op jit(solution)/shard_map/all_to_all | solution.py:47
  47.7 38.1 %collective-permute-start.3 = (bf16[32,24,1024]{2,1,0:T(8,128)(2,1)S(1)}, bf16[32,24,1024]{2,1,0:T(8,128)(2,1)}, u32[]{:S(2)}, u32[]{:S(2)}) collective-permute-start(bf16[32,24,1024]{2,1,0:T(8,128)(2,1)S(1)} %all-to-all-done.2), channel_id=1, source_target_pairs={{0,1},{1,2},{2,3},{3,0},{4,5},{5,6},{6,7},{7,4},{8,9},{9,10},{10,1... | collective-permute-start | bytes 4718600 | tf_op jit(solution)/shard_map/ppermute | solution.py:18
  53.0 27.2 %all-to-all-start = ((bf16[32,24,1024]{2,1,0:T(8,128)(2,1)}), bf16[32,24,1024]{2,1,0:T(8,128)(2,1)S(1)}, u32[]{:S(2)}, u32[]{:S(2)}) async-start(bf16[32,24,1024]{2,1,0:T(8,128)(2,1)} %bitcast.87), calls=%async_computation | async-start | bytes 3145728 | tf_op jit(solution)/shard_map/all_to_all | solution.py:47
  57.4 250.8 %reduce-scatter.3.cloned.1.call-start = ((), (), s32[]{:S(2)}) async-start(), calls=%async_computation.6 | async-start | bytes 7864320 | tf_op jit(solution)/shard_map/reduce_scatter | solution.py:50
  57.5 63.0 %collective-permute-start.4 = (bf16[32,24,1024]{2,1,0:T(8,128)(2,1)S(1)}, bf16[32,24,1024]{2,1,0:T(8,128)(2,1)}, u32[]{:S(2)}, u32[]{:S(2)}) collective-permute-start(bf16[32,24,1024]{2,1,0:T(8,128)(2,1)S(1)} %all-to-all-done.2), channel_id=1, source_target_pairs={{0,2},{1,3},{2,0},{3,1},{4,6},{5,7},{6,4},{7,5},{8,10},{9,11},{10,... | collective-permute-start | bytes 4718600 | tf_op jit(solution)/shard_map/ppermute | solution.py:18
  60.8 67.1 %collective-permute-start.5 = (bf16[32,24,1024]{2,1,0:T(8,128)(2,1)S(1)}, bf16[32,24,1024]{2,1,0:T(8,128)(2,1)}, u32[]{:S(2)}, u32[]{:S(2)}) collective-permute-start(bf16[32,24,1024]{2,1,0:T(8,128)(2,1)S(1)} %all-to-all-done.2), channel_id=1, source_target_pairs={{0,3},{1,0},{2,1},{3,2},{4,7},{5,4},{6,5},{7,6},{8,11},{9,8},{10,9... | collective-permute-start | bytes 4718600 | tf_op jit(solution)/shard_map/ppermute | solution.py:18
  80.2 73.1 %collective-permute-start = (bf16[32,24,1024]{2,1,0:T(8,128)(2,1)S(1)}, bf16[32,24,1024]{2,1,0:T(8,128)(2,1)}, u32[]{:S(2)}, u32[]{:S(2)}) collective-permute-start(bf16[32,24,1024]{2,1,0:T(8,128)(2,1)S(1)} %all-to-all-done), channel_id=1, source_target_pairs={{0,1},{1,2},{2,3},{3,0},{4,5},{5,6},{6,7},{7,4},{8,9},{9,10},{10,1... | collective-permute-start | bytes 4718600 | tf_op jit(solution)/shard_map/ppermute | solution.py:18
  81.8 106.1 %collective-permute-start.1 = (bf16[32,24,1024]{2,1,0:T(8,128)(2,1)S(1)}, bf16[32,24,1024]{2,1,0:T(8,128)(2,1)}, u32[]{:S(2)}, u32[]{:S(2)}) collective-permute-start(bf16[32,24,1024]{2,1,0:T(8,128)(2,1)S(1)} %all-to-all-done), channel_id=1, source_target_pairs={{0,2},{1,3},{2,0},{3,1},{4,6},{5,7},{6,4},{7,5},{8,10},{9,11},{10,... | collective-permute-start | bytes 4718600 | tf_op jit(solution)/shard_map/ppermute | solution.py:18
  85.8 109.6 %collective-permute-start.2 = (bf16[32,24,1024]{2,1,0:T(8,128)(2,1)S(1)}, bf16[32,24,1024]{2,1,0:T(8,128)(2,1)}, u32[]{:S(2)}, u32[]{:S(2)}) collective-permute-start(bf16[32,24,1024]{2,1,0:T(8,128)(2,1)S(1)} %all-to-all-done), channel_id=1, source_target_pairs={{0,3},{1,0},{2,1},{3,2},{4,7},{5,4},{6,5},{7,6},{8,11},{9,8},{10,9... | collective-permute-start | bytes 4718600 | tf_op jit(solution)/shard_map/ppermute | solution.py:18
  221.6 2.6 copy-start.2
  242.0 6.6 %slice-start = ((s8[6291456]{0:T(1024)(128)(4,1)}), s8[2097152]{0:T(1024)(128)(4,1)S(1)}, s32[]{:S(2)}) async-start(s8[6291456]{0:T(1024)(128)(4,1)} %bitcast.92), calls=%async_computation.8 | async-start | bytes 4194304
  242.0 132.5 %reduce-scatter.5.cloned.1.call-start = ((), (), s32[]{:S(2)}) async-start(), calls=%async_computation.7 | async-start | bytes 7864320 | tf_op jit(solution)/shard_map/reduce_scatter | solution.py:50
  242.3 6.3 %slice-start.1 = ((s8[6291456]{0:T(1024)(128)(4,1)}), s8[4194304]{0:T(1024)(128)(4,1)S(1)}, s32[]{:S(2)}) async-start(s8[6291456]{0:T(1024)(128)(4,1)} %bitcast.92), calls=%async_computation.9 | async-start | bytes 8388608
  246.0 2.6 copy-start.3
  266.3 115.8 %copy-start.5 = (s32[128]{0:T(128)S(1)}, s32[128]{0:T(128)}, u32[]{:S(2)}) copy-start(s32[128]{0:T(128)} %param.15) | copy-start | bytes 1540
  266.3 116.6 %copy-start.4 = (s32[128,8]{0,1:T(8,128)S(1)}, s32[128,8]{0,1:T(8,128)}, u32[]{:S(2)}) copy-start(s32[128,8]{0,1:T(8,128)} %param.14) | copy-start | bytes 12292
  308.3 66.2 %all-to-all-start.1 = ((bf16[32,24,1024]{2,1,0:T(8,128)(2,1)}), bf16[32,24,1024]{2,1,0:T(8,128)(2,1)S(1)}, u32[]{:S(2)}, u32[]{:S(2)}) async-start(bf16[32,24,1024]{2,1,0:T(8,128)(2,1)} %reduce-scatter.3.cloned.1.call-done), calls=%async_computation.2 | async-start | bytes 3145728 | tf_op jit(solution)/shard_map/all_to_all | solution.py:51
  374.5 30.3 %all-to-all-start.3 = ((bf16[32,24,1024]{2,1,0:T(8,128)(2,1)}), bf16[32,24,1024]{2,1,0:T(8,128)(2,1)S(1)}, u32[]{:S(2)}, u32[]{:S(2)}) async-start(bf16[32,24,1024]{2,1,0:T(8,128)(2,1)} %reduce-scatter.5.cloned.1.call-done), calls=%async_computation.5 | async-start | bytes 3145728 | tf_op jit(solution)/shard_map/all_to_all | solution.py:51
  405.5 9.1 %copy-start.1 = (bf16[128,1024]{1,0:T(8,128)(2,1)S(1)}, bf16[128,1024]{1,0:T(8,128)(2,1)}, u32[]{:S(2)}) copy-start(bf16[128,1024]{1,0:T(8,128)(2,1)} %param.9) | copy-start | bytes 786436
Sparse Core Ops, SparseCore 0:
  242.1 66.0 reduce-scatter.2
  310.7 63.7 reduce-scatter.4

commit v2 on v0

--- a/solution.py
+++ b/solution.py
@@ -29,11 +29,12 @@
     row_ids = jnp.arange(pairs, dtype=jnp.int32) // choose
     slot_rows = jnp.zeros((experts * capacity,), jnp.int32).at[target].set(row_ids)
     slot_rows = slot_rows.reshape(groups, local_experts, capacity)
+    arrived = lax.all_to_all(tokens[slot_rows[:, 0]], "expert", split_axis=0, concat_axis=0, tiled=True)
+    full0 = lax.all_gather(arrived, "hidden", axis=2, tiled=True)
+    whole_rows = lax.all_gather(tokens, "hidden", axis=1, tiled=True)
+    full1 = lax.all_to_all(whole_rows[slot_rows[:, 1]], "expert", split_axis=0, concat_axis=0, tiled=True)
     per_expert = []
-    for c in range(local_experts):
-        send = tokens[slot_rows[:, c]]
-        arrived = lax.all_to_all(send, "expert", split_axis=0, concat_axis=0, tiled=True)
-        full = lax.all_gather(arrived, "hidden", axis=2, tiled=True)
+    for c, full in enumerate((full0, full1)):
         part = expert_part(full, w_gate[c], w_up[c], w_down[c])
         summed = lax.psum_scatter(part, "hidden", scatter_dimension=2, tiled=True)
         per_expert.append(lax.all_to_all(summed, "expert", split_axis=0, concat_axis=0, tiled=True))

time: 359 us -> 334 us (0.930)
  waiting for transfers between devices: 211 us -> 100 us
  blocking collectives: 57.7 us -> 138 us
  local copies, waits for them, and re-layouts: 18.6 us -> 31.6 us
  starting transfers between devices: 15.5 us -> 7.73 us
    all_gather x2, waiting for transfers between devices: 83.6 us -> 0.04 us  [the longest x1 0.02 us: body(): whole_rows = lax.all_gather(tokens, 'hidden', axis=1, tiled=True)]
    all_to_all x2 -> x3, blocking collectives: 57.7 us -> 138 us  [the longest x1 76.7 us: body(): lax.all_to_all(whole_rows[slot_rows[:, 1]], 'expert', split_axis=0, conca...]
    reduce_scatter x2, waiting for transfers between devices: 107 us -> 78.3 us  [body(): summed = lax.psum_scatter(part, 'hidden', scatter_dimension=2, tiled=True)]
    gather x2, local copies, waits for them, and re-layouts: 5.62 us -> 16.1 us  [the longest x1 13.3 us: body(): whole_rows[slot_rows[:, 1]]]
    all_to_all x2 -> x1, starting transfers between devices: 15.2 us -> 7.61 us  [body(): lax.all_to_all(summed, 'expert', split_axis=0, concat_axis=0, tiled=True)]
    all_to_all x2 -> x1, waiting for transfers between devices: 20.9 us -> 20.9 us  [body(): lax.all_to_all(summed, 'expert', split_axis=0, concat_axis=0, tiled=True)]
  transfers between devices with their start and end apart: 6 -> 5, of which waited for: 5 -> 3; matrix products, arithmetic and copies ran while one was open for 12% -> 19% of each run, Pallas kernels for 0% -> 0%
where the time goes in v2:
time: 334 us
  blocking collectives  138 us (41%)
  waiting for transfers between devices  100 us (30%)
  matrix products  38.4 us (11%)
  local copies, waits for them, and re-layouts  31.6 us (9%)
  between operations  13.4 us (4%)
  starting transfers between devices  7.73 us (2%)
  other arithmetic  4.21 us (1%)
    reduce_scatter x2, waiting for transfers between devices, body(): summed = lax.psum_scatter(part, 'hidden', scatter_dimension=2, tiled=True)  78.3 us
    all_to_all x1, blocking collectives, body(): lax.all_to_all(whole_rows[slot_rows[:, 1]], 'expert', split_axis=0, conca...  76.7 us
    all_to_all x1, blocking collectives, body(): lax.all_to_all(tokens[slot_rows[:, 0]], 'expert', split_axis=0, concat_ax...  31.3 us
    all_to_all x1, blocking collectives, body(): lax.all_to_all(summed, 'expert', split_axis=0, concat_axis=0, tiled=True)  30.4 us
    dot_general x2, matrix products, expert_part(): jnp.einsum('scf,fd->scd', hidden_acts, w_down, preferred_element_type=jnp...  26 us
    all_to_all x1, waiting for transfers between devices, body(): lax.all_to_all(summed, 'expert', split_axis=0, concat_axis=0, tiled=True)  20.9 us
    gather x1, local copies, waits for them, and re-layouts, body(): whole_rows[slot_rows[:, 1]]  13.3 us
    dot_general x2, matrix products, expert_part(): jnp.einsum('scd,df->scf', arrived, w_gate, preferred_element_type=jnp.flo...  11.8 us
  transfers between devices with their start and end apart: 5, of which 3 were waited for; matrix products, arithmetic and copies ran while one was open for 19% of the time, Pallas kernels for 0%

profile of v2, /device:TPU:1, one launch (start us, length us, event | category | flops | bytes accessed | tf_op | source)
XLA Modules:
  0.0 333.8 jit_solution(3194085995364132469)
XLA Ops:
  6.5 0.0 all-gather.5.cloned.1.call-start
  6.5 0.7 all-gather.5.cloned.1.call-update
  7.3 0.0 all-gather.3.cloned.1.call-start
  7.3 0.8 copy.12
  8.1 0.1 eq.15
  8.2 0.6 fusion.31
  8.8 0.1 convert_element_type.54
  8.9 0.1 mul.44
  9.0 4.3 %scatter_custom_fusion = s32[1536]{0:T(1024)S(1)} fusion(s32[1024]{0:T(1024)S(1)} %bitcast.70, s32[1024]{0:T(1024)S(1)} %add_select_fusion, s32[]{:T(128)} %constant.12.clone.1), kind=kCustom, calls=%fused_computation.55 | custom fusion | bytes 6148 | tf_op jit(solution)/shard_map/scatter | solution.py:30
  13.4 0.1 reshape.130
  13.5 0.1 reshape.142
  13.6 0.0 copy-done
  13.6 2.8 gather_fusion.1
  16.4 31.3 %all_to_all.20 = bf16[32,24,1024]{2,1,0:T(8,128)(2,1)} all-to-all(bf16[32,24,1024]{2,1,0:T(8,128)(2,1)S(1)} %bitcast.66), channel_id=1, replica_groups=mesh['expert'=32,'hidden'=4] {'expert'}, dimensions={0} | all-to-all | bytes 3145728 | tf_op jit(solution)/shard_map/all_to_all | solution.py:32
  47.8 0.0 all-gather.3.cloned.1.call-update
  47.8 0.0 reduce-scatter.5.cloned.1.call-start
  47.8 0.1 reshape.150
  47.9 0.0 all-gather.5.cloned.1.call-done
  48.0 13.3 %gather_fusion.2 = bf16[768,4096]{1,0:T(8,128)(2,1)} fusion(bf16[128,4096]{1,0:T(8,128)(2,1)} %all-gather.5.cloned.1.call-done, s32[1024]{0:T(1024)S(1)} %pad_clamp_fusion), kind=kCustom, calls=%fused_computation.2 | custom fusion | bytes 12585984 | tf_op jit(solution)/shard_map/gather | solution.py:35
  61.3 76.7 %all_to_all.21 = bf16[32,24,4096]{2,1,0:T(8,128)(2,1)S(1)} all-to-all(bf16[32,24,4096]{2,1,0:T(8,128)(2,1)} %bitcast.63), channel_id=1, replica_groups=mesh['expert'=32,'hidden'=4] {'expert'}, dimensions={0} | all-to-all | bytes 12582912 | tf_op jit(solution)/shard_map/all_to_all | solution.py:35
  138.0 2.6 copy-done.1
  140.6 5.3 %fusion.5 = f32[32,24,384]{2,1,0:T(8,128)S(1)} fusion(bf16[32,24,4096]{2,1,0:T(8,128)(2,1)S(1)} %all_to_all.21, bf16[2,4096,384]{2,1,0:T(8,128)(2,1)} %param.8), kind=kOutput, calls=%fused_computation.16 | convolution fusion | flops 2415919104 | bytes 10616832 | tf_op jit(solution)/shard_map/scd,df->scf/dot_general | solution.py:7
  145.9 12.4 %convolution_convert_fusion = bf16[32,24,4096]{2,1,0:T(8,128)(2,1)} fusion(bf16[2,384,4096]{2,1,0:T(8,128)(2,1)} %param.10, bf16[32,24,4096]{2,1,0:T(8,128)(2,1)} %copy-done.1, bf16[2,4096,384]{2,1,0:T(8,128)(2,1)} %param.9, f32[32,24,384]{2,1,0:T(8,128)S(1)} %fusion.5), kind=kOutput, calls=%fused_computation.6 | convolution fusion | flops 4836753408 | bytes 20054016 | tf_op jit(solution)/shard_map/scf,fd->scd/dot_general | solution.py:10
  158.3 0.0 reduce-scatter.5.cloned.1.call-update
  158.3 0.0 reduce-scatter.3.cloned.1.call-start
  158.4 0.0 all-gather.3.cloned.1.call-done
  158.4 6.5 %fusion.10 = f32[32,24,384]{2,1,0:T(8,128)S(1)} fusion(bf16[32,24,4096]{2,1,0:T(8,128)(2,1)} %all-gather.3.cloned.1.call-done, bf16[2,4096,384]{2,1,0:T(8,128)(2,1)} %param.8), kind=kOutput, calls=%fused_computation.21 | convolution fusion | flops 2415919104 | bytes 10616832 | tf_op jit(solution)/shard_map/scd,df->scf/dot_general | solution.py:7
  164.9 13.6 %convolution_convert_fusion.1 = bf16[32,24,4096]{2,1,0:T(8,128)(2,1)} fusion(bf16[2,384,4096]{2,1,0:T(8,128)(2,1)} %param.10, bf16[32,24,4096]{2,1,0:T(8,128)(2,1)} %all-gather.3.cloned.1.call-done, bf16[2,4096,384]{2,1,0:T(8,128)(2,1)} %param.9, f32[32,24,384]{2,1,0:T(8,128)S(1)} %fusion.10), kind=kOutput, calls=%fused_computation.7 | convolution fusion | flops 4836753408 | bytes 20054016 | tf_op jit(solution)/shard_map/scf,fd->scd/dot_general | solution.py:10
  178.5 0.0 reduce-scatter.3.cloned.1.call-update
  178.5 0.0 copy-start.3
  178.5 0.0 copy-start.2
  178.5 42.7 %reduce-scatter.5.cloned.1.call-done = bf16[32,24,1024]{2,1,0:T(8,128)(2,1)} async-done(((bf16[32,24,4096]{2,1,0:T(8,128)(2,1)}), bf16[32,24,1024]{2,1,0:T(8,128)(2,1)}) %reduce-scatter.5.cloned.1.call-update) | async-done | bytes 1572880 | tf_op jit(solution)/shard_map/reduce_scatter | solution.py:39
  221.2 30.4 %all_to_all.22 = bf16[32,24,1024]{2,1,0:T(8,128)(2,1)S(1)} all-to-all(bf16[32,24,1024]{2,1,0:T(8,128)(2,1)} %reduce-scatter.5.cloned.1.call-done), channel_id=1, replica_groups=mesh['expert'=32,'hidden'=4] {'expert'}, dimensions={0} | all-to-all | bytes 3145728 | tf_op jit(solution)/shard_map/all_to_all | solution.py:40
  251.6 35.6 %reduce-scatter.3.cloned.1.call-done = bf16[32,24,1024]{2,1,0:T(8,128)(2,1)} async-done(((bf16[32,24,4096]{2,1,0:T(8,128)(2,1)}), bf16[32,24,1024]{2,1,0:T(8,128)(2,1)}) %reduce-scatter.3.cloned.1.call-update) | async-done | bytes 1572880 | tf_op jit(solution)/shard_map/reduce_scatter | solution.py:39
  287.2 7.6 %all-to-all-start.1 = ((bf16[32,24,1024]{2,1,0:T(8,128)(2,1)}), bf16[32,24,1024]{2,1,0:T(8,128)(2,1)S(1)}, u32[]{:S(2)}, u32[]{:S(2)}) async-start(bf16[32,24,1024]{2,1,0:T(8,128)(2,1)} %reduce-scatter.3.cloned.1.call-done), calls=%async_computation.2 | async-start | bytes 3145728 | tf_op jit(solution)/shard_map/all_to_all | solution.py:40
  294.9 0.0 copy-done.3
  294.9 0.6 gather_fusion.3
  295.6 0.1 reshape.166
  295.6 0.0 copy-done.2
  295.7 0.1 copy.11
  295.8 0.6 gather_fusion
  296.4 0.1 reduce_sum.27
  296.5 0.1 broadcast_divide_fusion
  296.6 20.9 %all-to-all-done.1 = bf16[32,24,1024]{2,1,0:T(8,128)(2,1)S(1)} async-done(((bf16[32,24,1024]{2,1,0:T(8,128)(2,1)}), bf16[32,24,1024]{2,1,0:T(8,128)(2,1)S(1)}, u32[]{:S(2)}, u32[]{:S(2)}) %all-to-all-start.1) | async-done | bytes 1572896 | tf_op jit(solution)/shard_map/all_to_all | solution.py:40
  317.5 0.3 pad_maximum_fusion
  317.8 0.4 copy.15
  318.2 5.3 %gather_fusion.4 = bf16[1024,1024]{1,0:T(8,128)(2,1)} fusion(bf16[1536,1024]{1,0:T(8,128)(2,1)S(1)} %bitcast.62, s32[1024]{0:T(1024)S(1)} %broadcast_clamp_fusion), kind=kCustom, calls=%fused_computation.4 | custom fusion | bytes 4198400 | tf_op jit(solution)/shard_map/gather | solution.py:46
  323.6 3.7 %fusion = bf16[128,1024]{1,0:T(8,128)(2,1)} fusion(bf16[1024,1024]{1,0:T(8,128)(2,1)} %gather_fusion.4, f32[128,8]{1,0:T(8,128)S(1)} %broadcast_divide_fusion), kind=kLoop, calls=%fused_computation.9 | loop fusion | flops 3014656 | bytes 2363392 | tf_op jit(solution)/shard_map/reduce_sum | solution.py:47
  (16 shorter events, 0.1 us)
Async XLA Ops:
  6.5 7.1 %copy-start = (bf16[128,1024]{1,0:T(8,128)(2,1)S(1)}, bf16[128,1024]{1,0:T(8,128)(2,1)}, u32[]{:S(2)}) copy-start(bf16[128,1024]{1,0:T(8,128)(2,1)} %param.7) | copy-start | bytes 786436
  6.5 41.4 %all-gather.5.cloned.1.call-start = ((), (), s32[]{:S(2)}) async-start(), calls=%async_computation.8 | async-start | bytes 1310720 | tf_op jit(solution)/shard_map/all_gather | solution.py:34
  7.3 151.2 %all-gather.3.cloned.1.call-start = ((), (), s32[]{:S(2)}) async-start(), calls=%async_computation.6 | async-start | bytes 7864320 | tf_op jit(solution)/shard_map/all_gather | solution.py:33
  47.8 173.4 %reduce-scatter.5.cloned.1.call-start = ((), (), s32[]{:S(2)}) async-start(), calls=%async_computation.9 | async-start | bytes 7864320 | tf_op jit(solution)/shard_map/reduce_scatter | solution.py:39
  138.0 2.6 copy-start.1
  158.3 128.9 %reduce-scatter.3.cloned.1.call-start = ((), (), s32[]{:S(2)}) async-start(), calls=%async_computation.7 | async-start | bytes 7864320 | tf_op jit(solution)/shard_map/reduce_scatter | solution.py:39
  178.5 116.4 %copy-start.3 = (s32[128]{0:T(128)S(1)}, s32[128]{0:T(128)}, u32[]{:S(2)}) copy-start(s32[128]{0:T(128)} %param.13) | copy-start | bytes 1540
  178.5 117.2 %copy-start.2 = (s32[128,8]{0,1:T(8,128)S(1)}, s32[128,8]{0,1:T(8,128)}, u32[]{:S(2)}) copy-start(s32[128,8]{0,1:T(8,128)} %param.12) | copy-start | bytes 12292
  287.2 30.3 %all-to-all-start.1 = ((bf16[32,24,1024]{2,1,0:T(8,128)(2,1)}), bf16[32,24,1024]{2,1,0:T(8,128)(2,1)S(1)}, u32[]{:S(2)}, u32[]{:S(2)}) async-start(bf16[32,24,1024]{2,1,0:T(8,128)(2,1)} %reduce-scatter.3.cloned.1.call-done), calls=%async_computation.2 | async-start | bytes 3145728 | tf_op jit(solution)/shard_map/all_to_all | solution.py:40
Sparse Core Ops, SparseCore 0:
  9.0 25.7 all-gather.4
  47.9 63.9 all-gather.2
  158.5 62.6 reduce-scatter.4
  223.4 63.7 reduce-scatter.2

commit v3 on v2

--- a/solution.py
+++ b/solution.py
@@ -32,12 +32,16 @@
     arrived = lax.all_to_all(tokens[slot_rows[:, 0]], "expert", split_axis=0, concat_axis=0, tiled=True)
     full0 = lax.all_gather(arrived, "hidden", axis=2, tiled=True)
     whole_rows = lax.all_gather(tokens, "hidden", axis=1, tiled=True)
-    full1 = lax.all_to_all(whole_rows[slot_rows[:, 1]], "expert", split_axis=0, concat_axis=0, tiled=True)
-    per_expert = []
-    for c, full in enumerate((full0, full1)):
-        part = expert_part(full, w_gate[c], w_up[c], w_down[c])
-        summed = lax.psum_scatter(part, "hidden", scatter_dimension=2, tiled=True)
-        per_expert.append(lax.all_to_all(summed, "expert", split_axis=0, concat_axis=0, tiled=True))
+    lead = capacity // 2
+    head = lax.all_to_all(whole_rows[slot_rows[:, 1, :lead]], "expert", split_axis=0, concat_axis=0, tiled=True)
+    full0, head = lax.optimization_barrier((full0, head))
+    part0 = expert_part(full0, w_gate[0], w_up[0], w_down[0])
+    summed0 = lax.psum_scatter(part0, "hidden", scatter_dimension=2, tiled=True)
+    tail_rows, part0 = lax.optimization_barrier((slot_rows[:, 1, lead:], part0))
+    tail = lax.all_to_all(whole_rows[tail_rows], "expert", split_axis=0, concat_axis=0, tiled=True)
+    part1 = expert_part(jnp.concatenate([head, tail], 1), w_gate[1], w_up[1], w_down[1])
+    summed1 = lax.psum_scatter(part1, "hidden", scatter_dimension=2, tiled=True)
+    per_expert = [lax.all_to_all(s, "expert", split_axis=0, concat_axis=0, tiled=True) for s in (summed0, summed1)]
     returned = jnp.stack(per_expert, 1)
     returned = returned.reshape(experts * capacity, returned.shape[3])
     source = target.reshape(local_rows, choose)[ancestors]

time: 334 us -> 329 us (0.985)
  waiting for transfers between devices: 100 us -> 56.7 us
  blocking collectives: 138 us -> 169 us
  local copies, waits for them, and re-layouts: 31.6 us -> 40 us
    reduce_scatter x2, waiting for transfers between devices: 78.3 us -> 35 us  [the longest x1 35 us: body(): summed1 = lax.psum_scatter(part1, 'hidden', scatter_dimension=2, tiled=True)]
    all_to_all x2 -> x3, blocking collectives: 107 us -> 138 us  [the longest x1 55.8 us: body(): lax.all_to_all(whole_rows[tail_rows], 'expert', split_axis=0, concat_axis...]
    gather x1 -> x4, local copies, waits for them, and re-layouts: 13.3 us -> 21.2 us  [the longest x2 11.6 us: body(): whole_rows[slot_rows[:, 1, :lead]]]
  transfers between devices with their start and end apart: 5 -> 5, of which waited for: 3 -> 2; matrix products, arithmetic and copies ran while one was open for 19% -> 15% of each run, Pallas kernels for 0% -> 0%
where the time goes in v3:
time: 329 us
  blocking collectives  169 us (51%)
  waiting for transfers between devices  56.7 us (17%)
  local copies, waits for them, and re-layouts  40 us (12%)
  matrix products  37.7 us (11%)
  between operations  13.4 us (4%)
  starting transfers between devices  7.92 us (2%)
  other arithmetic  4.23 us (1%)
    all_to_all x1, blocking collectives, body(): lax.all_to_all(whole_rows[tail_rows], 'expert', split_axis=0, concat_axis...  55.8 us
    all_to_all x1, blocking collectives, body(): lax.all_to_all(whole_rows[slot_rows[:, 1, :lead]], 'expert', split_axis=0...  54.9 us
    reduce_scatter x1, waiting for transfers between devices, body(): summed1 = lax.psum_scatter(part1, 'hidden', scatter_dimension=2, tiled=True)  35 us
    all_to_all x1, blocking collectives, body(): lax.all_to_all(tokens[slot_rows[:, 0]], 'expert', split_axis=0, concat_ax...  31.3 us
    all_to_all x1, blocking collectives, body(): lax.all_to_all(s, 'expert', split_axis=0, concat_axis=0, tiled=True)  26.7 us
    dot_general x2, matrix products, expert_part(): jnp.einsum('scf,fd->scd', hidden_acts, w_down, preferred_element_type=jnp...  25.2 us
    all_to_all x1, waiting for transfers between devices, body(): lax.all_to_all(s, 'expert', split_axis=0, concat_axis=0, tiled=True)  20.9 us
    dot_general x2, matrix products, expert_part(): jnp.einsum('scd,df->scf', arrived, w_gate, preferred_element_type=jnp.flo...  11.9 us
  transfers between devices with their start and end apart: 5, of which 2 were waited for; matrix products, arithmetic and copies ran while one was open for 15% of the time, Pallas kernels for 0%

profile of v3, /device:TPU:1, one launch (start us, length us, event | category | flops | bytes accessed | tf_op | source)
XLA Modules:
  0.0 328.7 jit_solution(16957346639973395464)
XLA Ops:
  6.5 0.7 all-gather.5.cloned.1.call-update
  7.3 0.0 all-gather.3.cloned.1.call-start
  7.3 0.8 copy.11
  8.1 0.1 eq.15
  8.2 0.6 fusion.31
  8.8 0.1 convert_element_type.54
  8.9 0.1 mul.44
  9.0 4.3 %scatter_custom_fusion = s32[1536]{0:T(1024)S(1)} fusion(s32[1024]{0:T(1024)S(1)} %bitcast.67, s32[1024]{0:T(1024)S(1)} %add_select_fusion, s32[]{:T(128)} %constant.12.clone.1), kind=kCustom, calls=%fused_computation.59 | custom fusion | bytes 6148 | tf_op jit(solution)/shard_map/scatter | solution.py:30
  13.4 0.1 reshape.130
  13.5 0.1 reshape.142
  13.6 2.8 gather_fusion.1
  16.4 31.3 %all_to_all.25 = bf16[32,24,1024]{2,1,0:T(8,128)(2,1)} all-to-all(bf16[32,24,1024]{2,1,0:T(8,128)(2,1)S(1)} %bitcast.62), channel_id=1, replica_groups=mesh['expert'=32,'hidden'=4] {'expert'}, dimensions={0} | all-to-all | bytes 3145728 | tf_op jit(solution)/shard_map/all_to_all | solution.py:32
  47.7 0.0 all-gather.3.cloned.1.call-update
  47.8 0.0 reduce-scatter.3.cloned.1.call-start
  47.8 0.1 fusion.51
  47.9 0.1 reshape.150
  48.0 0.0 all-gather.5.cloned.1.call-done
  48.1 8.9 %gather_fusion.2 = bf16[384,4096]{1,0:T(8,128)(2,1)S(1)} fusion(bf16[128,4096]{1,0:T(8,128)(2,1)} %all-gather.5.cloned.1.call-done, s32[1024]{0:T(1024)S(1)} %pad_clamp_fusion.1), kind=kCustom, calls=%fused_computation.2 | custom fusion | bytes 6292992 | tf_op jit(solution)/shard_map/gather | solution.py:36
  57.0 2.7 reshape.149
  59.7 54.9 %all_to_all.26 = bf16[32,12,4096]{2,1,0:T(8,128)(2,1)} all-to-all(bf16[32,12,4096]{2,1,0:T(8,128)(2,1)} %reshape.149), channel_id=1, replica_groups=mesh['expert'=32,'hidden'=4] {'expert'}, dimensions={0} | all-to-all | bytes 6291456 | tf_op jit(solution)/shard_map/all_to_all | solution.py:36
  114.6 6.5 %fusion.10 = f32[32,24,384]{2,1,0:T(8,128)S(1)} fusion(bf16[32,24,4096]{2,1,0:T(8,128)(2,1)} %all-gather.3.cloned.1.call-done, bf16[2,4096,384]{2,1,0:T(8,128)(2,1)} %param.8), kind=kOutput, calls=%fused_computation.23 | convolution fusion | flops 2415919104 | bytes 10616832 | tf_op jit(solution)/shard_map/scd,df->scf/dot_general | solution.py:7
  121.1 12.4 %convolution_convert_fusion.1 = bf16[32,24,4096]{2,1,0:T(8,128)(2,1)} fusion(bf16[2,384,4096]{2,1,0:T(8,128)(2,1)} %param.10, bf16[32,24,4096]{2,1,0:T(8,128)(2,1)} %all-gather.3.cloned.1.call-done, bf16[2,4096,384]{2,1,0:T(8,128)(2,1)} %param.9, f32[32,24,384]{2,1,0:T(8,128)S(1)} %fusion.10), kind=kOutput, calls=%fused_computation.8 | convolution fusion | flops 4836753408 | bytes 20054016 | tf_op jit(solution)/shard_map/scf,fd->scd/dot_general | solution.py:10
  133.5 0.0 reduce-scatter.3.cloned.1.call-update
  133.6 0.2 reduce-scatter.5.cloned.1.call-start
  133.8 0.1 reshape.158
  133.9 0.8 copy-done
  134.8 4.0 %gather_fusion.3 = bf16[384,4096]{1,0:T(8,128)(2,1)} fusion(bf16[128,4096]{1,0:T(8,128)(2,1)S(1)} %copy-done, s32[1024]{0:T(1024)S(1)} %pad_clamp_fusion), kind=kCustom, calls=%fused_computation.3 | custom fusion | bytes 6292992 | tf_op jit(solution)/shard_map/gather | solution.py:41
  138.8 5.6 %reshape.157 = bf16[32,12,4096]{2,1,0:T(8,128)(2,1)} reshape(bf16[384,4096]{1,0:T(8,128)(2,1)} %gather_fusion.3) | data formatting | bytes 6291456 | tf_op jit(solution)/shard_map/gather | solution.py:41
  144.4 55.8 %all_to_all.27 = bf16[32,12,4096]{2,1,0:T(8,128)(2,1)S(1)} all-to-all(bf16[32,12,4096]{2,1,0:T(8,128)(2,1)} %reshape.157), channel_id=1, replica_groups=mesh['expert'=32,'hidden'=4] {'expert'}, dimensions={0} | all-to-all | bytes 6291456 | tf_op jit(solution)/shard_map/all_to_all | solution.py:41
  200.2 1.9 copy-done.3
  202.2 5.4 %fusion.5 = f32[32,24,384]{2,1,0:T(8,128)S(1)} fusion(bf16[2,4096,384]{2,1,0:T(8,128)(2,1)} %param.8, bf16[32,12,4096]{2,1,0:T(8,128)(2,1)S(1)} %all_to_all.27, bf16[32,12,4096]{2,1,0:T(8,128)(2,1)S(1)} %copy-done.2), kind=kOutput, calls=%fused_computation.18 | convolution fusion | flops 2428502016 | bytes 10616832 | tf_op jit(solution)/shard_map/scd,df->scf/dot_general | solution.py:7
  207.6 12.7 %convolution_convert_fusion = bf16[32,24,4096]{2,1,0:T(8,128)(2,1)} fusion(bf16[2,384,4096]{2,1,0:T(8,128)(2,1)} %param.10, bf16[2,4096,384]{2,1,0:T(8,128)(2,1)} %param.9, bf16[32,12,4096]{2,1,0:T(8,128)(2,1)} %copy-done.3, bf16[32,12,4096]{2,1,0:T(8,128)(2,1)} %all_to_all.26, f32[32,24,384]{2,1,0:T(8,128)S(1)} %fusion.5), kind=kOutput, calls=%fused_computation.7 | convolution fusion | flops 4849336320 | bytes 22151168 | tf_op jit(solution)/shard_map/scf,fd->scd/dot_general | solution.py:10
  220.3 0.0 reduce-scatter.5.cloned.1.call-update
  220.4 0.0 reduce-scatter.3.cloned.1.call-done
  220.4 26.7 %all_to_all.28 = bf16[32,24,1024]{2,1,0:T(8,128)(2,1)S(1)} all-to-all(bf16[32,24,1024]{2,1,0:T(8,128)(2,1)} %reduce-scatter.3.cloned.1.call-done), channel_id=1, replica_groups=mesh['expert'=32,'hidden'=4] {'expert'}, dimensions={0} | all-to-all | bytes 3145728 | tf_op jit(solution)/shard_map/all_to_all | solution.py:44
  247.1 35.0 %reduce-scatter.5.cloned.1.call-done = bf16[32,24,1024]{2,1,0:T(8,128)(2,1)} async-done(((bf16[32,24,4096]{2,1,0:T(8,128)(2,1)}), bf16[32,24,1024]{2,1,0:T(8,128)(2,1)}) %reduce-scatter.5.cloned.1.call-update) | async-done | bytes 1572880 | tf_op jit(solution)/shard_map/reduce_scatter | solution.py:43
  282.1 7.6 %all-to-all-start.4 = ((bf16[32,24,1024]{2,1,0:T(8,128)(2,1)}), bf16[32,24,1024]{2,1,0:T(8,128)(2,1)S(1)}, u32[]{:S(2)}, u32[]{:S(2)}) async-start(bf16[32,24,1024]{2,1,0:T(8,128)(2,1)} %reduce-scatter.5.cloned.1.call-done), calls=%async_computation.6 | async-start | bytes 3145728 | tf_op jit(solution)/shard_map/all_to_all | solution.py:44
  289.8 0.1 copy.10
  289.9 0.6 gather_fusion
  290.6 0.6 gather_fusion.4
  291.2 0.1 reshape.174
  291.3 0.1 reduce_sum.27
  291.4 0.1 broadcast_divide_fusion
  291.5 20.9 %all-to-all-done.4 = bf16[32,24,1024]{2,1,0:T(8,128)(2,1)S(1)} async-done(((bf16[32,24,1024]{2,1,0:T(8,128)(2,1)}), bf16[32,24,1024]{2,1,0:T(8,128)(2,1)S(1)}, u32[]{:S(2)}, u32[]{:S(2)}) %all-to-all-start.4) | async-done | bytes 1572896 | tf_op jit(solution)/shard_map/all_to_all | solution.py:44
  312.4 0.3 pad_maximum_fusion.1
  312.7 0.4 copy.13
  313.1 5.3 %gather_fusion.5 = bf16[1024,1024]{1,0:T(8,128)(2,1)} fusion(bf16[1536,1024]{1,0:T(8,128)(2,1)S(1)} %bitcast.59, s32[1024]{0:T(1024)S(1)} %broadcast_clamp_fusion), kind=kCustom, calls=%fused_computation.5 | custom fusion | bytes 4198400 | tf_op jit(solution)/shard_map/gather | solution.py:50
  318.5 3.7 %fusion = bf16[128,1024]{1,0:T(8,128)(2,1)} fusion(bf16[1024,1024]{1,0:T(8,128)(2,1)} %gather_fusion.5, f32[128,8]{1,0:T(8,128)S(1)} %broadcast_divide_fusion), kind=kLoop, calls=%fused_computation.11 | loop fusion | flops 3014656 | bytes 2363392 | tf_op jit(solution)/shard_map/reduce_sum | solution.py:51
  (28 shorter events, 0.1 us)
Async XLA Ops:
  6.5 7.1 %copy-start.1 = (bf16[128,1024]{1,0:T(8,128)(2,1)S(1)}, bf16[128,1024]{1,0:T(8,128)(2,1)}, u32[]{:S(2)}) copy-start(bf16[128,1024]{1,0:T(8,128)(2,1)} %param.7) | copy-start | bytes 786436
  6.5 41.5 %all-gather.5.cloned.1.call-start = ((), (), s32[]{:S(2)}) async-start(), calls=%async_computation.8 | async-start | bytes 1310720 | tf_op jit(solution)/shard_map/all_gather | solution.py:34
  7.3 107.4 %all-gather.3.cloned.1.call-start = ((), (), s32[]{:S(2)}) async-start(), calls=%async_computation.7 | async-start | bytes 7864320 | tf_op jit(solution)/shard_map/all_gather | solution.py:33
  47.8 172.6 %reduce-scatter.3.cloned.1.call-start = ((), (), s32[]{:S(2)}) async-start(), calls=%async_computation.9 | async-start | bytes 7864320 | tf_op jit(solution)/shard_map/reduce_scatter | solution.py:39
  133.5 1.2 copy-start
  133.6 148.6 %reduce-scatter.5.cloned.1.call-start = ((), (), s32[]{:S(2)}) async-start(), calls=%async_computation.10 | async-start | bytes 7864320 | tf_op jit(solution)/shard_map/reduce_scatter | solution.py:43
  144.4 57.7 %copy-start.2 = (bf16[32,12,4096]{2,1,0:T(8,128)(2,1)S(1)}, bf16[32,12,4096]{2,1,0:T(8,128)(2,1)}, u32[]{:S(2)}) copy-start(bf16[32,12,4096]{2,1,0:T(8,128)(2,1)} %all_to_all.26) | copy-start | bytes 9437188
  200.2 1.9 copy-start.3
  220.3 69.4 %copy-start.4 = (s32[128,8]{0,1:T(8,128)S(1)}, s32[128,8]{0,1:T(8,128)}, u32[]{:S(2)}) copy-start(s32[128,8]{0,1:T(8,128)} %param.12) | copy-start | bytes 12292
  220.4 69.5 %copy-start.5 = (s32[128]{0:T(128)S(1)}, s32[128]{0:T(128)}, u32[]{:S(2)}) copy-start(s32[128]{0:T(128)} %param.13) | copy-start | bytes 1540
  282.1 30.3 %all-to-all-start.4 = ((bf16[32,24,1024]{2,1,0:T(8,128)(2,1)}), bf16[32,24,1024]{2,1,0:T(8,128)(2,1)S(1)}, u32[]{:S(2)}, u32[]{:S(2)}) async-start(bf16[32,24,1024]{2,1,0:T(8,128)(2,1)} %reduce-scatter.5.cloned.1.call-done), calls=%async_computation.6 | async-start | bytes 3145728 | tf_op jit(solution)/shard_map/all_to_all | solution.py:44
Sparse Core Ops, SparseCore 0:
  9.0 25.7 all-gather.4
  47.9 63.9 all-gather.2
  133.7 62.6 reduce-scatter.2
  220.5 61.6 reduce-scatter.4

commit v4 on v3

--- a/solution.py
+++ b/solution.py
@@ -32,7 +32,7 @@
     arrived = lax.all_to_all(tokens[slot_rows[:, 0]], "expert", split_axis=0, concat_axis=0, tiled=True)
     full0 = lax.all_gather(arrived, "hidden", axis=2, tiled=True)
     whole_rows = lax.all_gather(tokens, "hidden", axis=1, tiled=True)
-    lead = capacity // 2
+    lead = 2 * capacity // 3
     head = lax.all_to_all(whole_rows[slot_rows[:, 1, :lead]], "expert", split_axis=0, concat_axis=0, tiled=True)
     full0, head = lax.optimization_barrier((full0, head))
     part0 = expert_part(full0, w_gate[0], w_up[0], w_down[0])

time: 329 us -> 309 us (0.939)
  blocking collectives: 169 us -> 117 us
  waiting for transfers between devices: 56.7 us -> 85 us
  starting transfers between devices: 7.92 us -> 14.4 us
  local copies, waits for them, and re-layouts: 40 us -> 36.1 us
    all_to_all x1 -> x0, blocking collectives: 55.8 us -> none  [body(): lax.all_to_all(whole_rows[tail_rows], 'expert', split_axis=0, concat_axis...]
    all_to_all x0 -> x1, waiting for transfers between devices: none -> 23.7 us  [body(): lax.all_to_all(whole_rows[tail_rows], 'expert', split_axis=0, concat_axis...]
    all_to_all x0 -> x1, starting transfers between devices: none -> 6.69 us  [body(): lax.all_to_all(whole_rows[tail_rows], 'expert', split_axis=0, concat_axis...]
    gather x2 -> x1, local copies, waits for them, and re-layouts: 9.64 us -> 3.2 us  [body(): whole_rows[tail_rows]]
    reduce_scatter x1, waiting for transfers between devices: 0.02 us -> 3.97 us  [body(): summed0 = lax.psum_scatter(part0, 'hidden', scatter_dimension=2, tiled=True)]
    all_to_all x1, blocking collectives: 26.7 us -> 30.4 us  [body(): lax.all_to_all(s, 'expert', split_axis=0, concat_axis=0, tiled=True)]
    gather x2 -> x1, local copies, waits for them, and re-layouts: 11.6 us -> 9.93 us  [body(): whole_rows[slot_rows[:, 1, :lead]]]
  transfers between devices with their start and end apart: 5 -> 6, of which waited for: 2 -> 4; matrix products, arithmetic and copies ran while one was open for 15% -> 16% of each run, Pallas kernels for 0% -> 0%
where the time goes in v4:
time: 309 us; the launch traced here: 308 us
  blocking collectives  117 us (38%)
  waiting for transfers between devices  85 us (28%)
  matrix products  38.5 us (12%)
  local copies, waits for them, and re-layouts  36.1 us (12%)
  starting transfers between devices  14.4 us (5%)
  between operations  13.4 us (4%)
  other arithmetic  4.22 us (1%)
    all_to_all x1, blocking collectives, body(): lax.all_to_all(whole_rows[slot_rows[:, 1, :lead]], 'expert', split_axis=0...  55 us
    reduce_scatter x1, waiting for transfers between devices, body(): summed1 = lax.psum_scatter(part1, 'hidden', scatter_dimension=2, tiled=True)  35.7 us
    all_to_all x1, blocking collectives, body(): lax.all_to_all(tokens[slot_rows[:, 0]], 'expert', split_axis=0, concat_ax...  31.3 us
    all_to_all x1, blocking collectives, body(): lax.all_to_all(s, 'expert', split_axis=0, concat_axis=0, tiled=True)  30.4 us
    dot_general x2, matrix products, expert_part(): jnp.einsum('scf,fd->scd', hidden_acts, w_down, preferred_element_type=jnp...  24.9 us
    all_to_all x1, waiting for transfers between devices, body(): lax.all_to_all(whole_rows[tail_rows], 'expert', split_axis=0, concat_axis...  23.7 us
    all_to_all x1, waiting for transfers between devices, body(): lax.all_to_all(s, 'expert', split_axis=0, concat_axis=0, tiled=True)  20.9 us
    dot_general x2, matrix products, expert_part(): jnp.einsum('scd,df->scf', arrived, w_gate, preferred_element_type=jnp.flo...  13 us
  transfers between devices with their start and end apart: 6, of which 4 were waited for; matrix products, arithmetic and copies ran while one was open for 16% of the time, Pallas kernels for 0%

profile of v4, /device:TPU:1, one launch (start us, length us, event | category | flops | bytes accessed | tf_op | source)
XLA Modules:
  0.0 308.3 jit_solution(5670343743146838679)
XLA Ops:
  6.5 0.7 all-gather.5.cloned.1.call-update
  7.3 0.0 all-gather.3.cloned.1.call-start
  7.3 0.8 copy.11
  8.1 0.1 eq.15
  8.2 0.6 fusion.31
  8.8 0.1 convert_element_type.54
  8.9 0.1 mul.44
  9.0 4.3 %scatter_custom_fusion = s32[1536]{0:T(1024)S(1)} fusion(s32[1024]{0:T(1024)S(1)} %bitcast.73, s32[1024]{0:T(1024)S(1)} %add_select_fusion, s32[]{:T(128)} %constant.12.clone.1), kind=kCustom, calls=%fused_computation.60 | custom fusion | bytes 6148 | tf_op jit(solution)/shard_map/scatter | solution.py:30
  13.4 0.1 reshape.130
  13.5 0.1 reshape.142
  13.6 2.8 gather_fusion.1
  16.4 31.3 %all_to_all.25 = bf16[32,24,1024]{2,1,0:T(8,128)(2,1)} all-to-all(bf16[32,24,1024]{2,1,0:T(8,128)(2,1)S(1)} %bitcast.68), channel_id=1, replica_groups=mesh['expert'=32,'hidden'=4] {'expert'}, dimensions={0} | all-to-all | bytes 3145728 | tf_op jit(solution)/shard_map/all_to_all | solution.py:32
  47.7 0.0 all-gather.3.cloned.1.call-update
  47.8 0.0 reduce-scatter.3.cloned.1.call-start
  47.9 0.1 reshape.150
  48.0 0.0 all-gather.5.cloned.1.call-done
  48.0 9.9 %gather_fusion.2 = bf16[512,4096]{1,0:T(8,128)(2,1)} fusion(bf16[128,4096]{1,0:T(8,128)(2,1)} %all-gather.5.cloned.1.call-done, s32[1024]{0:T(1024)S(1)} %pad_clamp_fusion.1), kind=kCustom, calls=%fused_computation.2 | custom fusion | bytes 8390656 | tf_op jit(solution)/shard_map/gather | solution.py:36
  57.9 55.0 %all_to_all.26 = bf16[32,16,4096]{2,1,0:T(8,128)(2,1)} all-to-all(bf16[32,16,4096]{2,1,0:T(8,128)(2,1)} %bitcast.64), channel_id=1, replica_groups=mesh['expert'=32,'hidden'=4] {'expert'}, dimensions={0} | all-to-all | bytes 8388608 | tf_op jit(solution)/shard_map/all_to_all | solution.py:36
  112.9 6.5 %fusion.10 = f32[32,24,384]{2,1,0:T(8,128)S(1)} fusion(bf16[32,24,4096]{2,1,0:T(8,128)(2,1)} %all-gather.3.cloned.1.call-done, bf16[2,4096,384]{2,1,0:T(8,128)(2,1)} %param.8), kind=kOutput, calls=%fused_computation.22 | convolution fusion | flops 2415919104 | bytes 10616832 | tf_op jit(solution)/shard_map/scd,df->scf/dot_general | solution.py:7
  119.3 12.4 %convolution_convert_fusion.1 = bf16[32,24,4096]{2,1,0:T(8,128)(2,1)} fusion(bf16[2,384,4096]{2,1,0:T(8,128)(2,1)} %param.10, bf16[32,24,4096]{2,1,0:T(8,128)(2,1)} %all-gather.3.cloned.1.call-done, bf16[2,4096,384]{2,1,0:T(8,128)(2,1)} %param.9, f32[32,24,384]{2,1,0:T(8,128)S(1)} %fusion.10), kind=kOutput, calls=%fused_computation.8 | convolution fusion | flops 4836753408 | bytes 20054016 | tf_op jit(solution)/shard_map/scf,fd->scd/dot_general | solution.py:10
  131.8 0.0 reduce-scatter.3.cloned.1.call-update
  131.8 0.1 slice.50
  131.9 0.5 copy-done.3
  132.4 0.1 reshape.158
  132.5 0.5 copy-done
  133.0 3.2 %gather_fusion.3 = bf16[256,4096]{1,0:T(8,128)(2,1)} fusion(bf16[128,4096]{1,0:T(8,128)(2,1)S(1)} %copy-done, s32[1024]{0:T(1024)S(1)} %get-tuple-element.13), kind=kCustom, calls=%fused_computation.3 | custom fusion | bytes 4195328 | tf_op jit(solution)/shard_map/gather | solution.py:41
  136.2 6.7 %all-to-all-start.3 = ((bf16[32,8,4096]{2,1,0:T(8,128)(2,1)}), bf16[32,8,4096]{2,1,0:T(8,128)(2,1)S(1)}, u32[]{:S(2)}, u32[]{:S(2)}) async-start(bf16[32,8,4096]{2,1,0:T(8,128)(2,1)} %bitcast.65), calls=%async_computation.4 | async-start | bytes 4194304 | tf_op jit(solution)/shard_map/all_to_all | solution.py:41
  142.9 0.0 reduce-scatter.5.cloned.1.call-start
  143.0 4.6 %constant_dynamic-update-slice_fusion.1 = bf16[32,24,4096]{2,1,0:T(8,128)(2,1)} fusion(bf16[32,16,4096]{2,1,0:T(8,128)(2,1)} %all_to_all.26), kind=kLoop, calls=%fused_computation.59 | loop fusion | bytes 8388608
  147.6 23.7 %all-to-all-done.3 = bf16[32,8,4096]{2,1,0:T(8,128)(2,1)S(1)} async-done(((bf16[32,8,4096]{2,1,0:T(8,128)(2,1)}), bf16[32,8,4096]{2,1,0:T(8,128)(2,1)S(1)}, u32[]{:S(2)}, u32[]{:S(2)}) %all-to-all-start.3) | async-done | bytes 2097184 | tf_op jit(solution)/shard_map/all_to_all | solution.py:41
  171.2 1.5 constant_dynamic-update-slice_fusion
  172.7 6.6 %fusion.5 = f32[32,24,384]{2,1,0:T(8,128)S(1)} fusion(bf16[32,24,4096]{2,1,0:T(8,128)(2,1)} %constant_dynamic-update-slice_fusion, bf16[2,4096,384]{2,1,0:T(8,128)(2,1)} %param.8), kind=kOutput, calls=%fused_computation.17 | convolution fusion | flops 2415919104 | bytes 10616832 | tf_op jit(solution)/shard_map/scd,df->scf/dot_general | solution.py:7
  179.3 12.4 %convolution_convert_fusion = bf16[32,24,4096]{2,1,0:T(8,128)(2,1)} fusion(bf16[2,384,4096]{2,1,0:T(8,128)(2,1)} %param.10, bf16[32,24,4096]{2,1,0:T(8,128)(2,1)} %constant_dynamic-update-slice_fusion, bf16[2,4096,384]{2,1,0:T(8,128)(2,1)} %param.9, f32[32,24,384]{2,1,0:T(8,128)S(1)} %fusion.5), kind=kOutput, calls=%fused_computation.7 | convolution fusion | flops 4836753408 | bytes 20054016 | tf_op jit(solution)/shard_map/scf,fd->scd/dot_general | solution.py:10
  191.8 4.0 %reduce-scatter.3.cloned.1.call-done = bf16[32,24,1024]{2,1,0:T(8,128)(2,1)} async-done(((bf16[32,24,4096]{2,1,0:T(8,128)(2,1)}), bf16[32,24,1024]{2,1,0:T(8,128)(2,1)}) %reduce-scatter.3.cloned.1.call-update) | async-done | bytes 1572880 | tf_op jit(solution)/shard_map/reduce_scatter | solution.py:39
  195.7 30.4 %all_to_all.27 = bf16[32,24,1024]{2,1,0:T(8,128)(2,1)S(1)} all-to-all(bf16[32,24,1024]{2,1,0:T(8,128)(2,1)} %reduce-scatter.3.cloned.1.call-done), channel_id=1, replica_groups=mesh['expert'=32,'hidden'=4] {'expert'}, dimensions={0} | all-to-all | bytes 3145728 | tf_op jit(solution)/shard_map/all_to_all | solution.py:44
  226.2 35.7 %reduce-scatter.5.cloned.1.call-done = bf16[32,24,1024]{2,1,0:T(8,128)(2,1)} async-done(((bf16[32,24,4096]{2,1,0:T(8,128)(2,1)}), bf16[32,24,1024]{2,1,0:T(8,128)(2,1)}) %reduce-scatter.5.cloned.1.call-update) | async-done | bytes 1572880 | tf_op jit(solution)/shard_map/reduce_scatter | solution.py:43
  261.8 7.6 %all-to-all-start.4 = ((bf16[32,24,1024]{2,1,0:T(8,128)(2,1)}), bf16[32,24,1024]{2,1,0:T(8,128)(2,1)S(1)}, u32[]{:S(2)}, u32[]{:S(2)}) async-start(bf16[32,24,1024]{2,1,0:T(8,128)(2,1)} %reduce-scatter.5.cloned.1.call-done), calls=%async_computation.6 | async-start | bytes 3145728 | tf_op jit(solution)/shard_map/all_to_all | solution.py:44
  269.4 0.1 copy.10
  269.5 0.6 gather_fusion
  270.2 0.6 gather_fusion.4
  270.8 0.1 reshape.174
  270.9 0.1 reduce_sum.27
  271.0 0.1 broadcast_divide_fusion
  271.1 20.9 %all-to-all-done.4 = bf16[32,24,1024]{2,1,0:T(8,128)(2,1)S(1)} async-done(((bf16[32,24,1024]{2,1,0:T(8,128)(2,1)}), bf16[32,24,1024]{2,1,0:T(8,128)(2,1)S(1)}, u32[]{:S(2)}, u32[]{:S(2)}) %all-to-all-start.4) | async-done | bytes 1572896 | tf_op jit(solution)/shard_map/all_to_all | solution.py:44
  292.1 0.3 pad_maximum_fusion
  292.4 0.4 copy.13
  292.8 5.3 %gather_fusion.5 = bf16[1024,1024]{1,0:T(8,128)(2,1)} fusion(bf16[1536,1024]{1,0:T(8,128)(2,1)S(1)} %bitcast.63, s32[1024]{0:T(1024)S(1)} %broadcast_clamp_fusion), kind=kCustom, calls=%fused_computation.5 | custom fusion | bytes 4198400 | tf_op jit(solution)/shard_map/gather | solution.py:50
  298.1 3.7 %fusion = bf16[128,1024]{1,0:T(8,128)(2,1)} fusion(bf16[1024,1024]{1,0:T(8,128)(2,1)} %gather_fusion.5, f32[128,8]{1,0:T(8,128)S(1)} %broadcast_divide_fusion), kind=kLoop, calls=%fused_computation.10 | loop fusion | flops 3014656 | bytes 2363392 | tf_op jit(solution)/shard_map/reduce_sum | solution.py:51
  (25 shorter events, 0.2 us)
Async XLA Ops:
  6.5 7.1 %copy-start.1 = (bf16[128,1024]{1,0:T(8,128)(2,1)S(1)}, bf16[128,1024]{1,0:T(8,128)(2,1)}, u32[]{:S(2)}) copy-start(bf16[128,1024]{1,0:T(8,128)(2,1)} %param.7) | copy-start | bytes 786436
  6.5 41.4 %all-gather.5.cloned.1.call-start = ((), (), s32[]{:S(2)}) async-start(), calls=%async_computation.8 | async-start | bytes 1310720 | tf_op jit(solution)/shard_map/all_gather | solution.py:34
  7.3 105.6 %all-gather.3.cloned.1.call-start = ((), (), s32[]{:S(2)}) async-start(), calls=%async_computation.7 | async-start | bytes 7864320 | tf_op jit(solution)/shard_map/all_gather | solution.py:33
  47.8 148.0 %reduce-scatter.3.cloned.1.call-start = ((), (), s32[]{:S(2)}) async-start(), calls=%async_computation.9 | async-start | bytes 7864320 | tf_op jit(solution)/shard_map/reduce_scatter | solution.py:39
  131.8 0.7 copy-start.3
  131.8 1.2 copy-start
  136.2 35.0 %all-to-all-start.3 = ((bf16[32,8,4096]{2,1,0:T(8,128)(2,1)}), bf16[32,8,4096]{2,1,0:T(8,128)(2,1)S(1)}, u32[]{:S(2)}, u32[]{:S(2)}) async-start(bf16[32,8,4096]{2,1,0:T(8,128)(2,1)} %bitcast.65), calls=%async_computation.4 | async-start | bytes 4194304 | tf_op jit(solution)/shard_map/all_to_all | solution.py:41
  142.9 118.9 %reduce-scatter.5.cloned.1.call-start = ((), (), s32[]{:S(2)}) async-start(), calls=%async_computation.10 | async-start | bytes 7864320 | tf_op jit(solution)/shard_map/reduce_scatter | solution.py:43
  191.8 77.6 %copy-start.2 = (s32[128,8]{0,1:T(8,128)S(1)}, s32[128,8]{0,1:T(8,128)}, u32[]{:S(2)}) copy-start(s32[128,8]{0,1:T(8,128)} %param.12) | copy-start | bytes 12292
  261.8 30.3 %all-to-all-start.4 = ((bf16[32,24,1024]{2,1,0:T(8,128)(2,1)}), bf16[32,24,1024]{2,1,0:T(8,128)(2,1)S(1)}, u32[]{:S(2)}, u32[]{:S(2)}) async-start(bf16[32,24,1024]{2,1,0:T(8,128)(2,1)} %reduce-scatter.5.cloned.1.call-done), calls=%async_computation.6 | async-start | bytes 3145728 | tf_op jit(solution)/shard_map/all_to_all | solution.py:44
Sparse Core Ops, SparseCore 0:
  9.0 25.7 all-gather.4
  47.9 63.9 all-gather.2
  131.9 63.7 reduce-scatter.2
  198.0 63.7 reduce-scatter.4

commit v5 on v4

--- a/solution.py
+++ b/solution.py
@@ -27,7 +27,8 @@
     places = jnp.sum(earlier * one_hot.astype(jnp.float32), 1).astype(jnp.int32)
     target = chosen * capacity + places
     row_ids = jnp.arange(pairs, dtype=jnp.int32) // choose
-    slot_rows = jnp.zeros((experts * capacity,), jnp.int32).at[target].set(row_ids)
+    picks = (target[:, None] == jnp.arange(experts * capacity, dtype=jnp.int32)[None, :]).astype(jnp.bfloat16)
+    slot_rows = jnp.dot(row_ids.astype(jnp.bfloat16), picks, preferred_element_type=jnp.float32).astype(jnp.int32)
     slot_rows = slot_rows.reshape(groups, local_experts, capacity)
     arrived = lax.all_to_all(tokens[slot_rows[:, 0]], "expert", split_axis=0, concat_axis=0, tiled=True)
     full0 = lax.all_gather(arrived, "hidden", axis=2, tiled=True)

time: 309 us -> 306 us (level)
  local copies, waits for them, and re-layouts: 36.1 us -> 32.1 us
    scatter x1 -> x0, local copies, waits for them, and re-layouts: 4.32 us -> none  [body(): jnp.zeros((experts * capacity,), jnp.int32).at[target].set(row_ids)]
    unnamed x10 -> x12, local copies, waits for them, and re-layouts: 6.44 us -> 6.51 us
  transfers between devices with their start and end apart: 6 -> 6, of which waited for: 4 -> 4; matrix products, arithmetic and copies ran while one was open for 16% -> 15% of each run, Pallas kernels for 0% -> 0%
where the time goes in v5:
time: 306 us; the launch traced here: 305 us
  blocking collectives  117 us (38%)
  waiting for transfers between devices  84.5 us (28%)
  matrix products  39.8 us (13%)
  local copies, waits for them, and re-layouts  32.1 us (10%)
  starting transfers between devices  14.4 us (5%)
  between operations  13.4 us (4%)
  other arithmetic  4.22 us (1%)
    all_to_all x1, blocking collectives, body(): lax.all_to_all(whole_rows[slot_rows[:, 1, :lead]], 'expert', split_axis=0...  55 us
    reduce_scatter x1, waiting for transfers between devices, body(): summed1 = lax.psum_scatter(part1, 'hidden', scatter_dimension=2, tiled=True)  35.6 us
    all_to_all x1, blocking collectives, body(): lax.all_to_all(tokens[slot_rows[:, 0]], 'expert', split_axis=0, concat_ax...  31.3 us
    all_to_all x1, blocking collectives, body(): lax.all_to_all(s, 'expert', split_axis=0, concat_axis=0, tiled=True)  30.4 us
    dot_general x2, matrix products, expert_part(): jnp.einsum('scf,fd->scd', hidden_acts, w_down, preferred_element_type=jnp...  24.9 us
    all_to_all x1, waiting for transfers between devices, body(): lax.all_to_all(whole_rows[tail_rows], 'expert', split_axis=0, concat_axis...  23.6 us
    all_to_all x1, waiting for transfers between devices, body(): lax.all_to_all(s, 'expert', split_axis=0, concat_axis=0, tiled=True)  20.6 us
    dot_general x2, matrix products, expert_part(): jnp.einsum('scd,df->scf', arrived, w_gate, preferred_element_type=jnp.flo...  13 us
  transfers between devices with their start and end apart: 6, of which 4 were waited for; matrix products, arithmetic and copies ran while one was open for 15% of the time, Pallas kernels for 0%

profile of v5, /device:TPU:1, one launch (start us, length us, event | category | flops | bytes accessed | tf_op | source)
XLA Modules:
  0.0 305.1 jit_solution(5399726940818421301)
XLA Ops:
  6.5 0.7 all-gather.5.cloned.1.call-update
  7.3 0.0 all-gather.3.cloned.1.call-start
  7.3 0.8 copy.17
  8.1 0.1 reshape.109
  8.2 0.6 fusion.33
  8.8 1.3 fusion.34
  10.1 0.1 reshape.110
  10.3 0.1 reshape.122
  10.4 2.8 gather_fusion.1
  13.2 31.3 %all_to_all.25 = bf16[32,24,1024]{2,1,0:T(8,128)(2,1)} all-to-all(bf16[32,24,1024]{2,1,0:T(8,128)(2,1)S(1)} %bitcast.66), channel_id=1, replica_groups=mesh['expert'=32,'hidden'=4] {'expert'}, dimensions={0} | all-to-all | bytes 3145728 | tf_op jit(solution)/shard_map/all_to_all | solution.py:33
  44.5 0.0 all-gather.3.cloned.1.call-update
  44.5 0.0 reduce-scatter.3.cloned.1.call-start
  44.6 0.1 reshape.130
  44.7 0.0 all-gather.5.cloned.1.call-done
  44.7 9.9 %gather_fusion.2 = bf16[512,4096]{1,0:T(8,128)(2,1)} fusion(bf16[128,4096]{1,0:T(8,128)(2,1)} %all-gather.5.cloned.1.call-done, s32[1024]{0:T(1024)S(1)} %pad_clamp_fusion.1), kind=kCustom, calls=%fused_computation.2 | custom fusion | bytes 8390656 | tf_op jit(solution)/shard_map/gather | solution.py:37
  54.7 55.0 %all_to_all.26 = bf16[32,16,4096]{2,1,0:T(8,128)(2,1)} all-to-all(bf16[32,16,4096]{2,1,0:T(8,128)(2,1)} %bitcast.62), channel_id=1, replica_groups=mesh['expert'=32,'hidden'=4] {'expert'}, dimensions={0} | all-to-all | bytes 8388608 | tf_op jit(solution)/shard_map/all_to_all | solution.py:37
  109.6 6.5 %fusion.11 = f32[32,24,384]{2,1,0:T(8,128)S(1)} fusion(bf16[32,24,4096]{2,1,0:T(8,128)(2,1)} %all-gather.3.cloned.1.call-done, bf16[2,4096,384]{2,1,0:T(8,128)(2,1)} %param.8), kind=kOutput, calls=%fused_computation.23 | convolution fusion | flops 2415919104 | bytes 10616832 | tf_op jit(solution)/shard_map/scd,df->scf/dot_general | solution.py:7
  116.1 12.4 %convolution_convert_fusion.1 = bf16[32,24,4096]{2,1,0:T(8,128)(2,1)} fusion(bf16[2,384,4096]{2,1,0:T(8,128)(2,1)} %param.10, bf16[32,24,4096]{2,1,0:T(8,128)(2,1)} %all-gather.3.cloned.1.call-done, bf16[2,4096,384]{2,1,0:T(8,128)(2,1)} %param.9, f32[32,24,384]{2,1,0:T(8,128)S(1)} %fusion.11), kind=kOutput, calls=%fused_computation.7 | convolution fusion | flops 4836753408 | bytes 20054016 | tf_op jit(solution)/shard_map/scf,fd->scd/dot_general | solution.py:10
  128.6 0.0 reduce-scatter.3.cloned.1.call-update
  128.6 0.1 slice.50
  128.7 0.5 copy-done.4
  129.2 0.1 reshape.138
  129.3 0.5 copy-done
  129.8 3.2 %gather_fusion.3 = bf16[256,4096]{1,0:T(8,128)(2,1)} fusion(bf16[128,4096]{1,0:T(8,128)(2,1)S(1)} %copy-done, s32[1024]{0:T(1024)S(1)} %get-tuple-element.11), kind=kCustom, calls=%fused_computation.3 | custom fusion | bytes 4195328 | tf_op jit(solution)/shard_map/gather | solution.py:42
  133.0 6.7 %all-to-all-start.3 = ((bf16[32,8,4096]{2,1,0:T(8,128)(2,1)}), bf16[32,8,4096]{2,1,0:T(8,128)(2,1)S(1)}, u32[]{:S(2)}, u32[]{:S(2)}) async-start(bf16[32,8,4096]{2,1,0:T(8,128)(2,1)} %bitcast.63), calls=%async_computation.4 | async-start | bytes 4194304 | tf_op jit(solution)/shard_map/all_to_all | solution.py:42
  139.7 0.0 reduce-scatter.5.cloned.1.call-start
  139.7 4.7 %constant_dynamic-update-slice_fusion.1 = bf16[32,24,4096]{2,1,0:T(8,128)(2,1)} fusion(bf16[32,16,4096]{2,1,0:T(8,128)(2,1)} %all_to_all.26), kind=kLoop, calls=%fused_computation.61 | loop fusion | bytes 8388608
  144.4 23.6 %all-to-all-done.3 = bf16[32,8,4096]{2,1,0:T(8,128)(2,1)S(1)} async-done(((bf16[32,8,4096]{2,1,0:T(8,128)(2,1)}), bf16[32,8,4096]{2,1,0:T(8,128)(2,1)S(1)}, u32[]{:S(2)}, u32[]{:S(2)}) %all-to-all-start.3) | async-done | bytes 2097184 | tf_op jit(solution)/shard_map/all_to_all | solution.py:42
  168.0 1.6 constant_dynamic-update-slice_fusion
  169.6 6.6 %fusion.6 = f32[32,24,384]{2,1,0:T(8,128)S(1)} fusion(bf16[32,24,4096]{2,1,0:T(8,128)(2,1)} %constant_dynamic-update-slice_fusion, bf16[2,4096,384]{2,1,0:T(8,128)(2,1)} %param.8), kind=kOutput, calls=%fused_computation.18 | convolution fusion | flops 2415919104 | bytes 10616832 | tf_op jit(solution)/shard_map/scd,df->scf/dot_general | solution.py:7
  176.2 12.4 %convolution_convert_fusion = bf16[32,24,4096]{2,1,0:T(8,128)(2,1)} fusion(bf16[2,384,4096]{2,1,0:T(8,128)(2,1)} %param.10, bf16[32,24,4096]{2,1,0:T(8,128)(2,1)} %constant_dynamic-update-slice_fusion, bf16[2,4096,384]{2,1,0:T(8,128)(2,1)} %param.9, f32[32,24,384]{2,1,0:T(8,128)S(1)} %fusion.6), kind=kOutput, calls=%fused_computation.6 | convolution fusion | flops 4836753408 | bytes 20054016 | tf_op jit(solution)/shard_map/scf,fd->scd/dot_general | solution.py:10
  188.7 3.9 %reduce-scatter.3.cloned.1.call-done = bf16[32,24,1024]{2,1,0:T(8,128)(2,1)} async-done(((bf16[32,24,4096]{2,1,0:T(8,128)(2,1)}), bf16[32,24,1024]{2,1,0:T(8,128)(2,1)}) %reduce-scatter.3.cloned.1.call-update) | async-done | bytes 1572880 | tf_op jit(solution)/shard_map/reduce_scatter | solution.py:40
  192.5 30.4 %all_to_all.27 = bf16[32,24,1024]{2,1,0:T(8,128)(2,1)S(1)} all-to-all(bf16[32,24,1024]{2,1,0:T(8,128)(2,1)} %reduce-scatter.3.cloned.1.call-done), channel_id=1, replica_groups=mesh['expert'=32,'hidden'=4] {'expert'}, dimensions={0} | all-to-all | bytes 3145728 | tf_op jit(solution)/shard_map/all_to_all | solution.py:45
  222.9 35.6 %reduce-scatter.5.cloned.1.call-done = bf16[32,24,1024]{2,1,0:T(8,128)(2,1)} async-done(((bf16[32,24,4096]{2,1,0:T(8,128)(2,1)}), bf16[32,24,1024]{2,1,0:T(8,128)(2,1)}) %reduce-scatter.5.cloned.1.call-update) | async-done | bytes 1572880 | tf_op jit(solution)/shard_map/reduce_scatter | solution.py:44
  258.6 7.6 %all-to-all-start.4 = ((bf16[32,24,1024]{2,1,0:T(8,128)(2,1)}), bf16[32,24,1024]{2,1,0:T(8,128)(2,1)S(1)}, u32[]{:S(2)}, u32[]{:S(2)}) async-start(bf16[32,24,1024]{2,1,0:T(8,128)(2,1)} %reduce-scatter.5.cloned.1.call-done), calls=%async_computation.6 | async-start | bytes 3145728 | tf_op jit(solution)/shard_map/all_to_all | solution.py:45
  266.2 0.1 copy.16
  266.3 0.1 convert_element_type.56
  266.5 0.1 copy.20
  266.6 0.7 gather_fusion
  267.2 0.6 gather_fusion.4
  267.9 0.1 reshape.154
  268.0 0.1 reduce_sum.27
  268.1 0.1 broadcast_divide_fusion
  268.2 20.6 %all-to-all-done.4 = bf16[32,24,1024]{2,1,0:T(8,128)(2,1)S(1)} async-done(((bf16[32,24,1024]{2,1,0:T(8,128)(2,1)}), bf16[32,24,1024]{2,1,0:T(8,128)(2,1)S(1)}, u32[]{:S(2)}, u32[]{:S(2)}) %all-to-all-start.4) | async-done | bytes 1572896 | tf_op jit(solution)/shard_map/all_to_all | solution.py:45
  288.8 0.3 pad_maximum_fusion
  289.1 0.4 copy.18
  289.6 5.3 %gather_fusion.5 = bf16[1024,1024]{1,0:T(8,128)(2,1)} fusion(bf16[1536,1024]{1,0:T(8,128)(2,1)S(1)} %bitcast.61, s32[1024]{0:T(1024)S(1)} %broadcast_clamp_fusion), kind=kCustom, calls=%fused_computation.5 | custom fusion | bytes 4198400 | tf_op jit(solution)/shard_map/gather | solution.py:51
  294.9 3.7 %fusion.1 = bf16[128,1024]{1,0:T(8,128)(2,1)} fusion(bf16[1024,1024]{1,0:T(8,128)(2,1)} %gather_fusion.5, f32[128,8]{1,0:T(8,128)S(1)} %broadcast_divide_fusion), kind=kLoop, calls=%fused_computation.11 | loop fusion | flops 3014656 | bytes 2363392 | tf_op jit(solution)/shard_map/reduce_sum | solution.py:52
  (30 shorter events, 0.2 us)
Async XLA Ops:
  6.5 3.8 %copy-start.1 = (bf16[128,1024]{1,0:T(8,128)(2,1)S(1)}, bf16[128,1024]{1,0:T(8,128)(2,1)}, u32[]{:S(2)}) copy-start(bf16[128,1024]{1,0:T(8,128)(2,1)} %param.7) | copy-start | bytes 786436
  6.5 38.2 %all-gather.5.cloned.1.call-start = ((), (), s32[]{:S(2)}) async-start(), calls=%async_computation.8 | async-start | bytes 1310720 | tf_op jit(solution)/shard_map/all_gather | solution.py:35
  7.3 102.4 %all-gather.3.cloned.1.call-start = ((), (), s32[]{:S(2)}) async-start(), calls=%async_computation.7 | async-start | bytes 7864320 | tf_op jit(solution)/shard_map/all_gather | solution.py:34
  44.5 148.0 %reduce-scatter.3.cloned.1.call-start = ((), (), s32[]{:S(2)}) async-start(), calls=%async_computation.9 | async-start | bytes 7864320 | tf_op jit(solution)/shard_map/reduce_scatter | solution.py:40
  128.6 0.7 copy-start.4
  128.6 1.2 copy-start
  133.0 35.0 %all-to-all-start.3 = ((bf16[32,8,4096]{2,1,0:T(8,128)(2,1)}), bf16[32,8,4096]{2,1,0:T(8,128)(2,1)S(1)}, u32[]{:S(2)}, u32[]{:S(2)}) async-start(bf16[32,8,4096]{2,1,0:T(8,128)(2,1)} %bitcast.63), calls=%async_computation.4 | async-start | bytes 4194304 | tf_op jit(solution)/shard_map/all_to_all | solution.py:42
  139.7 118.9 %reduce-scatter.5.cloned.1.call-start = ((), (), s32[]{:S(2)}) async-start(), calls=%async_computation.10 | async-start | bytes 7864320 | tf_op jit(solution)/shard_map/reduce_scatter | solution.py:44
  188.6 77.6 %copy-start.3 = (s32[128,8]{0,1:T(8,128)S(1)}, s32[128,8]{0,1:T(8,128)}, u32[]{:S(2)}) copy-start(s32[128,8]{0,1:T(8,128)} %param.12) | copy-start | bytes 12292
  188.6 77.8 %copy-start.2 = (s32[128,8]{0,1:T(8,128)S(1)}, s32[128,8]{0,1:T(8,128)}, u32[]{:S(2)}) copy-start(s32[128,8]{0,1:T(8,128)} %param.11) | copy-start | bytes 12292
  258.6 30.3 %all-to-all-start.4 = ((bf16[32,24,1024]{2,1,0:T(8,128)(2,1)}), bf16[32,24,1024]{2,1,0:T(8,128)(2,1)S(1)}, u32[]{:S(2)}, u32[]{:S(2)}) async-start(bf16[32,24,1024]{2,1,0:T(8,128)(2,1)} %reduce-scatter.5.cloned.1.call-done), calls=%async_computation.6 | async-start | bytes 3145728 | tf_op jit(solution)/shard_map/all_to_all | solution.py:45
Sparse Core Ops, SparseCore 0:
  9.0 25.7 all-gather.4
  44.7 63.9 all-gather.2
  128.7 63.7 reduce-scatter.2
  194.8 63.7 reduce-scatter.4

commit v6 on v5

--- a/solution.py
+++ b/solution.py
@@ -9,6 +9,14 @@
     hidden_acts = (jax.nn.silu(gate_acts) * up_acts).astype(jnp.bfloat16)
     partial_value = jnp.einsum("scf,fd->scd", hidden_acts, w_down, preferred_element_type=jnp.float32)
     return partial_value.astype(jnp.bfloat16)
+
+
+def reduce_hidden(part):
+    size = lax.axis_size("hidden")
+    quarters = part.reshape(part.shape[:-1] + (size, part.shape[-1] // size))
+    quarters = jnp.moveaxis(quarters, -2, 0)
+    gathered = lax.all_to_all(quarters, "hidden", split_axis=0, concat_axis=0, tiled=True)
+    return jnp.sum(gathered.astype(jnp.float32), 0).astype(jnp.bfloat16)
 
 
 def body(tokens, w_gate, w_up, w_down, routes, gate_levels, ancestors):
@@ -40,8 +48,11 @@
     summed0 = lax.psum_scatter(part0, "hidden", scatter_dimension=2, tiled=True)
     tail_rows, part0 = lax.optimization_barrier((slot_rows[:, 1, lead:], part0))
     tail = lax.all_to_all(whole_rows[tail_rows], "expert", split_axis=0, concat_axis=0, tiled=True)
-    part1 = expert_part(jnp.concatenate([head, tail], 1), w_gate[1], w_up[1], w_down[1])
-    summed1 = lax.psum_scatter(part1, "hidden", scatter_dimension=2, tiled=True)
+    part_head = expert_part(head, w_gate[1], w_up[1], w_down[1])
+    summed_head = lax.psum_scatter(part_head, "hidden", scatter_dimension=2, tiled=True)
+    part_tail = expert_part(tail, w_gate[1], w_up[1], w_down[1])
+    summed_tail = reduce_hidden(part_tail)
+    summed1 = jnp.concatenate([summed_head, summed_tail], 1)
     per_expert = [lax.all_to_all(s, "expert", split_axis=0, concat_axis=0, tiled=True) for s in (summed0, summed1)]
     returned = jnp.stack(per_expert, 1)
     returned = returned.reshape(experts * capacity, returned.shape[3])

time: 306 us -> 319 us (1.042)
  blocking collectives: 117 us -> 201 us
  waiting for transfers between devices: 84.5 us -> 21.3 us
  starting transfers between devices: 14.4 us -> 3.88 us
  matrix products: 39.8 us -> 46.7 us
  local copies, waits for them, and re-layouts: 32.1 us -> 26.1 us
    all_to_all x0 -> x2, blocking collectives: none -> 87 us  [the longest x1 52.5 us: reduce_hidden(): lax.all_to_all(quarters, 'hidden', split_axis=0, concat_axis=0, tiled=True)]
    reduce_scatter x1, waiting for transfers between devices: 35.6 us -> 0.02 us  [body(): lax.psum_scatter(part_head, 'hidden', scatter_dimension=2, tiled=True)]
    all_to_all x1 -> x0, waiting for transfers between devices: 23.6 us -> none  [body(): lax.all_to_all(whole_rows[tail_rows], 'expert', split_axis=0, concat_axis...]
    all_to_all x1 -> x0, starting transfers between devices: 6.67 us -> none  [body(): lax.all_to_all(whole_rows[tail_rows], 'expert', split_axis=0, concat_axis...]
    dot_general x2 -> x3, matrix products: 24.9 us -> 29.6 us  [expert_part(): jnp.einsum('scf,fd->scd', hidden_acts, w_down, preferred_element_type=jnp...]
    reduce_scatter x1, waiting for transfers between devices: 3.85 us -> 0.01 us  [body(): summed0 = lax.psum_scatter(part0, 'hidden', scatter_dimension=2, tiled=True)]
    all_to_all x1, starting transfers between devices: 7.6 us -> 3.76 us  [body(): lax.all_to_all(s, 'expert', split_axis=0, concat_axis=0, tiled=True)]
    unnamed x12 -> x13, local copies, waits for them, and re-layouts: 6.51 us -> 3.15 us
  transfers between devices with their start and end apart: 6 -> 5, of which waited for: 4 -> 1; matrix products, arithmetic and copies ran while one was open for 15% -> 16% of each run, Pallas kernels for 0% -> 0%
where the time goes in v6:
time: 319 us; the launch traced here: 318 us
  blocking collectives  201 us (63%)
  matrix products  46.7 us (15%)
  local copies, waits for them, and re-layouts  26.1 us (8%)
  waiting for transfers between devices  21.3 us (7%)
  between operations  13.5 us (4%)
  other arithmetic  6.01 us (2%)
  starting transfers between devices  3.88 us (1%)
    all_to_all x1, blocking collectives, body(): lax.all_to_all(whole_rows[slot_rows[:, 1, :lead]], 'expert', split_axis=0...  55 us
    all_to_all x1, blocking collectives, reduce_hidden(): lax.all_to_all(quarters, 'hidden', split_axis=0, concat_axis=0, tiled=True)  52.5 us
    all_to_all x1, blocking collectives, body(): lax.all_to_all(whole_rows[tail_rows], 'expert', split_axis=0, concat_axis...  34.5 us
    all_to_all x1, blocking collectives, body(): lax.all_to_all(tokens[slot_rows[:, 0]], 'expert', split_axis=0, concat_ax...  31.3 us
    dot_general x3, matrix products, expert_part(): jnp.einsum('scf,fd->scd', hidden_acts, w_down, preferred_element_type=jnp...  29.6 us
    all_to_all x1, blocking collectives, body(): lax.all_to_all(s, 'expert', split_axis=0, concat_axis=0, tiled=True)  27.5 us
    all_to_all x1, waiting for transfers between devices, body(): lax.all_to_all(s, 'expert', split_axis=0, concat_axis=0, tiled=True)  20.5 us
    dot_general x3, matrix products, expert_part(): jnp.einsum('scd,df->scf', arrived, w_gate, preferred_element_type=jnp.flo...  15.3 us
  transfers between devices with their start and end apart: 5, of which 1 were waited for; matrix products, arithmetic and copies ran while one was open for 16% of the time, Pallas kernels for 0%

profile of v6, /device:TPU:1, one launch (start us, length us, event | category | flops | bytes accessed | tf_op | source)
XLA Modules:
  0.0 318.2 jit_solution(18126302475347370867)
XLA Ops:
  6.5 0.7 all-gather.5.cloned.1.call-update
  7.3 0.0 all-gather.3.cloned.1.call-start
  7.3 0.8 copy.23
  8.1 0.1 reshape.112
  8.2 0.6 fusion.47
  8.8 1.3 fusion.48
  10.1 0.1 reshape.113
  10.3 0.1 reshape.126
  10.4 2.8 gather_fusion.1
  13.2 31.3 %all_to_all.30 = bf16[32,24,1024]{2,1,0:T(8,128)(2,1)} all-to-all(bf16[32,24,1024]{2,1,0:T(8,128)(2,1)S(1)} %bitcast.85), channel_id=1, replica_groups=mesh['expert'=32,'hidden'=4] {'expert'}, dimensions={0} | all-to-all | bytes 3145728 | tf_op jit(solution)/shard_map/all_to_all | solution.py:41
  44.5 0.0 reduce-scatter.5.cloned.1.call-start
  44.6 0.1 reshape.134
  44.7 0.0 all-gather.5.cloned.1.call-done
  44.7 10.0 %gather_fusion.2 = bf16[512,4096]{1,0:T(8,128)(2,1)} fusion(bf16[128,4096]{1,0:T(8,128)(2,1)} %all-gather.5.cloned.1.call-done, s32[1024]{0:T(1024)S(1)} %pad_clamp_fusion.1), kind=kCustom, calls=%fused_computation.2 | custom fusion | bytes 8390656 | tf_op jit(solution)/shard_map/gather | solution.py:45
  54.7 55.0 %all_to_all.31 = bf16[32,16,4096]{2,1,0:T(8,128)(2,1)} all-to-all(bf16[32,16,4096]{2,1,0:T(8,128)(2,1)} %bitcast.80), channel_id=1, replica_groups=mesh['expert'=32,'hidden'=4] {'expert'}, dimensions={0} | all-to-all | bytes 8388608 | tf_op jit(solution)/shard_map/all_to_all | solution.py:45
  109.7 5.5 %fusion.11 = f32[32,16,384]{2,1,0:T(8,128)S(1)} fusion(bf16[32,16,4096]{2,1,0:T(8,128)(2,1)} %all_to_all.31, bf16[2,4096,384]{2,1,0:T(8,128)(2,1)} %param.8), kind=kOutput, calls=%fused_computation.24 | convolution fusion | flops 1610612736 | bytes 8126464 | tf_op jit(solution)/shard_map/scd,df->scf/dot_general | solution.py:7
  115.2 10.5 %convolution_convert_fusion.1 = bf16[32,16,4096]{2,1,0:T(8,128)(2,1)} fusion(bf16[2,384,4096]{2,1,0:T(8,128)(2,1)} %param.10, bf16[32,16,4096]{2,1,0:T(8,128)(2,1)} %all_to_all.31, bf16[2,4096,384]{2,1,0:T(8,128)(2,1)} %param.9, f32[32,16,384]{2,1,0:T(8,128)S(1)} %fusion.11), kind=kOutput, calls=%fused_computation.9 | convolution fusion | flops 3224502272 | bytes 15466496 | tf_op jit(solution)/shard_map/scf,fd->scd/dot_general | solution.py:10
  125.7 0.0 reduce-scatter.3.cloned.1.call-start
  125.8 6.5 %fusion.16 = f32[32,24,384]{2,1,0:T(8,128)S(1)} fusion(bf16[32,24,4096]{2,1,0:T(8,128)(2,1)} %all-gather.3.cloned.1.call-done, bf16[2,4096,384]{2,1,0:T(8,128)(2,1)} %param.8), kind=kOutput, calls=%fused_computation.29 | convolution fusion | flops 2415919104 | bytes 10616832 | tf_op jit(solution)/shard_map/scd,df->scf/dot_general | solution.py:7
  132.3 13.2 %convolution_convert_fusion = bf16[32,24,4096]{2,1,0:T(8,128)(2,1)} fusion(bf16[2,384,4096]{2,1,0:T(8,128)(2,1)} %param.10, bf16[32,24,4096]{2,1,0:T(8,128)(2,1)} %all-gather.3.cloned.1.call-done, bf16[2,4096,384]{2,1,0:T(8,128)(2,1)} %param.9, f32[32,24,384]{2,1,0:T(8,128)S(1)} %fusion.16), kind=kOutput, calls=%fused_computation.6 | convolution fusion | flops 4836753408 | bytes 20054016 | tf_op jit(solution)/shard_map/scf,fd->scd/dot_general | solution.py:10
  145.5 0.1 slice.53
  145.6 0.1 reshape.142
  145.7 1.0 copy-done
  146.7 1.8 gather_fusion.3
  148.5 34.5 %all_to_all.32 = bf16[32,8,4096]{2,1,0:T(8,128)(2,1)S(1)} all-to-all(bf16[32,8,4096]{2,1,0:T(8,128)(2,1)S(1)} %bitcast.82), channel_id=1, replica_groups=mesh['expert'=32,'hidden'=4] {'expert'}, dimensions={0} | all-to-all | bytes 4194304 | tf_op jit(solution)/shard_map/all_to_all | solution.py:50
  183.1 1.3 copy-done.2
  184.4 3.3 %fusion.9 = f32[32,8,384]{2,1,0:T(8,128)S(1)} fusion(bf16[32,8,4096]{2,1,0:T(8,128)(2,1)S(1)} %all_to_all.32, bf16[2,4096,384]{2,1,0:T(8,128)(2,1)} %param.8), kind=kOutput, calls=%fused_computation.22 | convolution fusion | flops 805306368 | bytes 5636096 | tf_op jit(solution)/shard_map/scd,df->scf/dot_general | solution.py:7
  187.7 5.9 %convolution_convert_fusion.2 = bf16[32,8,4096]{2,1,0:T(8,128)(2,1)S(1)} fusion(bf16[2,384,4096]{2,1,0:T(8,128)(2,1)} %param.10, bf16[32,8,4096]{2,1,0:T(8,128)(2,1)} %copy-done.2, bf16[2,4096,384]{2,1,0:T(8,128)(2,1)} %param.9, f32[32,8,384]{2,1,0:T(8,128)S(1)} %fusion.9), kind=kOutput, calls=%fused_computation.10 | convolution fusion | flops 1612251136 | bytes 10878976 | tf_op jit(solution)/shard_map/scf,fd->scd/dot_general | solution.py:10
  193.6 0.2 copy.29
  193.8 52.5 %all_to_all.33 = bf16[4,32,8,1024]{3,2,1,0:T(8,128)(2,1)S(1)} all-to-all(bf16[4,32,8,1024]{3,2,1,0:T(8,128)(2,1)S(1)} %bitcast.81), channel_id=1, replica_groups=mesh['expert'=32,'hidden'=4] {'hidden'}, dimensions={0} | all-to-all | bytes 4194304 | tf_op jit(solution)/shard_map/all_to_all | solution.py:18
  246.3 0.4 reduce_sum.41
  246.7 0.0 reduce-scatter.5.cloned.1.call-done
  246.7 1.4 pad_maximum_fusion.1
  248.1 27.5 %all_to_all.34 = bf16[32,24,1024]{2,1,0:T(8,128)(2,1)S(1)} all-to-all(bf16[32,24,1024]{2,1,0:T(8,128)(2,1)S(1)} %pad_maximum_fusion.1), channel_id=1, replica_groups=mesh['expert'=32,'hidden'=4] {'expert'}, dimensions={0} | all-to-all | bytes 3145728 | tf_op jit(solution)/shard_map/all_to_all | solution.py:56
  275.7 3.8 %all-to-all-start.2 = ((bf16[32,24,1024]{2,1,0:T(8,128)(2,1)}), bf16[32,24,1024]{2,1,0:T(8,128)(2,1)S(1)}, u32[]{:S(2)}, u32[]{:S(2)}) async-start(bf16[32,24,1024]{2,1,0:T(8,128)(2,1)} %reduce-scatter.3.cloned.1.call-done), calls=%async_computation.3 | async-start | bytes 3145728 | tf_op jit(solution)/shard_map/all_to_all | solution.py:56
  279.5 0.1 copy.22
  279.6 0.1 convert_element_type.66
  279.7 0.1 copy.27
  279.9 0.6 gather_fusion
  280.5 0.6 gather_fusion.4
  281.2 0.1 reshape.158
  281.3 0.1 reduce_sum.39
  281.4 0.1 broadcast_divide_fusion
  281.5 20.5 %all-to-all-done.2 = bf16[32,24,1024]{2,1,0:T(8,128)(2,1)S(1)} async-done(((bf16[32,24,1024]{2,1,0:T(8,128)(2,1)}), bf16[32,24,1024]{2,1,0:T(8,128)(2,1)S(1)}, u32[]{:S(2)}, u32[]{:S(2)}) %all-to-all-start.2) | async-done | bytes 1572896 | tf_op jit(solution)/shard_map/all_to_all | solution.py:56
  301.9 0.3 pad_maximum_fusion
  302.2 0.4 copy.25
  302.7 5.4 %gather_fusion.5 = bf16[1024,1024]{1,0:T(8,128)(2,1)} fusion(bf16[1536,1024]{1,0:T(8,128)(2,1)S(1)} %bitcast.79, s32[1024]{0:T(1024)S(1)} %broadcast_clamp_fusion), kind=kCustom, calls=%fused_computation.5 | custom fusion | bytes 4198400 | tf_op jit(solution)/shard_map/gather | solution.py:62
  308.0 3.7 %fusion.1 = bf16[128,1024]{1,0:T(8,128)(2,1)} fusion(bf16[1024,1024]{1,0:T(8,128)(2,1)} %gather_fusion.5, f32[128,8]{1,0:T(8,128)S(1)} %broadcast_divide_fusion), kind=kLoop, calls=%fused_computation.12 | loop fusion | flops 3014656 | bytes 2363392 | tf_op jit(solution)/shard_map/reduce_sum | solution.py:63
  (36 shorter events, 0.3 us)
Async XLA Ops:
  6.5 3.8 %copy-start.1 = (bf16[128,1024]{1,0:T(8,128)(2,1)S(1)}, bf16[128,1024]{1,0:T(8,128)(2,1)}, u32[]{:S(2)}) copy-start(bf16[128,1024]{1,0:T(8,128)(2,1)} %param.7) | copy-start | bytes 786436
  6.5 38.2 %all-gather.5.cloned.1.call-start = ((), (), s32[]{:S(2)}) async-start(), calls=%async_computation.9 | async-start | bytes 1310720 | tf_op jit(solution)/shard_map/all_gather | solution.py:43
  7.3 102.4 %all-gather.3.cloned.1.call-start = ((), (), s32[]{:S(2)}) async-start(), calls=%async_computation.8 | async-start | bytes 7864320 | tf_op jit(solution)/shard_map/all_gather | solution.py:42
  44.5 202.2 %reduce-scatter.5.cloned.1.call-start = ((), (), s32[]{:S(2)}) async-start(), calls=%async_computation.11 | async-start | bytes 5242880 | tf_op jit(solution)/shard_map/reduce_scatter | solution.py:52
  125.7 149.9 %reduce-scatter.3.cloned.1.call-start = ((), (), s32[]{:S(2)}) async-start(), calls=%async_computation.10 | async-start | bytes 7864320 | tf_op jit(solution)/shard_map/reduce_scatter | solution.py:48
  145.4 1.2 copy-start
  183.1 1.4 copy-start.2
  248.1 31.4 %copy-start.4 = (s32[128,8]{0,1:T(8,128)S(1)}, s32[128,8]{0,1:T(8,128)}, u32[]{:S(2)}) copy-start(s32[128,8]{0,1:T(8,128)} %param.12) | copy-start | bytes 12292
  248.1 31.6 %copy-start.3 = (s32[128,8]{0,1:T(8,128)S(1)}, s32[128,8]{0,1:T(8,128)}, u32[]{:S(2)}) copy-start(s32[128,8]{0,1:T(8,128)} %param.11) | copy-start | bytes 12292
  248.1 31.7 %copy-start.5 = (s32[128]{0:T(128)S(1)}, s32[128]{0:T(128)}, u32[]{:S(2)}) copy-start(s32[128]{0:T(128)} %param.13) | copy-start | bytes 1540
  275.7 26.3 %all-to-all-start.2 = ((bf16[32,24,1024]{2,1,0:T(8,128)(2,1)}), bf16[32,24,1024]{2,1,0:T(8,128)(2,1)S(1)}, u32[]{:S(2)}, u32[]{:S(2)}) async-start(bf16[32,24,1024]{2,1,0:T(8,128)(2,1)} %reduce-scatter.3.cloned.1.call-done), calls=%async_computation.3 | async-start | bytes 3145728 | tf_op jit(solution)/shard_map/all_to_all | solution.py:56
Sparse Core Ops, SparseCore 0:
  9.0 25.7 all-gather.4
  44.7 63.9 all-gather.2
  125.9 46.5 reduce-scatter.4
  174.7 86.2 reduce-scatter.2

commit v7 on v5

--- a/solution.py
+++ b/solution.py
@@ -43,13 +43,20 @@
     part1 = expert_part(jnp.concatenate([head, tail], 1), w_gate[1], w_up[1], w_down[1])
     summed1 = lax.psum_scatter(part1, "hidden", scatter_dimension=2, tiled=True)
     per_expert = [lax.all_to_all(s, "expert", split_axis=0, concat_axis=0, tiled=True) for s in (summed0, summed1)]
-    returned = jnp.stack(per_expert, 1)
-    returned = returned.reshape(experts * capacity, returned.shape[3])
     source = target.reshape(local_rows, choose)[ancestors]
     levels = gate_levels.astype(jnp.float32)[ancestors]
     weights = levels / jnp.sum(levels, 1, keepdims=True)
-    picked = returned[source].astype(jnp.float32)
-    combined = jnp.sum(weights[:, :, None] * picked, 1)
+    slots = jnp.arange(experts * capacity, dtype=jnp.int32)
+    mixing = jnp.sum(jnp.where(source[:, :, None] == slots[None, None, :], weights[:, :, None], 0.0), 1)
+    mixing = mixing.reshape(local_rows, groups, local_experts, capacity)
+    combined = sum(
+        jnp.dot(
+            mixing[:, :, c].reshape(local_rows, groups * capacity),
+            back.reshape(groups * capacity, back.shape[2]).astype(jnp.float32),
+            precision=lax.Precision.HIGHEST,
+        )
+        for c, back in enumerate(per_expert)
+    )
     return combined.astype(jnp.bfloat16)
 
 

time: 306 us -> 299 us (0.977)
  waiting for transfers between devices: 84.5 us -> 76.7 us
  matrix products: 39.8 us -> 44.1 us
    all_to_all x1, waiting for transfers between devices: 20.6 us -> 12.7 us  [body(): lax.all_to_all(s, 'expert', split_axis=0, concat_axis=0, tiled=True)]
    gather x1 -> x0, local copies, waits for them, and re-layouts: 5.35 us -> none  [body(): picked = returned[source].astype(jnp.float32)]
    dot_general x0 -> x2, matrix products: none -> 4.3 us  [body(): jnp.dot(mixing[:, :, c].reshape(local_rows, groups * capacity), back.resh...]
  transfers between devices with their start and end apart: 6 -> 6, of which waited for: 4 -> 4; matrix products, arithmetic and copies ran while one was open for 15% -> 18% of each run, Pallas kernels for 0% -> 0%
where the time goes in v7:
time: 299 us; the launch traced here: 298 us
  blocking collectives  117 us (39%)
  waiting for transfers between devices  76.7 us (26%)
  matrix products  44.1 us (15%)
  local copies, waits for them, and re-layouts  29.5 us (10%)
  starting transfers between devices  14.4 us (5%)
  between operations  13.4 us (4%)
  other arithmetic  3.2 us (1%)
    all_to_all x1, blocking collectives, body(): lax.all_to_all(whole_rows[slot_rows[:, 1, :lead]], 'expert', split_axis=0...  55 us
    reduce_scatter x1, waiting for transfers between devices, body(): summed1 = lax.psum_scatter(part1, 'hidden', scatter_dimension=2, tiled=True)  35.7 us
    all_to_all x1, blocking collectives, body(): lax.all_to_all(tokens[slot_rows[:, 0]], 'expert', split_axis=0, concat_ax...  31.3 us
    all_to_all x1, blocking collectives, body(): lax.all_to_all(s, 'expert', split_axis=0, concat_axis=0, tiled=True)  30.4 us
    dot_general x2, matrix products, expert_part(): jnp.einsum('scf,fd->scd', hidden_acts, w_down, preferred_element_type=jnp...  24.9 us
    all_to_all x1, waiting for transfers between devices, body(): lax.all_to_all(whole_rows[tail_rows], 'expert', split_axis=0, concat_axis...  23.7 us
    dot_general x2, matrix products, expert_part(): jnp.einsum('scd,df->scf', arrived, w_gate, preferred_element_type=jnp.flo...  13 us
    all_to_all x1, waiting for transfers between devices, body(): lax.all_to_all(s, 'expert', split_axis=0, concat_axis=0, tiled=True)  12.7 us
  transfers between devices with their start and end apart: 6, of which 4 were waited for; matrix products, arithmetic and copies ran while one was open for 18% of the time, Pallas kernels for 0%

profile of v7, /device:TPU:1, one launch (start us, length us, event | category | flops | bytes accessed | tf_op | source)
XLA Modules:
  0.0 298.0 jit_solution(15591539414474010761)
XLA Ops:
  6.5 0.7 all-gather.5.cloned.1.call-update
  7.3 0.0 all-gather.3.cloned.1.call-start
  7.3 0.8 copy.20
  8.1 0.1 eq.20
  8.2 0.6 fusion.33
  8.8 1.3 fusion.34
  10.1 0.1 reshape.102
  10.3 0.1 reshape.123
  10.4 2.8 gather_fusion.2
  13.2 31.3 %all_to_all.25 = bf16[32,24,1024]{2,1,0:T(8,128)(2,1)} all-to-all(bf16[32,24,1024]{2,1,0:T(8,128)(2,1)S(1)} %bitcast.64), channel_id=1, replica_groups=mesh['expert'=32,'hidden'=4] {'expert'}, dimensions={0} | all-to-all | bytes 3145728 | tf_op jit(solution)/shard_map/all_to_all | solution.py:33
  44.5 0.0 all-gather.3.cloned.1.call-update
  44.5 0.0 reduce-scatter.3.cloned.1.call-start
  44.6 0.1 reshape.131
  44.7 0.0 all-gather.5.cloned.1.call-done
  44.7 9.9 %gather_fusion.3 = bf16[512,4096]{1,0:T(8,128)(2,1)} fusion(bf16[128,4096]{1,0:T(8,128)(2,1)} %all-gather.5.cloned.1.call-done, s32[1024]{0:T(1024)S(1)} %pad_clamp_fusion.1), kind=kCustom, calls=%fused_computation.3 | custom fusion | bytes 8390656 | tf_op jit(solution)/shard_map/gather | solution.py:37
  54.7 55.0 %all_to_all.26 = bf16[32,16,4096]{2,1,0:T(8,128)(2,1)} all-to-all(bf16[32,16,4096]{2,1,0:T(8,128)(2,1)} %bitcast.60), channel_id=1, replica_groups=mesh['expert'=32,'hidden'=4] {'expert'}, dimensions={0} | all-to-all | bytes 8388608 | tf_op jit(solution)/shard_map/all_to_all | solution.py:37
  109.6 6.5 %fusion.10 = f32[32,24,384]{2,1,0:T(8,128)S(1)} fusion(bf16[32,24,4096]{2,1,0:T(8,128)(2,1)} %all-gather.3.cloned.1.call-done, bf16[2,4096,384]{2,1,0:T(8,128)(2,1)} %param.8), kind=kOutput, calls=%fused_computation.21 | convolution fusion | flops 2415919104 | bytes 10616832 | tf_op jit(solution)/shard_map/scd,df->scf/dot_general | solution.py:7
  116.1 12.4 %convolution_convert_fusion.1 = bf16[32,24,4096]{2,1,0:T(8,128)(2,1)} fusion(bf16[2,384,4096]{2,1,0:T(8,128)(2,1)} %param.10, bf16[32,24,4096]{2,1,0:T(8,128)(2,1)} %all-gather.3.cloned.1.call-done, bf16[2,4096,384]{2,1,0:T(8,128)(2,1)} %param.9, f32[32,24,384]{2,1,0:T(8,128)S(1)} %fusion.10), kind=kOutput, calls=%fused_computation.6 | convolution fusion | flops 4836753408 | bytes 20054016 | tf_op jit(solution)/shard_map/scf,fd->scd/dot_general | solution.py:10
  128.5 0.0 reduce-scatter.3.cloned.1.call-update
  128.6 0.1 slice.58
  128.7 0.5 copy-done.4
  129.2 0.1 reshape.139
  129.3 0.5 copy-done
  129.8 3.2 %gather_fusion.4 = bf16[256,4096]{1,0:T(8,128)(2,1)} fusion(bf16[128,4096]{1,0:T(8,128)(2,1)S(1)} %copy-done, s32[1024]{0:T(1024)S(1)} %get-tuple-element.13), kind=kCustom, calls=%fused_computation.4 | custom fusion | bytes 4195328 | tf_op jit(solution)/shard_map/gather | solution.py:42
  133.0 6.7 %all-to-all-start.3 = ((bf16[32,8,4096]{2,1,0:T(8,128)(2,1)}), bf16[32,8,4096]{2,1,0:T(8,128)(2,1)S(1)}, u32[]{:S(2)}, u32[]{:S(2)}) async-start(bf16[32,8,4096]{2,1,0:T(8,128)(2,1)} %bitcast.61), calls=%async_computation.4 | async-start | bytes 4194304 | tf_op jit(solution)/shard_map/all_to_all | solution.py:42
  139.7 0.0 reduce-scatter.5.cloned.1.call-start
  139.7 4.6 %constant_dynamic-update-slice_fusion.1 = bf16[32,24,4096]{2,1,0:T(8,128)(2,1)} fusion(bf16[32,16,4096]{2,1,0:T(8,128)(2,1)} %all_to_all.26), kind=kLoop, calls=%fused_computation.60 | loop fusion | bytes 8388608
  144.4 23.7 %all-to-all-done.3 = bf16[32,8,4096]{2,1,0:T(8,128)(2,1)S(1)} async-done(((bf16[32,8,4096]{2,1,0:T(8,128)(2,1)}), bf16[32,8,4096]{2,1,0:T(8,128)(2,1)S(1)}, u32[]{:S(2)}, u32[]{:S(2)}) %all-to-all-start.3) | async-done | bytes 2097184 | tf_op jit(solution)/shard_map/all_to_all | solution.py:42
  168.0 1.5 constant_dynamic-update-slice_fusion
  169.5 6.6 %fusion.5 = f32[32,24,384]{2,1,0:T(8,128)S(1)} fusion(bf16[32,24,4096]{2,1,0:T(8,128)(2,1)} %constant_dynamic-update-slice_fusion, bf16[2,4096,384]{2,1,0:T(8,128)(2,1)} %param.8), kind=kOutput, calls=%fused_computation.16 | convolution fusion | flops 2415919104 | bytes 10616832 | tf_op jit(solution)/shard_map/scd,df->scf/dot_general | solution.py:7
  176.1 12.4 %convolution_convert_fusion = bf16[32,24,4096]{2,1,0:T(8,128)(2,1)} fusion(bf16[2,384,4096]{2,1,0:T(8,128)(2,1)} %param.10, bf16[32,24,4096]{2,1,0:T(8,128)(2,1)} %constant_dynamic-update-slice_fusion, bf16[2,4096,384]{2,1,0:T(8,128)(2,1)} %param.9, f32[32,24,384]{2,1,0:T(8,128)S(1)} %fusion.5), kind=kOutput, calls=%fused_computation.5 | convolution fusion | flops 4836753408 | bytes 20054016 | tf_op jit(solution)/shard_map/scf,fd->scd/dot_general | solution.py:10
  188.6 4.0 %reduce-scatter.3.cloned.1.call-done = bf16[32,24,1024]{2,1,0:T(8,128)(2,1)} async-done(((bf16[32,24,4096]{2,1,0:T(8,128)(2,1)}), bf16[32,24,1024]{2,1,0:T(8,128)(2,1)}) %reduce-scatter.3.cloned.1.call-update) | async-done | bytes 1572880 | tf_op jit(solution)/shard_map/reduce_scatter | solution.py:40
  192.5 30.4 %all_to_all.27 = bf16[32,24,1024]{2,1,0:T(8,128)(2,1)S(1)} all-to-all(bf16[32,24,1024]{2,1,0:T(8,128)(2,1)} %reduce-scatter.3.cloned.1.call-done), channel_id=1, replica_groups=mesh['expert'=32,'hidden'=4] {'expert'}, dimensions={0} | all-to-all | bytes 3145728 | tf_op jit(solution)/shard_map/all_to_all | solution.py:45
  222.9 35.7 %reduce-scatter.5.cloned.1.call-done = bf16[32,24,1024]{2,1,0:T(8,128)(2,1)} async-done(((bf16[32,24,4096]{2,1,0:T(8,128)(2,1)}), bf16[32,24,1024]{2,1,0:T(8,128)(2,1)}) %reduce-scatter.5.cloned.1.call-update) | async-done | bytes 1572880 | tf_op jit(solution)/shard_map/reduce_scatter | solution.py:44
  258.6 7.6 %all-to-all-start.4 = ((bf16[32,24,1024]{2,1,0:T(8,128)(2,1)}), bf16[32,24,1024]{2,1,0:T(8,128)(2,1)S(1)}, u32[]{:S(2)}, u32[]{:S(2)}) async-start(bf16[32,24,1024]{2,1,0:T(8,128)(2,1)} %reduce-scatter.5.cloned.1.call-done), calls=%async_computation.6 | async-start | bytes 3145728 | tf_op jit(solution)/shard_map/all_to_all | solution.py:45
  266.2 0.1 copy.23
  266.3 0.1 convert_element_type.48
  266.5 0.1 copy.22
  266.6 0.7 gather_fusion.1
  267.2 0.6 gather_fusion
  267.9 0.1 reduce_sum.28
  268.0 0.1 broadcast_divide_fusion
  268.1 2.9 select_reduce_fusion
  271.0 2.3 copy.24
  273.3 1.2 fusion.49
  274.5 1.7 fusion.50
  276.2 12.7 %all-to-all-done.4 = bf16[32,24,1024]{2,1,0:T(8,128)(2,1)S(1)} async-done(((bf16[32,24,1024]{2,1,0:T(8,128)(2,1)}), bf16[32,24,1024]{2,1,0:T(8,128)(2,1)S(1)}, u32[]{:S(2)}, u32[]{:S(2)}) %all-to-all-start.4) | async-done | bytes 1572896 | tf_op jit(solution)/shard_map/all_to_all | solution.py:45
  288.8 2.6 fusion.31
  (28 shorter events, 0.2 us)
Async XLA Ops:
  6.5 3.8 %copy-start.1 = (bf16[128,1024]{1,0:T(8,128)(2,1)S(1)}, bf16[128,1024]{1,0:T(8,128)(2,1)}, u32[]{:S(2)}) copy-start(bf16[128,1024]{1,0:T(8,128)(2,1)} %param.7) | copy-start | bytes 786436
  6.5 38.2 %all-gather.5.cloned.1.call-start = ((), (), s32[]{:S(2)}) async-start(), calls=%async_computation.8 | async-start | bytes 1310720 | tf_op jit(solution)/shard_map/all_gather | solution.py:35
  7.3 102.4 %all-gather.3.cloned.1.call-start = ((), (), s32[]{:S(2)}) async-start(), calls=%async_computation.7 | async-start | bytes 7864320 | tf_op jit(solution)/shard_map/all_gather | solution.py:34
  44.5 148.0 %reduce-scatter.3.cloned.1.call-start = ((), (), s32[]{:S(2)}) async-start(), calls=%async_computation.9 | async-start | bytes 7864320 | tf_op jit(solution)/shard_map/reduce_scatter | solution.py:40
  128.5 0.7 copy-start.4
  128.5 1.2 copy-start
  133.0 35.0 %all-to-all-start.3 = ((bf16[32,8,4096]{2,1,0:T(8,128)(2,1)}), bf16[32,8,4096]{2,1,0:T(8,128)(2,1)S(1)}, u32[]{:S(2)}, u32[]{:S(2)}) async-start(bf16[32,8,4096]{2,1,0:T(8,128)(2,1)} %bitcast.61), calls=%async_computation.4 | async-start | bytes 4194304 | tf_op jit(solution)/shard_map/all_to_all | solution.py:42
  139.7 118.9 %reduce-scatter.5.cloned.1.call-start = ((), (), s32[]{:S(2)}) async-start(), calls=%async_computation.10 | async-start | bytes 7864320 | tf_op jit(solution)/shard_map/reduce_scatter | solution.py:44
  188.5 77.7 %copy-start.3 = (s32[128,8]{0,1:T(8,128)S(1)}, s32[128,8]{0,1:T(8,128)}, u32[]{:S(2)}) copy-start(s32[128,8]{0,1:T(8,128)} %param.12) | copy-start | bytes 12292
  188.5 77.9 %copy-start.2 = (s32[128,8]{0,1:T(8,128)S(1)}, s32[128,8]{0,1:T(8,128)}, u32[]{:S(2)}) copy-start(s32[128,8]{0,1:T(8,128)} %param.11) | copy-start | bytes 12292
  258.6 30.3 %all-to-all-start.4 = ((bf16[32,24,1024]{2,1,0:T(8,128)(2,1)}), bf16[32,24,1024]{2,1,0:T(8,128)(2,1)S(1)}, u32[]{:S(2)}, u32[]{:S(2)}) async-start(bf16[32,24,1024]{2,1,0:T(8,128)(2,1)} %reduce-scatter.5.cloned.1.call-done), calls=%async_computation.6 | async-start | bytes 3145728 | tf_op jit(solution)/shard_map/all_to_all | solution.py:45
Sparse Core Ops, SparseCore 0:
  9.0 25.7 all-gather.4
  44.7 63.9 all-gather.2
  128.7 63.7 reduce-scatter.2
  194.8 63.7 reduce-scatter.4

commit v8 on v7

--- a/solution.py
+++ b/solution.py
@@ -4,8 +4,15 @@
 from jax.sharding import PartitionSpec as P
 
 def expert_part(arrived, w_gate, w_up, w_down):
-    gate_acts = jnp.einsum("scd,df->scf", arrived, w_gate, preferred_element_type=jnp.float32)
-    up_acts = jnp.einsum("scd,df->scf", arrived, w_up, preferred_element_type=jnp.float32)
+    if arrived.ndim == 4:
+        quarters = arrived.shape[0]
+        w_gate = w_gate.reshape(quarters, w_gate.shape[0] // quarters, w_gate.shape[1])
+        w_up = w_up.reshape(quarters, w_up.shape[0] // quarters, w_up.shape[1])
+        gate_acts = jnp.einsum("qscd,qdf->scf", arrived, w_gate, preferred_element_type=jnp.float32)
+        up_acts = jnp.einsum("qscd,qdf->scf", arrived, w_up, preferred_element_type=jnp.float32)
+    else:
+        gate_acts = jnp.einsum("scd,df->scf", arrived, w_gate, preferred_element_type=jnp.float32)
+        up_acts = jnp.einsum("scd,df->scf", arrived, w_up, preferred_element_type=jnp.float32)
     hidden_acts = (jax.nn.silu(gate_acts) * up_acts).astype(jnp.bfloat16)
     partial_value = jnp.einsum("scf,fd->scd", hidden_acts, w_down, preferred_element_type=jnp.float32)
     return partial_value.astype(jnp.bfloat16)
@@ -31,7 +38,7 @@
     slot_rows = jnp.dot(row_ids.astype(jnp.bfloat16), picks, preferred_element_type=jnp.float32).astype(jnp.int32)
     slot_rows = slot_rows.reshape(groups, local_experts, capacity)
     arrived = lax.all_to_all(tokens[slot_rows[:, 0]], "expert", split_axis=0, concat_axis=0, tiled=True)
-    full0 = lax.all_gather(arrived, "hidden", axis=2, tiled=True)
+    full0 = lax.all_gather(arrived, "hidden", axis=0, tiled=False)
     whole_rows = lax.all_gather(tokens, "hidden", axis=1, tiled=True)
     lead = 2 * capacity // 3
     head = lax.all_to_all(whole_rows[slot_rows[:, 1, :lead]], "expert", split_axis=0, concat_axis=0, tiled=True)

time: 299 us -> 303 us (1.013)
  blocking collectives: 117 us -> 61.7 us
  waiting for transfers between devices: 76.7 us -> 126 us
  starting transfers between devices: 14.4 us -> 19.6 us
  local copies, waits for them, and re-layouts: 29.5 us -> 33.7 us
    all_to_all x1 -> x0, blocking collectives: 55 us -> none  [body(): lax.all_to_all(whole_rows[slot_rows[:, 1, :lead]], 'expert', split_axis=0...]
    all_to_all x0 -> x1, waiting for transfers between devices: none -> 47.7 us  [body(): lax.all_to_all(whole_rows[slot_rows[:, 1, :lead]], 'expert', split_axis=0...]
    dot_general x0 -> x1, matrix products: none -> 8.31 us  [expert_part(): jnp.einsum('qscd,qdf->scf', arrived, w_gate, preferred_element_type=jnp.f...]
    dot_general x2 -> x1, matrix products: 13 us -> 6.46 us  [expert_part(): jnp.einsum('scd,df->scf', arrived, w_gate, preferred_element_type=jnp.flo...]
    all_to_all x0 -> x1, starting transfers between devices: none -> 4.67 us  [body(): lax.all_to_all(whole_rows[slot_rows[:, 1, :lead]], 'expert', split_axis=0...]
    slice x0 -> x3, local copies, waits for them, and re-layouts: none -> 3.84 us  [body(): part0 = expert_part(full0, w_gate[0], w_up[0], w_down[0])]
  transfers between devices with their start and end apart: 6 -> 7, of which waited for: 4 -> 5; matrix products, arithmetic and copies ran while one was open for 18% -> 19% of each run, Pallas kernels for 0% -> 0%
where the time goes in v8:
time: 303 us
  waiting for transfers between devices  126 us (42%)
  blocking collectives  61.7 us (20%)
  matrix products  45.1 us (15%)
  local copies, waits for them, and re-layouts  33.7 us (11%)
  starting transfers between devices  19.6 us (6%)
  between operations  13.4 us (4%)
  other arithmetic  3.19 us (1%)
    all_to_all x1, waiting for transfers between devices, body(): lax.all_to_all(whole_rows[slot_rows[:, 1, :lead]], 'expert', split_axis=0...  47.7 us
    reduce_scatter x1, waiting for transfers between devices, body(): summed1 = lax.psum_scatter(part1, 'hidden', scatter_dimension=2, tiled=True)  35.7 us
    all_to_all x1, blocking collectives, body(): lax.all_to_all(tokens[slot_rows[:, 0]], 'expert', split_axis=0, concat_ax...  31.3 us
    all_to_all x1, blocking collectives, body(): lax.all_to_all(s, 'expert', split_axis=0, concat_axis=0, tiled=True)  30.4 us
    dot_general x2, matrix products, expert_part(): jnp.einsum('scf,fd->scd', hidden_acts, w_down, preferred_element_type=jnp...  24.2 us
    all_to_all x1, waiting for transfers between devices, body(): lax.all_to_all(whole_rows[tail_rows], 'expert', split_axis=0, concat_axis...  23.4 us
    all_to_all x1, waiting for transfers between devices, body(): lax.all_to_all(s, 'expert', split_axis=0, concat_axis=0, tiled=True)  12.7 us
    gather x1, local copies, waits for them, and re-layouts, body(): whole_rows[slot_rows[:, 1, :lead]]  9.94 us
  transfers between devices with their start and end apart: 7, of which 5 were waited for; matrix products, arithmetic and copies ran while one was open for 19% of the time, Pallas kernels for 0%

profile of v8, /device:TPU:1, one launch (start us, length us, event | category | flops | bytes accessed | tf_op | source)
XLA Modules:
  0.0 302.6 jit_solution(16887193457828514258)
XLA Ops:
  6.5 0.7 all-gather.4.cloned.1.call-update
  7.3 0.0 all-gather.6.cloned.1.call-start
  7.3 0.8 copy.25
  8.1 0.1 eq.20
  8.2 0.6 fusion.23
  8.8 1.3 fusion.24
  10.1 0.1 reshape.102
  10.3 0.1 reshape.123
  10.4 2.8 gather_fusion.2
  13.2 31.3 %all_to_all.25 = bf16[32,24,1024]{2,1,0:T(8,128)(2,1)} all-to-all(bf16[32,24,1024]{2,1,0:T(8,128)(2,1)S(1)} %bitcast.73), channel_id=1, replica_groups=mesh['expert'=32,'hidden'=4] {'expert'}, dimensions={0} | all-to-all | bytes 3145728 | tf_op jit(solution)/shard_map/all_to_all | solution.py:40
  44.6 0.1 reshape.131
  44.7 0.0 all-gather.4.cloned.1.call-done
  44.7 9.9 %gather_fusion.3 = bf16[512,4096]{1,0:T(8,128)(2,1)} fusion(bf16[128,4096]{1,0:T(8,128)(2,1)} %all-gather.4.cloned.1.call-done, s32[1024]{0:T(1024)S(1)} %pad_clamp_fusion.1), kind=kCustom, calls=%fused_computation.3 | custom fusion | bytes 8390656 | tf_op jit(solution)/shard_map/gather | solution.py:44
  54.6 4.7 %all-to-all-start.1 = ((bf16[32,16,4096]{2,1,0:T(8,128)(2,1)}), bf16[32,16,4096]{2,1,0:T(8,128)(2,1)}, u32[]{:S(2)}, u32[]{:S(2)}) async-start(bf16[32,16,4096]{2,1,0:T(8,128)(2,1)} %bitcast.69), calls=%async_computation.1 | async-start | bytes 8388608 | tf_op jit(solution)/shard_map/all_to_all | solution.py:44
  59.3 0.2 reduce-scatter.3.cloned.1.call-start
  59.5 3.8 %slice.36 = bf16[1,4096,384]{2,1,0:T(8,128)(2,1)} slice(bf16[2,4096,384]{2,1,0:T(8,128)(2,1)} %param.8), slice={[0:1], [0:4096], [0:384]} | slice | bytes 6291456 | tf_op jit(solution)/shard_map/slice | solution.py:46
  63.4 47.7 %all-to-all-done.1 = bf16[32,16,4096]{2,1,0:T(8,128)(2,1)} async-done(((bf16[32,16,4096]{2,1,0:T(8,128)(2,1)}), bf16[32,16,4096]{2,1,0:T(8,128)(2,1)}, u32[]{:S(2)}, u32[]{:S(2)}) %all-to-all-start.1) | async-done | bytes 4194336 | tf_op jit(solution)/shard_map/all_to_all | solution.py:44
  111.1 8.3 %convolution_bitcast_fusion.1 = f32[32,24,384]{2,1,0:T(8,128)} fusion(bf16[4,32,24,1024]{3,2,1,0:T(8,128)(2,1)} %bitcast.82, bf16[4,1024,384,1]{2,1,3,0:T(8,128)(2,1)} %bitcast.75), kind=kOutput, calls=%fused_computation.27 | convolution fusion | flops 2415919104 | bytes 10616832 | tf_op jit(solution)/shard_map/qscd,qdf->scf/dot_general | solution.py:11
  119.4 11.7 %convolution_convert_fusion.1 = bf16[32,24,4096]{2,1,0:T(8,128)(2,1)} fusion(bf16[2,384,4096]{2,1,0:T(8,128)(2,1)} %param.10, bf16[4,32,24,1024]{3,2,1,0:T(8,128)(2,1)} %bitcast.83, bf16[4,1024,384,1]{2,1,3,0:T(8,128)(2,1)S(1)} %bitcast.74, f32[32,24,384]{2,1,0:T(8,128)} %convolution_bitcast_fusion.1), kind=kOutput, calls=%fused_computation.6 | convolution fusion | flops 4836753408 | bytes 20054016 | tf_op jit(solution)/shard_map/scf,fd->scd/dot_general | solution.py:17
  131.2 0.1 slice.58
  131.2 0.5 copy-done.4
  131.8 0.1 reshape.139
  131.9 0.5 copy-done
  132.4 3.2 %gather_fusion.4 = bf16[256,4096]{1,0:T(8,128)(2,1)} fusion(bf16[128,4096]{1,0:T(8,128)(2,1)S(1)} %copy-done, s32[1024]{0:T(1024)S(1)} %get-tuple-element.13), kind=kCustom, calls=%fused_computation.4 | custom fusion | bytes 4195328 | tf_op jit(solution)/shard_map/gather | solution.py:49
  135.6 7.0 %all-to-all-start.3 = ((bf16[32,8,4096]{2,1,0:T(8,128)(2,1)}), bf16[32,8,4096]{2,1,0:T(8,128)(2,1)S(1)}, u32[]{:S(2)}, u32[]{:S(2)}) async-start(bf16[32,8,4096]{2,1,0:T(8,128)(2,1)} %bitcast.70), calls=%async_computation.4 | async-start | bytes 4194304 | tf_op jit(solution)/shard_map/all_to_all | solution.py:49
  142.6 0.0 reduce-scatter.5.cloned.1.call-start
  142.7 4.9 %constant_dynamic-update-slice_fusion.1 = bf16[32,24,4096]{2,1,0:T(8,128)(2,1)} fusion(bf16[32,16,4096]{2,1,0:T(8,128)(2,1)} %all-to-all-done.1), kind=kLoop, calls=%fused_computation.56 | loop fusion | bytes 8388608
  147.5 23.4 %all-to-all-done.3 = bf16[32,8,4096]{2,1,0:T(8,128)(2,1)S(1)} async-done(((bf16[32,8,4096]{2,1,0:T(8,128)(2,1)}), bf16[32,8,4096]{2,1,0:T(8,128)(2,1)S(1)}, u32[]{:S(2)}, u32[]{:S(2)}) %all-to-all-start.3) | async-done | bytes 2097184 | tf_op jit(solution)/shard_map/all_to_all | solution.py:49
  171.0 1.5 constant_dynamic-update-slice_fusion
  172.4 6.5 %fusion.5 = f32[32,24,384]{2,1,0:T(8,128)S(1)} fusion(bf16[32,24,4096]{2,1,0:T(8,128)(2,1)} %constant_dynamic-update-slice_fusion, bf16[2,4096,384]{2,1,0:T(8,128)(2,1)} %param.8), kind=kOutput, calls=%fused_computation.16 | convolution fusion | flops 2415919104 | bytes 10616832 | tf_op jit(solution)/shard_map/scd,df->scf/dot_general | solution.py:14
  178.9 12.4 %convolution_convert_fusion = bf16[32,24,4096]{2,1,0:T(8,128)(2,1)} fusion(bf16[2,384,4096]{2,1,0:T(8,128)(2,1)} %param.10, bf16[32,24,4096]{2,1,0:T(8,128)(2,1)} %constant_dynamic-update-slice_fusion, bf16[2,4096,384]{2,1,0:T(8,128)(2,1)} %param.9, f32[32,24,384]{2,1,0:T(8,128)S(1)} %fusion.5), kind=kOutput, calls=%fused_computation.5 | convolution fusion | flops 4836753408 | bytes 20054016 | tf_op jit(solution)/shard_map/scf,fd->scd/dot_general | solution.py:17
  191.4 5.7 %reduce-scatter.3.cloned.1.call-done = bf16[32,24,1024]{2,1,0:T(8,128)(2,1)} async-done(((bf16[32,24,4096]{2,1,0:T(8,128)(2,1)}), bf16[32,24,1024]{2,1,0:T(8,128)(2,1)}) %reduce-scatter.3.cloned.1.call-update) | async-done | bytes 1572880 | tf_op jit(solution)/shard_map/reduce_scatter | solution.py:47
  197.1 30.4 %all_to_all.26 = bf16[32,24,1024]{2,1,0:T(8,128)(2,1)S(1)} all-to-all(bf16[32,24,1024]{2,1,0:T(8,128)(2,1)} %reduce-scatter.3.cloned.1.call-done), channel_id=1, replica_groups=mesh['expert'=32,'hidden'=4] {'expert'}, dimensions={0} | all-to-all | bytes 3145728 | tf_op jit(solution)/shard_map/all_to_all | solution.py:52
  227.5 35.7 %reduce-scatter.5.cloned.1.call-done = bf16[32,24,1024]{2,1,0:T(8,128)(2,1)} async-done(((bf16[32,24,4096]{2,1,0:T(8,128)(2,1)}), bf16[32,24,1024]{2,1,0:T(8,128)(2,1)}) %reduce-scatter.5.cloned.1.call-update) | async-done | bytes 1572880 | tf_op jit(solution)/shard_map/reduce_scatter | solution.py:51
  263.2 7.6 %all-to-all-start.4 = ((bf16[32,24,1024]{2,1,0:T(8,128)(2,1)}), bf16[32,24,1024]{2,1,0:T(8,128)(2,1)S(1)}, u32[]{:S(2)}, u32[]{:S(2)}) async-start(bf16[32,24,1024]{2,1,0:T(8,128)(2,1)} %reduce-scatter.5.cloned.1.call-done), calls=%async_computation.6 | async-start | bytes 3145728 | tf_op jit(solution)/shard_map/all_to_all | solution.py:52
  270.8 0.1 copy.28
  270.9 0.1 convert_element_type.48
  271.1 0.1 copy.27
  271.2 0.7 gather_fusion.1
  271.8 0.6 gather_fusion
  272.5 0.1 reduce_sum.28
  272.6 0.1 broadcast_divide_fusion
  272.7 2.9 select_reduce_fusion
  275.6 2.3 copy.29
  277.9 1.2 fusion.37
  279.1 1.7 fusion.38
  280.8 12.7 %all-to-all-done.4 = bf16[32,24,1024]{2,1,0:T(8,128)(2,1)S(1)} async-done(((bf16[32,24,1024]{2,1,0:T(8,128)(2,1)}), bf16[32,24,1024]{2,1,0:T(8,128)(2,1)S(1)}, u32[]{:S(2)}, u32[]{:S(2)}) %all-to-all-start.4) | async-done | bytes 1572896 | tf_op jit(solution)/shard_map/all_to_all | solution.py:52
  293.4 2.6 fusion.21
  (32 shorter events, 0.2 us)
Async XLA Ops:
  6.5 3.8 %copy-start.1 = (bf16[128,1024]{1,0:T(8,128)(2,1)S(1)}, bf16[128,1024]{1,0:T(8,128)(2,1)}, u32[]{:S(2)}) copy-start(bf16[128,1024]{1,0:T(8,128)(2,1)} %param.7) | copy-start | bytes 786436
  6.5 38.2 %all-gather.4.cloned.1.call-start = ((), (), s32[]{:S(2)}) async-start(), calls=%async_computation.7 | async-start | bytes 1310720 | tf_op jit(solution)/shard_map/all_gather | solution.py:42
  7.3 103.8 %all-gather.6.cloned.1.call-start = ((), (), s32[]{:S(2)}) async-start(), calls=%async_computation.10 | async-start | bytes 7864320 | tf_op jit(solution)/shard_map/all_gather | solution.py:41
  54.6 56.4 %all-to-all-start.1 = ((bf16[32,16,4096]{2,1,0:T(8,128)(2,1)}), bf16[32,16,4096]{2,1,0:T(8,128)(2,1)}, u32[]{:S(2)}, u32[]{:S(2)}) async-start(bf16[32,16,4096]{2,1,0:T(8,128)(2,1)} %bitcast.69), calls=%async_computation.1 | async-start | bytes 8388608 | tf_op jit(solution)/shard_map/all_to_all | solution.py:44
  59.3 137.8 %reduce-scatter.3.cloned.1.call-start = ((), (), s32[]{:S(2)}) async-start(), calls=%async_computation.8 | async-start | bytes 7864320 | tf_op jit(solution)/shard_map/reduce_scatter | solution.py:47
  111.1 8.3 %slice-start = ((bf16[2,4096,384]{2,1,0:T(8,128)(2,1)}), bf16[1,4096,384]{2,1,0:T(8,128)(2,1)S(1)}, s32[]{:S(2)}) async-start(bf16[2,4096,384]{2,1,0:T(8,128)(2,1)} %param.9), calls=%async_computation.11 | async-start | bytes 6291456 | tf_op jit(solution)/shard_map/slice | solution.py:46
  131.1 0.7 copy-start.4
  131.1 1.2 copy-start
  135.6 35.4 %all-to-all-start.3 = ((bf16[32,8,4096]{2,1,0:T(8,128)(2,1)}), bf16[32,8,4096]{2,1,0:T(8,128)(2,1)S(1)}, u32[]{:S(2)}, u32[]{:S(2)}) async-start(bf16[32,8,4096]{2,1,0:T(8,128)(2,1)} %bitcast.70), calls=%async_computation.4 | async-start | bytes 4194304 | tf_op jit(solution)/shard_map/all_to_all | solution.py:49
  142.6 120.6 %reduce-scatter.5.cloned.1.call-start = ((), (), s32[]{:S(2)}) async-start(), calls=%async_computation.9 | async-start | bytes 7864320 | tf_op jit(solution)/shard_map/reduce_scatter | solution.py:51
  191.3 79.5 %copy-start.3 = (s32[128,8]{0,1:T(8,128)S(1)}, s32[128,8]{0,1:T(8,128)}, u32[]{:S(2)}) copy-start(s32[128,8]{0,1:T(8,128)} %param.12) | copy-start | bytes 12292
  191.4 79.7 %copy-start.2 = (s32[128,8]{0,1:T(8,128)S(1)}, s32[128,8]{0,1:T(8,128)}, u32[]{:S(2)}) copy-start(s32[128,8]{0,1:T(8,128)} %param.11) | copy-start | bytes 12292
  263.2 30.3 %all-to-all-start.4 = ((bf16[32,24,1024]{2,1,0:T(8,128)(2,1)}), bf16[32,24,1024]{2,1,0:T(8,128)(2,1)S(1)}, u32[]{:S(2)}, u32[]{:S(2)}) async-start(bf16[32,24,1024]{2,1,0:T(8,128)(2,1)} %reduce-scatter.5.cloned.1.call-done), calls=%async_computation.6 | async-start | bytes 3145728 | tf_op jit(solution)/shard_map/all_to_all | solution.py:52
Sparse Core Ops, SparseCore 0:
  9.0 25.7 all-gather.3
  44.7 63.9 all-gather.5
  131.3 65.7 reduce-scatter.2
  199.4 63.7 reduce-scatter.4

commit v9 on v7

--- a/solution.py
+++ b/solution.py
@@ -6,7 +6,7 @@
 def expert_part(arrived, w_gate, w_up, w_down):
     gate_acts = jnp.einsum("scd,df->scf", arrived, w_gate, preferred_element_type=jnp.float32)
     up_acts = jnp.einsum("scd,df->scf", arrived, w_up, preferred_element_type=jnp.float32)
-    hidden_acts = (jax.nn.silu(gate_acts) * up_acts).astype(jnp.bfloat16)
+    hidden_acts = lax.optimization_barrier((jax.nn.silu(gate_acts) * up_acts).astype(jnp.bfloat16))
     partial_value = jnp.einsum("scf,fd->scd", hidden_acts, w_down, preferred_element_type=jnp.float32)
     return partial_value.astype(jnp.bfloat16)
 

time: 299 us -> 297 us (level)
  matrix products: 44.1 us -> 39.6 us
    dot_general x2, matrix products: 24.9 us -> 10.7 us  [expert_part(): jnp.einsum('scf,fd->scd', hidden_acts, w_down, preferred_element_type=jnp...]
    dot_general x0 -> x2, matrix products: none -> 9 us  [expert_part(): jnp.einsum('scd,df->scf', arrived, w_up, preferred_element_type=jnp.float32)]
    unnamed x12 -> x28, local copies, waits for them, and re-layouts: 6.44 us -> 6.57 us
  transfers between devices with their start and end apart: 6 -> 6, of which waited for: 4 -> 4; matrix products, arithmetic and copies ran while one was open for 18% -> 17% of each run, Pallas kernels for 0% -> 0%
where the time goes in v9:
time: 297 us
  blocking collectives  117 us (39%)
  waiting for transfers between devices  79.3 us (27%)
  matrix products  39.6 us (13%)
  local copies, waits for them, and re-layouts  29.8 us (10%)
  starting transfers between devices  14.5 us (5%)
  between operations  13.5 us (5%)
  other arithmetic  3.19 us (1%)
    all_to_all x1, blocking collectives, body(): lax.all_to_all(whole_rows[slot_rows[:, 1, :lead]], 'expert', split_axis=0...  55 us
    reduce_scatter x1, waiting for transfers between devices, body(): summed1 = lax.psum_scatter(part1, 'hidden', scatter_dimension=2, tiled=True)  35.6 us
    all_to_all x1, blocking collectives, body(): lax.all_to_all(tokens[slot_rows[:, 0]], 'expert', split_axis=0, concat_ax...  31.3 us
    all_to_all x1, blocking collectives, body(): lax.all_to_all(s, 'expert', split_axis=0, concat_axis=0, tiled=True)  30.4 us
    all_to_all x1, waiting for transfers between devices, body(): lax.all_to_all(whole_rows[tail_rows], 'expert', split_axis=0, concat_axis...  23.4 us
    dot_general x2, matrix products, expert_part(): jnp.einsum('scd,df->scf', arrived, w_gate, preferred_element_type=jnp.flo...  13.7 us
    all_to_all x1, waiting for transfers between devices, body(): lax.all_to_all(s, 'expert', split_axis=0, concat_axis=0, tiled=True)  12.7 us
    dot_general x2, matrix products, expert_part(): jnp.einsum('scf,fd->scd', hidden_acts, w_down, preferred_element_type=jnp...  10.7 us
  transfers between devices with their start and end apart: 6, of which 4 were waited for; matrix products, arithmetic and copies ran while one was open for 17% of the time, Pallas kernels for 0%

profile of v9, /device:TPU:1, one launch (start us, length us, event | category | flops | bytes accessed | tf_op | source)
XLA Modules:
  0.0 296.6 jit_solution(15663227271494489247)
XLA Ops:
  6.5 0.7 all-gather.5.cloned.1.call-update
  7.3 0.0 all-gather.3.cloned.1.call-start
  7.3 0.8 copy.20
  8.1 0.1 eq.20
  8.2 0.6 fusion.33
  8.8 1.3 fusion.34
  10.1 0.1 reshape.102
  10.3 0.1 reshape.123
  10.4 2.8 gather_fusion.2
  13.2 31.3 %all_to_all.25 = bf16[32,24,1024]{2,1,0:T(8,128)(2,1)} all-to-all(bf16[32,24,1024]{2,1,0:T(8,128)(2,1)S(1)} %bitcast.62), channel_id=1, replica_groups=mesh['expert'=32,'hidden'=4] {'expert'}, dimensions={0} | all-to-all | bytes 3145728 | tf_op jit(solution)/shard_map/all_to_all | solution.py:33
  44.5 0.0 reduce-scatter.3.cloned.1.call-start
  44.6 0.1 reshape.131
  44.7 0.0 all-gather.5.cloned.1.call-done
  44.7 10.0 %gather_fusion.3 = bf16[512,4096]{1,0:T(8,128)(2,1)} fusion(bf16[128,4096]{1,0:T(8,128)(2,1)} %all-gather.5.cloned.1.call-done, s32[1024]{0:T(1024)S(1)} %pad_clamp_fusion.1), kind=kCustom, calls=%fused_computation.3 | custom fusion | bytes 8390656 | tf_op jit(solution)/shard_map/gather | solution.py:37
  54.8 55.0 %all_to_all.26 = bf16[32,16,4096]{2,1,0:T(8,128)(2,1)} all-to-all(bf16[32,16,4096]{2,1,0:T(8,128)(2,1)} %bitcast.58), channel_id=1, replica_groups=mesh['expert'=32,'hidden'=4] {'expert'}, dimensions={0} | all-to-all | bytes 8388608 | tf_op jit(solution)/shard_map/all_to_all | solution.py:37
  109.7 6.6 %fusion.10 = f32[32,24,384]{2,1,0:T(8,128)S(1)} fusion(bf16[32,24,4096]{2,1,0:T(8,128)(2,1)} %all-gather.3.cloned.1.call-done, bf16[2,4096,384]{2,1,0:T(8,128)(2,1)} %param.8), kind=kOutput, calls=%fused_computation.21 | convolution fusion | flops 2415919104 | bytes 10616832 | tf_op jit(solution)/shard_map/scd,df->scf/dot_general | solution.py:7
  116.4 5.5 %fusion.28 = bf16[32,24,384]{2,1,0:T(8,128)(2,1)S(1)} fusion(bf16[32,24,4096]{2,1,0:T(8,128)(2,1)S(1)} %copy-done.5, bf16[2,4096,384]{2,1,0:T(8,128)(2,1)} %param.9, f32[32,24,384]{2,1,0:T(8,128)S(1)} %fusion.10), kind=kOutput, calls=%fused_computation.33 | convolution fusion | flops 2417688576 | bytes 11206656 | tf_op jit(solution)/shard_map/scd,df->scf/dot_general | solution.py:8
  121.9 5.3 %convolution_convert_fusion.1 = bf16[32,24,4096]{2,1,0:T(8,128)(2,1)} fusion(bf16[32,24,384]{2,1,0:T(8,128)(2,1)S(1)} %fusion.28, bf16[2,384,4096]{2,1,0:T(8,128)(2,1)S(1)} %bitcast.72), kind=kOutput, calls=%fused_computation.6 | convolution fusion | flops 2419064832 | bytes 10027008 | tf_op jit(solution)/shard_map/scf,fd->scd/dot_general | solution.py:10
  127.3 0.1 slice.58
  127.4 0.5 copy-done.6
  127.9 0.1 reshape.139
  128.0 0.5 copy-done
  128.5 3.2 %gather_fusion.4 = bf16[256,4096]{1,0:T(8,128)(2,1)} fusion(bf16[128,4096]{1,0:T(8,128)(2,1)S(1)} %copy-done, s32[1024]{0:T(1024)S(1)} %get-tuple-element.13), kind=kCustom, calls=%fused_computation.4 | custom fusion | bytes 4195328 | tf_op jit(solution)/shard_map/gather | solution.py:42
  131.7 6.6 %all-to-all-start.3 = ((bf16[32,8,4096]{2,1,0:T(8,128)(2,1)}), bf16[32,8,4096]{2,1,0:T(8,128)(2,1)S(1)}, u32[]{:S(2)}, u32[]{:S(2)}) async-start(bf16[32,8,4096]{2,1,0:T(8,128)(2,1)} %bitcast.59), calls=%async_computation.4 | async-start | bytes 4194304 | tf_op jit(solution)/shard_map/all_to_all | solution.py:42
  138.3 0.3 reduce-scatter.5.cloned.1.call-start
  138.5 4.7 %constant_dynamic-update-slice_fusion.1 = bf16[32,24,4096]{2,1,0:T(8,128)(2,1)} fusion(bf16[32,16,4096]{2,1,0:T(8,128)(2,1)} %all_to_all.26), kind=kLoop, calls=%fused_computation.58 | loop fusion | bytes 8388608
  143.3 23.4 %all-to-all-done.3 = bf16[32,8,4096]{2,1,0:T(8,128)(2,1)S(1)} async-done(((bf16[32,8,4096]{2,1,0:T(8,128)(2,1)}), bf16[32,8,4096]{2,1,0:T(8,128)(2,1)S(1)}, u32[]{:S(2)}, u32[]{:S(2)}) %all-to-all-start.3) | async-done | bytes 2097184 | tf_op jit(solution)/shard_map/all_to_all | solution.py:42
  166.6 1.5 constant_dynamic-update-slice_fusion
  168.1 7.1 %fusion.5 = f32[32,24,384]{2,1,0:T(8,128)S(1)} fusion(bf16[32,24,4096]{2,1,0:T(8,128)(2,1)} %constant_dynamic-update-slice_fusion, bf16[2,4096,384]{2,1,0:T(8,128)(2,1)} %param.8), kind=kOutput, calls=%fused_computation.16 | convolution fusion | flops 2415919104 | bytes 10616832 | tf_op jit(solution)/shard_map/scd,df->scf/dot_general | solution.py:7
  175.3 3.5 %fusion.25 = bf16[32,24,384]{2,1,0:T(8,128)(2,1)S(1)} fusion(bf16[32,24,4096]{2,1,0:T(8,128)(2,1)S(1)} %copy-done.2, bf16[2,4096,384]{2,1,0:T(8,128)(2,1)S(1)} %bitcast.70, f32[32,24,384]{2,1,0:T(8,128)S(1)} %fusion.5), kind=kOutput, calls=%fused_computation.32 | convolution fusion | flops 2417688576 | bytes 11206656 | tf_op jit(solution)/shard_map/scd,df->scf/dot_general | solution.py:8
  178.8 5.4 %convolution_convert_fusion = bf16[32,24,4096]{2,1,0:T(8,128)(2,1)} fusion(bf16[32,24,384]{2,1,0:T(8,128)(2,1)S(1)} %fusion.25, bf16[2,384,4096]{2,1,0:T(8,128)(2,1)S(1)} %bitcast.74), kind=kOutput, calls=%fused_computation.5 | convolution fusion | flops 2419064832 | bytes 10027008 | tf_op jit(solution)/shard_map/scf,fd->scd/dot_general | solution.py:10
  184.2 6.9 %reduce-scatter.3.cloned.1.call-done = bf16[32,24,1024]{2,1,0:T(8,128)(2,1)} async-done(((bf16[32,24,4096]{2,1,0:T(8,128)(2,1)}), bf16[32,24,1024]{2,1,0:T(8,128)(2,1)}) %reduce-scatter.3.cloned.1.call-update) | async-done | bytes 1572880 | tf_op jit(solution)/shard_map/reduce_scatter | solution.py:40
  191.1 30.4 %all_to_all.27 = bf16[32,24,1024]{2,1,0:T(8,128)(2,1)S(1)} all-to-all(bf16[32,24,1024]{2,1,0:T(8,128)(2,1)} %reduce-scatter.3.cloned.1.call-done), channel_id=1, replica_groups=mesh['expert'=32,'hidden'=4] {'expert'}, dimensions={0} | all-to-all | bytes 3145728 | tf_op jit(solution)/shard_map/all_to_all | solution.py:45
  221.5 35.6 %reduce-scatter.5.cloned.1.call-done = bf16[32,24,1024]{2,1,0:T(8,128)(2,1)} async-done(((bf16[32,24,4096]{2,1,0:T(8,128)(2,1)}), bf16[32,24,1024]{2,1,0:T(8,128)(2,1)}) %reduce-scatter.5.cloned.1.call-update) | async-done | bytes 1572880 | tf_op jit(solution)/shard_map/reduce_scatter | solution.py:44
  257.2 7.6 %all-to-all-start.4 = ((bf16[32,24,1024]{2,1,0:T(8,128)(2,1)}), bf16[32,24,1024]{2,1,0:T(8,128)(2,1)S(1)}, u32[]{:S(2)}, u32[]{:S(2)}) async-start(bf16[32,24,1024]{2,1,0:T(8,128)(2,1)} %reduce-scatter.5.cloned.1.call-done), calls=%async_computation.6 | async-start | bytes 3145728 | tf_op jit(solution)/shard_map/all_to_all | solution.py:45
  264.8 0.1 copy.23
  264.9 0.1 convert_element_type.48
  265.1 0.1 copy.22
  265.2 0.7 gather_fusion.1
  265.8 0.6 gather_fusion
  266.5 0.1 reduce_sum.28
  266.6 0.1 broadcast_divide_fusion
  266.7 2.9 select_reduce_fusion
  269.6 2.3 copy.24
  271.9 1.2 fusion.41
  273.1 1.7 fusion.42
  274.8 12.7 %all-to-all-done.4 = bf16[32,24,1024]{2,1,0:T(8,128)(2,1)S(1)} async-done(((bf16[32,24,1024]{2,1,0:T(8,128)(2,1)}), bf16[32,24,1024]{2,1,0:T(8,128)(2,1)S(1)}, u32[]{:S(2)}, u32[]{:S(2)}) %all-to-all-start.4) | async-done | bytes 1572896 | tf_op jit(solution)/shard_map/all_to_all | solution.py:45
  287.4 2.6 fusion.31
  (49 shorter events, 0.3 us)
Async XLA Ops:
  6.5 3.8 %copy-start.1 = (bf16[128,1024]{1,0:T(8,128)(2,1)S(1)}, bf16[128,1024]{1,0:T(8,128)(2,1)}, u32[]{:S(2)}) copy-start(bf16[128,1024]{1,0:T(8,128)(2,1)} %param.7) | copy-start | bytes 786436
  6.5 38.2 %all-gather.5.cloned.1.call-start = ((), (), s32[]{:S(2)}) async-start(), calls=%async_computation.8 | async-start | bytes 1310720 | tf_op jit(solution)/shard_map/all_gather | solution.py:35
  7.3 102.5 %all-gather.3.cloned.1.call-start = ((), (), s32[]{:S(2)}) async-start(), calls=%async_computation.7 | async-start | bytes 7864320 | tf_op jit(solution)/shard_map/all_gather | solution.py:34
  44.5 146.6 %reduce-scatter.3.cloned.1.call-start = ((), (), s32[]{:S(2)}) async-start(), calls=%async_computation.9 | async-start | bytes 7864320 | tf_op jit(solution)/shard_map/reduce_scatter | solution.py:40
  109.7 6.6 %copy-start.5 = (bf16[32,24,4096]{2,1,0:T(8,128)(2,1)S(1)}, bf16[32,24,4096]{2,1,0:T(8,128)(2,1)}, u32[]{:S(2)}) copy-start(bf16[32,24,4096]{2,1,0:T(8,128)(2,1)} %all-gather.3.cloned.1.call-done) | copy-start | bytes 18874372
  109.7 12.2 %slice-start.2 = ((s8[6291456]{0:T(1024)(128)(4,1)}), s8[4194304]{0:T(1024)(128)(4,1)S(1)}, s32[]{:S(2)}) async-start(s8[6291456]{0:T(1024)(128)(4,1)} %bitcast.71), calls=%async_computation.13 | async-start | bytes 8388608
  116.4 5.5 %slice-start.3 = ((s8[6291456]{0:T(1024)(128)(4,1)}), s8[2097152]{0:T(1024)(128)(4,1)S(1)}, s32[]{:S(2)}) async-start(s8[6291456]{0:T(1024)(128)(4,1)} %bitcast.71), calls=%async_computation.14 | async-start | bytes 4194304
  127.2 0.7 copy-start.6
  127.2 1.2 copy-start
  131.7 34.9 %all-to-all-start.3 = ((bf16[32,8,4096]{2,1,0:T(8,128)(2,1)}), bf16[32,8,4096]{2,1,0:T(8,128)(2,1)S(1)}, u32[]{:S(2)}, u32[]{:S(2)}) async-start(bf16[32,8,4096]{2,1,0:T(8,128)(2,1)} %bitcast.59), calls=%async_computation.4 | async-start | bytes 4194304 | tf_op jit(solution)/shard_map/all_to_all | solution.py:42
  138.3 118.9 %reduce-scatter.5.cloned.1.call-start = ((), (), s32[]{:S(2)}) async-start(), calls=%async_computation.10 | async-start | bytes 7864320 | tf_op jit(solution)/shard_map/reduce_scatter | solution.py:44
  166.6 8.6 %slice-start = ((s8[6291456]{0:T(1024)(128)(4,1)}), s8[4194304]{0:T(1024)(128)(4,1)S(1)}, s32[]{:S(2)}) async-start(s8[6291456]{0:T(1024)(128)(4,1)} %bitcast.69), calls=%async_computation.11 | async-start | bytes 8388608
  168.1 7.1 %copy-start.2 = (bf16[32,24,4096]{2,1,0:T(8,128)(2,1)S(1)}, bf16[32,24,4096]{2,1,0:T(8,128)(2,1)}, u32[]{:S(2)}) copy-start(bf16[32,24,4096]{2,1,0:T(8,128)(2,1)} %constant_dynamic-update-slice_fusion) | copy-start | bytes 18874372
  168.1 7.1 %slice-start.1 = ((s8[6291456]{0:T(1024)(128)(4,1)}), s8[2097152]{0:T(1024)(128)(4,1)S(1)}, s32[]{:S(2)}) async-start(s8[6291456]{0:T(1024)(128)(4,1)} %bitcast.69), calls=%async_computation.12 | async-start | bytes 4194304
  168.1 10.7 %slice-start.4 = ((s8[6291456]{0:T(1024)(128)(4,1)}), s8[4194304]{0:T(1024)(128)(4,1)S(1)}, s32[]{:S(2)}) async-start(s8[6291456]{0:T(1024)(128)(4,1)} %bitcast.73), calls=%async_computation.15 | async-start | bytes 8388608
  175.3 3.5 %slice-start.5 = ((s8[6291456]{0:T(1024)(128)(4,1)}), s8[2097152]{0:T(1024)(128)(4,1)S(1)}, s32[]{:S(2)}) async-start(s8[6291456]{0:T(1024)(128)(4,1)} %bitcast.73), calls=%async_computation.16 | async-start | bytes 4194304
  184.2 80.6 %copy-start.4 = (s32[128,8]{0,1:T(8,128)S(1)}, s32[128,8]{0,1:T(8,128)}, u32[]{:S(2)}) copy-start(s32[128,8]{0,1:T(8,128)} %param.12) | copy-start | bytes 12292
  184.2 80.8 %copy-start.3 = (s32[128,8]{0,1:T(8,128)S(1)}, s32[128,8]{0,1:T(8,128)}, u32[]{:S(2)}) copy-start(s32[128,8]{0,1:T(8,128)} %param.11) | copy-start | bytes 12292
  257.2 30.3 %all-to-all-start.4 = ((bf16[32,24,1024]{2,1,0:T(8,128)(2,1)}), bf16[32,24,1024]{2,1,0:T(8,128)(2,1)S(1)}, u32[]{:S(2)}, u32[]{:S(2)}) async-start(bf16[32,24,1024]{2,1,0:T(8,128)(2,1)} %reduce-scatter.5.cloned.1.call-done), calls=%async_computation.6 | async-start | bytes 3145728 | tf_op jit(solution)/shard_map/all_to_all | solution.py:45
Sparse Core Ops, SparseCore 0:
  9.0 25.7 all-gather.4
  44.7 63.9 all-gather.2
  127.4 63.6 reduce-scatter.2
  193.4 63.7 reduce-scatter.4

commit v10 on v9

--- a/solution.py
+++ b/solution.py
@@ -33,7 +33,7 @@
     arrived = lax.all_to_all(tokens[slot_rows[:, 0]], "expert", split_axis=0, concat_axis=0, tiled=True)
     full0 = lax.all_gather(arrived, "hidden", axis=2, tiled=True)
     whole_rows = lax.all_gather(tokens, "hidden", axis=1, tiled=True)
-    lead = 2 * capacity // 3
+    lead = 3 * capacity // 4
     head = lax.all_to_all(whole_rows[slot_rows[:, 1, :lead]], "expert", split_axis=0, concat_axis=0, tiled=True)
     full0, head = lax.optimization_barrier((full0, head))
     part0 = expert_part(full0, w_gate[0], w_up[0], w_down[0])

time: 297 us -> 329 us (1.11)
  blocking collectives: 117 us -> 143 us
  local copies, waits for them, and re-layouts: 29.8 us -> 33.8 us
    all_to_all x1 -> x0, waiting for transfers between devices: 23.4 us -> none  [body(): lax.all_to_all(whole_rows[tail_rows], 'expert', split_axis=0, concat_axis...]
    reduce_scatter x1, waiting for transfers between devices: 35.6 us -> 58.2 us  [body(): summed1 = lax.psum_scatter(part1, 'hidden', scatter_dimension=2, tiled=True)]
    all_to_all x1, blocking collectives: 55 us -> 77.5 us  [body(): lax.all_to_all(whole_rows[slot_rows[:, 1, :lead]], 'expert', split_axis=0...]
    gather x1 -> x2, local copies, waits for them, and re-layouts: 10 us -> 20.4 us  [body(): whole_rows[slot_rows[:, 1, :lead]]]
    all_to_all x1 -> x2, starting transfers between devices: 7.59 us -> 15.2 us  [body(): lax.all_to_all(s, 'expert', split_axis=0, concat_axis=0, tiled=True)]
    all_to_all x1 -> x0, starting transfers between devices: 6.58 us -> none  [body(): lax.all_to_all(whole_rows[tail_rows], 'expert', split_axis=0, concat_axis...]
    unnamed x28 -> x29, local copies, waits for them, and re-layouts: 6.57 us -> 1.77 us
    all_to_all x1, blocking collectives: 30.4 us -> 33.9 us  [body(): lax.all_to_all(whole_rows[tail_rows], 'expert', split_axis=0, concat_axis...]
  transfers between devices with their start and end apart: 6 -> 6, of which waited for: 4 -> 3; matrix products, arithmetic and copies ran while one was open for 17% -> 17% of each run, Pallas kernels for 0% -> 0%
where the time goes in v10:
time: 329 us; the launch traced here: 328 us
  blocking collectives  143 us (43%)
  waiting for transfers between devices  80.7 us (25%)
  matrix products  39.1 us (12%)
  local copies, waits for them, and re-layouts  33.8 us (10%)
  starting transfers between devices  15.3 us (5%)
  between operations  13.6 us (4%)
    all_to_all x1, blocking collectives, body(): lax.all_to_all(whole_rows[slot_rows[:, 1, :lead]], 'expert', split_axis=0...  77.5 us
    reduce_scatter x1, waiting for transfers between devices, body(): summed1 = lax.psum_scatter(part1, 'hidden', scatter_dimension=2, tiled=True)  58.2 us
    all_to_all x1, blocking collectives, body(): lax.all_to_all(whole_rows[tail_rows], 'expert', split_axis=0, concat_axis...  33.9 us
    all_to_all x1, blocking collectives, body(): lax.all_to_all(tokens[slot_rows[:, 0]], 'expert', split_axis=0, concat_ax...  31.3 us
    gather x2, local copies, waits for them, and re-layouts, body(): whole_rows[slot_rows[:, 1, :lead]]  20.4 us
    all_to_all x2, starting transfers between devices, body(): lax.all_to_all(s, 'expert', split_axis=0, concat_axis=0, tiled=True)  15.2 us
    dot_general x2, matrix products, expert_part(): jnp.einsum('scd,df->scf', arrived, w_gate, preferred_element_type=jnp.flo...  13.3 us
    all_to_all x2, waiting for transfers between devices, body(): lax.all_to_all(s, 'expert', split_axis=0, concat_axis=0, tiled=True)  12.9 us
  transfers between devices with their start and end apart: 6, of which 3 were waited for; matrix products, arithmetic and copies ran while one was open for 17% of the time, Pallas kernels for 0%

profile of v10, /device:TPU:1, one launch (start us, length us, event | category | flops | bytes accessed | tf_op | source)
XLA Modules:
  0.0 328.4 jit_solution(12442908232362226216)
XLA Ops:
  6.5 0.7 all-gather.5.cloned.1.call-update
  7.3 0.0 all-gather.3.cloned.1.call-start
  7.3 0.8 copy.20
  8.1 0.1 eq.20
  8.2 0.6 fusion.33
  8.8 1.3 fusion.34
  10.1 0.1 reshape.102
  10.3 0.1 reshape.123
  10.4 2.8 gather_fusion.2
  13.2 31.3 %all_to_all.25 = bf16[32,24,1024]{2,1,0:T(8,128)(2,1)} all-to-all(bf16[32,24,1024]{2,1,0:T(8,128)(2,1)S(1)} %bitcast.58), channel_id=1, replica_groups=mesh['expert'=32,'hidden'=4] {'expert'}, dimensions={0} | all-to-all | bytes 3145728 | tf_op jit(solution)/shard_map/all_to_all | solution.py:33
  44.5 0.0 all-gather.3.cloned.1.call-update
  44.5 0.0 reduce-scatter.3.cloned.1.call-start
  44.6 0.1 reshape.131
  44.7 0.0 all-gather.5.cloned.1.call-done
  44.8 12.8 %gather_fusion.3 = bf16[576,4096]{1,0:T(8,128)(2,1)} fusion(bf16[128,4096]{1,0:T(8,128)(2,1)} %all-gather.5.cloned.1.call-done, s32[1024]{0:T(1024)S(1)} %pad_clamp_fusion.1), kind=kCustom, calls=%fused_computation.3 | custom fusion | bytes 9439488 | tf_op jit(solution)/shard_map/gather | solution.py:37
  57.6 7.6 %reshape.130 = bf16[32,18,4096]{2,1,0:T(8,128)(2,1)} reshape(bf16[576,4096]{1,0:T(8,128)(2,1)} %gather_fusion.3) | data formatting | bytes 9437184 | tf_op jit(solution)/shard_map/gather | solution.py:37
  65.2 77.5 %all_to_all.26 = bf16[32,18,4096]{2,1,0:T(8,128)(2,1)} all-to-all(bf16[32,18,4096]{2,1,0:T(8,128)(2,1)} %reshape.130), channel_id=1, replica_groups=mesh['expert'=32,'hidden'=4] {'expert'}, dimensions={0} | all-to-all | bytes 9437184 | tf_op jit(solution)/shard_map/all_to_all | solution.py:37
  142.7 6.6 %fusion.10 = f32[32,24,384]{2,1,0:T(8,128)S(1)} fusion(bf16[32,24,4096]{2,1,0:T(8,128)(2,1)} %all-gather.3.cloned.1.call-done, bf16[2,4096,384]{2,1,0:T(8,128)(2,1)} %param.8), kind=kOutput, calls=%fused_computation.22 | convolution fusion | flops 2415919104 | bytes 10616832 | tf_op jit(solution)/shard_map/scd,df->scf/dot_general | solution.py:7
  149.3 5.5 %fusion.28 = bf16[32,24,384]{2,1,0:T(8,128)(2,1)S(1)} fusion(bf16[32,24,4096]{2,1,0:T(8,128)(2,1)S(1)} %copy-done.4, bf16[2,4096,384]{2,1,0:T(8,128)(2,1)} %param.9, f32[32,24,384]{2,1,0:T(8,128)S(1)} %fusion.10), kind=kOutput, calls=%fused_computation.34 | convolution fusion | flops 2417688576 | bytes 11206656 | tf_op jit(solution)/shard_map/scd,df->scf/dot_general | solution.py:8
  154.8 5.3 %convolution_convert_fusion.1 = bf16[32,24,4096]{2,1,0:T(8,128)(2,1)} fusion(bf16[32,24,384]{2,1,0:T(8,128)(2,1)S(1)} %fusion.28, bf16[2,384,4096]{2,1,0:T(8,128)(2,1)S(1)} %bitcast.68), kind=kOutput, calls=%fused_computation.6 | convolution fusion | flops 2419064832 | bytes 10027008 | tf_op jit(solution)/shard_map/scf,fd->scd/dot_general | solution.py:10
  160.1 0.0 reduce-scatter.3.cloned.1.call-update
  160.1 0.0 reduce-scatter.5.cloned.1.call-start
  160.2 0.1 slice.58
  160.3 0.1 reshape.139
  160.4 0.9 copy-done
  161.3 1.5 gather_fusion.4
  162.9 1.6 reshape.138
  164.5 33.9 %all_to_all.27 = bf16[32,6,4096]{2,1,0:T(8,128)(2,1)S(1)} all-to-all(bf16[32,6,4096]{2,1,0:T(8,128)(2,1)} %reshape.138), channel_id=1, replica_groups=mesh['expert'=32,'hidden'=4] {'expert'}, dimensions={0} | all-to-all | bytes 3145728 | tf_op jit(solution)/shard_map/all_to_all | solution.py:42
  198.4 6.7 %fusion.5 = f32[32,24,384]{2,1,0:T(8,128)S(1)} fusion(bf16[2,4096,384]{2,1,0:T(8,128)(2,1)} %param.8, bf16[32,6,4096]{2,1,0:T(8,128)(2,1)S(1)} %all_to_all.27, bf16[32,18,4096]{2,1,0:T(8,128)(2,1)} %all_to_all.26), kind=kOutput, calls=%fused_computation.17 | convolution fusion | flops 2428502016 | bytes 12189696 | tf_op jit(solution)/shard_map/scd,df->scf/dot_general | solution.py:7
  205.2 3.5 %fusion.25 = bf16[32,24,384]{2,1,0:T(8,128)(2,1)S(1)} fusion(bf16[2,4096,384]{2,1,0:T(8,128)(2,1)S(1)} %bitcast.66, bf16[32,6,4096]{2,1,0:T(8,128)(2,1)S(1)} %all_to_all.27, bf16[32,18,4096]{2,1,0:T(8,128)(2,1)S(1)} %bitcast.55, f32[32,24,384]{2,1,0:T(8,128)S(1)} %fusion.5), kind=kOutput, calls=%fused_computation.33 | convolution fusion | flops 2430271488 | bytes 13303808 | tf_op jit(solution)/shard_map/scd,df->scf/dot_general | solution.py:8
  208.7 5.3 %convolution_convert_fusion = bf16[32,24,4096]{2,1,0:T(8,128)(2,1)} fusion(bf16[32,24,384]{2,1,0:T(8,128)(2,1)S(1)} %fusion.25, bf16[2,384,4096]{2,1,0:T(8,128)(2,1)S(1)} %bitcast.70), kind=kOutput, calls=%fused_computation.5 | convolution fusion | flops 2419064832 | bytes 10027008 | tf_op jit(solution)/shard_map/scf,fd->scd/dot_general | solution.py:10
  214.1 8.8 %reduce-scatter.3.cloned.1.call-done = bf16[32,24,1024]{2,1,0:T(8,128)(2,1)} async-done(((bf16[32,24,4096]{2,1,0:T(8,128)(2,1)}), bf16[32,24,1024]{2,1,0:T(8,128)(2,1)}) %reduce-scatter.3.cloned.1.call-update) | async-done | bytes 1572880 | tf_op jit(solution)/shard_map/reduce_scatter | solution.py:40
  222.9 7.6 %all-to-all-start.2 = ((bf16[32,24,1024]{2,1,0:T(8,128)(2,1)}), bf16[32,24,1024]{2,1,0:T(8,128)(2,1)S(1)}, u32[]{:S(2)}, u32[]{:S(2)}) async-start(bf16[32,24,1024]{2,1,0:T(8,128)(2,1)} %reduce-scatter.3.cloned.1.call-done), calls=%async_computation.3 | async-start | bytes 3145728 | tf_op jit(solution)/shard_map/all_to_all | solution.py:45
  230.6 0.1 copy.23
  230.7 0.1 convert_element_type.48
  230.8 58.2 %reduce-scatter.5.cloned.1.call-done = bf16[32,24,1024]{2,1,0:T(8,128)(2,1)} async-done(((bf16[32,24,4096]{2,1,0:T(8,128)(2,1)}), bf16[32,24,1024]{2,1,0:T(8,128)(2,1)}) %reduce-scatter.5.cloned.1.call-update) | async-done | bytes 1572880 | tf_op jit(solution)/shard_map/reduce_scatter | solution.py:44
  289.0 7.6 %all-to-all-start.4 = ((bf16[32,24,1024]{2,1,0:T(8,128)(2,1)}), bf16[32,24,1024]{2,1,0:T(8,128)(2,1)S(1)}, u32[]{:S(2)}, u32[]{:S(2)}) async-start(bf16[32,24,1024]{2,1,0:T(8,128)(2,1)} %reduce-scatter.5.cloned.1.call-done), calls=%async_computation.6 | async-start | bytes 3145728 | tf_op jit(solution)/shard_map/all_to_all | solution.py:45
  296.6 0.1 copy.22
  296.8 0.6 gather_fusion.1
  297.4 0.6 gather_fusion
  298.1 0.1 reduce_sum.28
  298.2 0.1 broadcast_divide_fusion
  298.3 2.9 select_reduce_fusion
  301.2 2.3 copy.24
  303.5 1.2 fusion.43
  304.7 1.7 fusion.44
  306.4 12.9 %all-to-all-done.4 = bf16[32,24,1024]{2,1,0:T(8,128)(2,1)S(1)} async-done(((bf16[32,24,1024]{2,1,0:T(8,128)(2,1)}), bf16[32,24,1024]{2,1,0:T(8,128)(2,1)S(1)}, u32[]{:S(2)}, u32[]{:S(2)}) %all-to-all-start.4) | async-done | bytes 1572896 | tf_op jit(solution)/shard_map/all_to_all | solution.py:45
  319.3 2.6 fusion.31
  (53 shorter events, 0.2 us)
Async XLA Ops:
  6.5 3.8 %copy-start.1 = (bf16[128,1024]{1,0:T(8,128)(2,1)S(1)}, bf16[128,1024]{1,0:T(8,128)(2,1)}, u32[]{:S(2)}) copy-start(bf16[128,1024]{1,0:T(8,128)(2,1)} %param.7) | copy-start | bytes 786436
  6.5 38.2 %all-gather.5.cloned.1.call-start = ((), (), s32[]{:S(2)}) async-start(), calls=%async_computation.8 | async-start | bytes 1310720 | tf_op jit(solution)/shard_map/all_gather | solution.py:35
  7.3 135.4 %all-gather.3.cloned.1.call-start = ((), (), s32[]{:S(2)}) async-start(), calls=%async_computation.7 | async-start | bytes 7864320 | tf_op jit(solution)/shard_map/all_gather | solution.py:34
  44.5 178.4 %reduce-scatter.3.cloned.1.call-start = ((), (), s32[]{:S(2)}) async-start(), calls=%async_computation.9 | async-start | bytes 7864320 | tf_op jit(solution)/shard_map/reduce_scatter | solution.py:40
  142.7 6.6 %copy-start.4 = (bf16[32,24,4096]{2,1,0:T(8,128)(2,1)S(1)}, bf16[32,24,4096]{2,1,0:T(8,128)(2,1)}, u32[]{:S(2)}) copy-start(bf16[32,24,4096]{2,1,0:T(8,128)(2,1)} %all-gather.3.cloned.1.call-done) | copy-start | bytes 18874372
  142.7 12.2 %slice-start.4 = ((s8[6291456]{0:T(1024)(128)(4,1)}), s8[4194304]{0:T(1024)(128)(4,1)S(1)}, s32[]{:S(2)}) async-start(s8[6291456]{0:T(1024)(128)(4,1)} %bitcast.67), calls=%async_computation.15 | async-start | bytes 8388608
  149.3 5.5 %slice-start.5 = ((s8[6291456]{0:T(1024)(128)(4,1)}), s8[2097152]{0:T(1024)(128)(4,1)S(1)}, s32[]{:S(2)}) async-start(s8[6291456]{0:T(1024)(128)(4,1)} %bitcast.67), calls=%async_computation.16 | async-start | bytes 4194304
  160.1 1.2 copy-start
  160.1 128.9 %reduce-scatter.5.cloned.1.call-start = ((), (), s32[]{:S(2)}) async-start(), calls=%async_computation.10 | async-start | bytes 7864320 | tf_op jit(solution)/shard_map/reduce_scatter | solution.py:44
  164.5 40.6 %slice-start = ((s8[6291456]{0:T(1024)(128)(4,1)}), s8[4194304]{0:T(1024)(128)(4,1)S(1)}, s32[]{:S(2)}) async-start(s8[6291456]{0:T(1024)(128)(4,1)} %bitcast.54), calls=%async_computation.11 | async-start | bytes 8388608
  164.5 40.7 %slice-start.2 = ((s8[6291456]{0:T(1024)(128)(4,1)}), s8[4194304]{0:T(1024)(128)(4,1)S(1)}, s32[]{:S(2)}) async-start(s8[6291456]{0:T(1024)(128)(4,1)} %bitcast.65), calls=%async_computation.13 | async-start | bytes 8388608
  164.5 44.2 %slice-start.6 = ((s8[6291456]{0:T(1024)(128)(4,1)}), s8[4194304]{0:T(1024)(128)(4,1)S(1)}, s32[]{:S(2)}) async-start(s8[6291456]{0:T(1024)(128)(4,1)} %bitcast.69), calls=%async_computation.17 | async-start | bytes 8388608
  198.4 6.8 %slice-start.1 = ((s8[6291456]{0:T(1024)(128)(4,1)}), s8[2097152]{0:T(1024)(128)(4,1)S(1)}, s32[]{:S(2)}) async-start(s8[6291456]{0:T(1024)(128)(4,1)} %bitcast.54), calls=%async_computation.12 | async-start | bytes 4194304
  198.4 6.8 %slice-start.3 = ((s8[6291456]{0:T(1024)(128)(4,1)}), s8[2097152]{0:T(1024)(128)(4,1)S(1)}, s32[]{:S(2)}) async-start(s8[6291456]{0:T(1024)(128)(4,1)} %bitcast.65), calls=%async_computation.14 | async-start | bytes 4194304
  198.4 10.3 %slice-start.7 = ((s8[6291456]{0:T(1024)(128)(4,1)}), s8[2097152]{0:T(1024)(128)(4,1)S(1)}, s32[]{:S(2)}) async-start(s8[6291456]{0:T(1024)(128)(4,1)} %bitcast.69), calls=%async_computation.18 | async-start | bytes 4194304
  214.1 16.5 %copy-start.3 = (s32[128,8]{0,1:T(8,128)S(1)}, s32[128,8]{0,1:T(8,128)}, u32[]{:S(2)}) copy-start(s32[128,8]{0,1:T(8,128)} %param.12) | copy-start | bytes 12292
  214.1 82.5 %copy-start.2 = (s32[128,8]{0,1:T(8,128)S(1)}, s32[128,8]{0,1:T(8,128)}, u32[]{:S(2)}) copy-start(s32[128,8]{0,1:T(8,128)} %param.11) | copy-start | bytes 12292
  214.1 82.7 %copy-start.5 = (s32[128]{0:T(128)S(1)}, s32[128]{0:T(128)}, u32[]{:S(2)}) copy-start(s32[128]{0:T(128)} %param.13) | copy-start | bytes 1540
  222.9 66.1 %all-to-all-start.2 = ((bf16[32,24,1024]{2,1,0:T(8,128)(2,1)}), bf16[32,24,1024]{2,1,0:T(8,128)(2,1)S(1)}, u32[]{:S(2)}, u32[]{:S(2)}) async-start(bf16[32,24,1024]{2,1,0:T(8,128)(2,1)} %reduce-scatter.3.cloned.1.call-done), calls=%async_computation.3 | async-start | bytes 3145728 | tf_op jit(solution)/shard_map/all_to_all | solution.py:45
  289.0 30.3 %all-to-all-start.4 = ((bf16[32,24,1024]{2,1,0:T(8,128)(2,1)}), bf16[32,24,1024]{2,1,0:T(8,128)(2,1)S(1)}, u32[]{:S(2)}, u32[]{:S(2)}) async-start(bf16[32,24,1024]{2,1,0:T(8,128)(2,1)} %reduce-scatter.5.cloned.1.call-done), calls=%async_computation.6 | async-start | bytes 3145728 | tf_op jit(solution)/shard_map/all_to_all | solution.py:45
Sparse Core Ops, SparseCore 0:
  9.0 25.7 all-gather.4
  44.7 63.9 all-gather.2
  160.3 62.6 reduce-scatter.2
  225.2 63.7 reduce-scatter.4
